TPU v7x, 1024 devices: a whole 4x8x16 slice. The times are simulated.
1024 devices in a mesh: tile: 32 (over z, x_hi), kern: 32 (over y, x_lo, core).
Axes of the slice: x: 4 (x_hi: 2, x_lo: 2; x = x_hi * 2 + x_lo), y: 8, z: 16, core: 2. Of those that a mesh axis runs over, the one named last changes fastest.
Arguments:
- mask: float32 [64, 4096], P(None, 'tile'), may hold values from 0 to 1
- kernels: float32 [32, 2, 129, 129], P('kern'), may hold values from -0.046875 to 0.046875
- weights: float32 [32], P('kern'), may hold values from 0.3 to 3
- target: int32 [64, 4096], P(None, 'tile'), may hold values 0 or 1
- active: int32 [2, 128], P(None, 'tile'), may hold values 0 or 1
Outputs:
- mask_grad: float32 [64, 4096], P(None, 'tile')
All inputs are finite; a program needn't handle non-finite values. No bound on the sum of `target` or of `active` on one device may be relied on, other than what follows from the above.
Results may differ from a plain program's by a relative error of at most 0.0001.
Values sent between devices are 32-bit elements; how exact they have to be, the bound alone decides.
No kernel may reach another device: no remote copies, remote signals or barrier semaphores. Data moves between devices by JAX's collectives and lax.ppermute only.
A program may use at most 32 MiB of HBM per device.

v0:
```python
import math

import jax
import jax.numpy as jnp
from jax import lax
from jax.sharding import PartitionSpec as P

BLK = 32


STEEPNESS = 6.0
THRESHOLD = 0.8


def padded(shard, sides, width):
    for axis, dim in sides:
        peers, length = (lax.axis_size(axis), shard.shape[dim])
        up = [(i, (i + 1) % peers) for i in range(peers - 1)]
        down = [(j, i) for i, j in up]
        last = lax.slice_in_dim(shard, length - width, length, axis=dim)
        initial = lax.slice_in_dim(shard, 0, width, axis=dim)
        before = lax.ppermute(last, axis, up)
        after = lax.ppermute(initial, axis, down)
        shard = jnp.concatenate([before, shard, after], axis=dim)
    return shard


def product(left_mat, right_mat):
    return jnp.dot(
        left_mat, right_mat, precision=lax.Precision.HIGHEST, preferred_element_type=jnp.float32
    )


def twiddle(length):
    series = jnp.arange(length, dtype=jnp.int32)
    phase = series[:, None] * series[None, :] % length
    angle = phase.astype(jnp.float32) * (2.0 * math.pi / length)
    return (jnp.cos(angle), jnp.sin(angle))


def apply_left(cosine, sine, sign, real_part, imag_part):
    return (
        product(cosine, real_part) - sign * product(sine, imag_part),
        product(cosine, imag_part) + sign * product(sine, real_part),
    )


def apply_right(real_part, imag_part, cosine, sine, sign):
    return (
        product(real_part, cosine) - sign * product(imag_part, sine),
        product(imag_part, cosine) + sign * product(real_part, sine),
    )


def edge_pixels(frame, margin):
    return jnp.concatenate([frame[:, :margin], frame[:, frame.shape[1] - margin :]], axis=1)


def add_returned(own, returned, margin):
    from_left = returned[:, :margin]
    from_right = returned[:, returned.shape[1] - margin :]
    own = own.at[:, :margin].add(from_left)
    return own.at[:, own.shape[1] - margin :].add(from_right)


def resist_drive(intensity, target_rows, active_rows):
    resist = jax.nn.sigmoid(STEEPNESS * (intensity - THRESHOLD))
    return 2.0 * (resist - target_rows) * active_rows * STEEPNESS * resist * (1.0 - resist)


def body(mask, kernels, weights, target, active):
    band, own_cols = mask.shape
    width = kernels.shape[-1]
    margin = (width - 1) // 2
    frame_rows = band + 2 * margin
    frame_cols = own_cols + 2 * margin
    total_kernels = kernels.shape[0] * lax.axis_size("kern")
    scale = 1.0 / (frame_rows * frame_cols)
    row_cos, row_sin = twiddle(frame_rows)
    col_cos, col_sin = twiddle(frame_cols)
    extended = padded(mask, (("tile", 1),), margin)
    spec_real = product(row_cos[:, margin : margin + band], extended)
    spec_imag = -product(row_sin[:, margin : margin + band], extended)
    spec_real, spec_imag = apply_right(spec_real, spec_imag, col_cos, col_sin, -1.0)
    kernel_index = 0
    kern_real, kern_imag = apply_left(
        row_cos[:, :width],
        row_sin[:, :width],
        1.0,
        kernels[kernel_index, 0],
        kernels[kernel_index, 1],
    )
    kern_real, kern_imag = apply_right(
        kern_real, kern_imag, col_cos[:width, :], col_sin[:width, :], 1.0
    )
    prod_real = spec_real * kern_real - spec_imag * kern_imag
    prod_imag = spec_real * kern_imag + spec_imag * kern_real
    field_real, field_imag = apply_left(
        row_cos[:band, :], row_sin[:band, :], 1.0, prod_real, prod_imag
    )
    field_real, field_imag = apply_right(
        field_real, field_imag, col_cos[:, :own_cols], col_sin[:, :own_cols], 1.0
    )
    field_real = field_real * scale
    field_imag = field_imag * scale
    responses = [(kern_real, kern_imag, field_real, field_imag)]
    share_sum = weights[kernel_index] * (field_real * field_real + field_imag * field_imag)
    share_sum = share_sum / total_kernels
    target_float = target.astype(jnp.float32)
    pixel_active = jnp.repeat(jnp.repeat(active, BLK, axis=0), BLK, axis=1).astype(jnp.float32)
    intensity = lax.psum(share_sum, "kern")
    drive = resist_drive(intensity, target_float, pixel_active)
    kernel_index = 0
    kern_real, kern_imag, field_real, field_imag = responses[kernel_index]
    source_real, source_imag = apply_left(
        row_cos[:, :band], row_sin[:, :band], -1.0, drive * field_real, drive * field_imag
    )
    source_real, source_imag = apply_right(
        source_real, source_imag, col_cos[:own_cols, :], col_sin[:own_cols, :], -1.0
    )
    quot_real = source_real * kern_real + source_imag * kern_imag
    quot_imag = source_imag * kern_real - source_real * kern_imag
    back_real, back_imag = apply_left(
        row_cos[margin : margin + band, :],
        row_sin[margin : margin + band, :],
        1.0,
        quot_real,
        quot_imag,
    )
    back = product(back_real, col_cos) - product(back_imag, col_sin)
    frame_grad = 2.0 * weights[kernel_index] * scale / total_kernels * back
    summed = lax.psum(frame_grad, "kern")
    returned = padded(edge_pixels(summed, margin), (("tile", 1),), margin)
    mask_grad = add_returned(summed[:, margin : margin + own_cols], returned, margin)
    return mask_grad


def solution(mesh):
    return jax.shard_map(
        body,
        mesh=mesh,
        in_specs=(
            P(None, "tile"),
            P("kern", None, None, None),
            P("kern"),
            P(None, "tile"),
            P(None, "tile"),
        ),
        out_specs=P(None, "tile"),
        check_vma=False,
    )
```

profile of v0, /device:TPU:1, one launch (start us, length us, event | category | flops | bytes accessed | tf_op | source)
XLA Modules:
  0.0 383.8 jit_solution(10989584108686945410)
XLA Ops:
  6.5 0.9 fusion.110
  7.4 5.5 %collective-permute-start = (f32[64,64]{1,0:T(8,128)S(1)}, f32[64,64]{1,0:T(8,128)S(1)}, u32[]{:S(2)}, u32[]{:S(2)}) collective-permute-start(f32[64,64]{1,0:T(8,128)S(1)} %get-tuple-element.37), channel_id=1, source_target_pairs={{0,32},{32,64},{64,96},{96,128},{128,160},{160,192},{192,224},{224... | collective-permute-start | bytes 49160 | tf_op jit(solution)/shard_map/ppermute | solution.py:22
  12.9 1.3 collective-permute-start.1
  14.2 0.8 fusion.20
  15.0 0.8 fusion.19
  15.7 1.0 fusion.29
  16.7 1.0 fusion.28
  20.0 0.6 fusion.43
  23.3 0.7 copy-done
  24.3 1.3 fusion.34
  26.0 1.3 fusion.32
  27.3 1.3 fusion.3
  28.6 1.5 multiply_subtract_fusion.1
  32.0 109.9 %psum.14 = f32[64,128]{1,0:T(8,128)S(1)} all-reduce(f32[64,128]{1,0:T(8,128)S(1)} %get-tuple-element.39), channel_id=1, replica_groups=mesh['tile'=32,'kern'=32] {'kern'}, use_global_device_ids=true, to_apply=%region_0.1 | all-reduce | flops 8192 | bytes 65536 | tf_op jit(solution)/shard_map/psum | solution.py:111
  145.1 1.2 fusion.30
  146.3 1.9 fusion.6
  148.2 217.4 %all-reduce.2.cloned.1.call-done = f32[64,256]{1,0:T(8,128)} async-done(((f32[64,256]{1,0:T(8,128)}), f32[64,256]{1,0:T(8,128)}) %all-reduce.2.cloned.1.call-update) | async-done | bytes 65552 | tf_op jit(solution)/shard_map/psum | solution.py:132
  365.6 0.9 fusion.109
  366.5 2.1 collective-permute-start.2
  368.6 0.6 compare_reduce_fusion
  369.3 1.3 collective-permute-start.3
  370.7 0.7 add_select_fusion.2
  371.7 3.8 collective-permute-done.3
  375.5 1.5 scatter-add.9
  (56 shorter events, 10.3 us)
Async XLA Ops:
  6.5 359.1 %all-reduce.2.cloned.1.call-start = ((), (), s32[]{:S(2)}) async-start(), calls=%async_computation | async-start | bytes 131072 | tf_op jit(solution)/shard_map/psum | solution.py:132
  7.4 15.8 %collective-permute-start = (f32[64,64]{1,0:T(8,128)S(1)}, f32[64,64]{1,0:T(8,128)S(1)}, u32[]{:S(2)}, u32[]{:S(2)}) collective-permute-start(f32[64,64]{1,0:T(8,128)S(1)} %get-tuple-element.37), channel_id=1, source_target_pairs={{0,32},{32,64},{64,96},{96,128},{128,160},{160,192},{192,224},{224... | collective-permute-start | bytes 49160 | tf_op jit(solution)/shard_map/ppermute | solution.py:22
  12.9 10.3 %collective-permute-start.1 = (f32[64,64]{1,0:T(8,128)S(1)}, f32[64,64]{1,0:T(8,128)S(1)}, u32[]{:S(2)}, u32[]{:S(2)}) collective-permute-start(f32[64,64]{1,0:T(8,128)S(1)} %get-tuple-element.38), channel_id=1, source_target_pairs={{32,0},{64,32},{96,64},{128,96},{160,128},{192,160},{224,192},{256... | collective-permute-start | bytes 49160 | tf_op jit(solution)/shard_map/ppermute | solution.py:23
  15.7 2.0 copy-start.1
  22.2 0.7 copy-start.5
  23.2 0.8 copy-start
  32.0 109.9 %copy-start.4 = (s32[64,128]{1,0:T(8,128)S(1)}, s32[64,128]{1,0:T(8,128)}, u32[]{:S(2)}) copy-start(s32[64,128]{1,0:T(8,128)} %param.12) | copy-start | bytes 98308
  365.6 5.0 %copy-start.2 = (f32[64,256]{1,0:T(8,128)S(1)}, f32[64,256]{1,0:T(8,128)}, u32[]{:S(2)}) copy-start(f32[64,256]{1,0:T(8,128)} %all-reduce.2.cloned.1.call-done) | copy-start | bytes 196612
  366.5 4.2 %collective-permute-start.2 = (f32[64,64]{1,0:T(8,128)S(1)}, f32[64,64]{1,0:T(8,128)S(1)}, u32[]{:S(2)}, u32[]{:S(2)}) collective-permute-start(f32[64,64]{1,0:T(8,128)S(1)} %get-tuple-element.36), channel_id=1, source_target_pairs={{0,32},{32,64},{64,96},{96,128},{128,160},{160,192},{192,224},{224... | collective-permute-start | bytes 49160 | tf_op jit(solution)/shard_map/ppermute | solution.py:22
  369.3 6.2 %collective-permute-start.3 = (f32[64,64]{1,0:T(8,128)S(1)}, f32[64,64]{1,0:T(8,128)S(1)}, u32[]{:S(2)}, u32[]{:S(2)}) collective-permute-start(f32[64,64]{1,0:T(8,128)S(1)} %get-tuple-element.35), channel_id=1, source_target_pairs={{32,0},{64,32},{96,64},{128,96},{160,128},{192,160},{224,192},{256... | collective-permute-start | bytes 49160 | tf_op jit(solution)/shard_map/ppermute | solution.py:23
  371.7 3.9 %copy-start.3 = (f32[64,128]{1,0:T(8,128)}, f32[64,128]{1,0:T(8,128)S(1)}, u32[]{:S(2)}) copy-start(f32[64,128]{1,0:T(8,128)S(1)} %scatter-add.6) | copy-start | bytes 98308
Sparse Core Ops, SparseCore 0:
  148.3 217.2 all-reduce.1
where the time goes:
time: 387 us; the launch traced here: 384 us
  waiting for transfers between devices  221 us (57%)
  blocking collectives  110 us (28%)
  matrix products  18.4 us (5%)
  between operations  14.4 us (4%)
  starting transfers between devices  10.2 us (3%)
  other arithmetic  4.91 us (1%)
  local copies, waits for them, and re-layouts  4.85 us (1%)
    psum x1, waiting for transfers between devices, body(): summed = lax.psum(frame_grad, 'kern')  217 us
    psum x1, blocking collectives, body(): intensity = lax.psum(share_sum, 'kern')  110 us
    dot_general x36, matrix products, product(): jnp.dot(left_mat, right_mat, precision=lax.Precision.HIGHEST, preferred_e...  18.4 us
  transfers between devices with their start and end apart: 5, of which 2 were waited for; matrix products, arithmetic and copies ran while one was open for 3% of the time, Pallas kernels for 0%

commit v1 on v0

--- a/solution.py
+++ b/solution.py
@@ -23,6 +23,18 @@
         after = lax.ppermute(initial, axis, down)
         shard = jnp.concatenate([before, shard, after], axis=dim)
     return shard
+
+
+def exchange_sum(value, axis):
+    peers = lax.axis_size(axis)
+    if peers & (peers - 1):
+        return lax.psum(value, axis)
+    stride = 1
+    while stride < peers:
+        pairs = [(i, i ^ stride) for i in range(peers)]
+        value = value + lax.ppermute(value, axis, pairs)
+        stride *= 2
+    return value
 
 
 def product(left_mat, right_mat):
@@ -108,7 +120,7 @@
     share_sum = share_sum / total_kernels
     target_float = target.astype(jnp.float32)
     pixel_active = jnp.repeat(jnp.repeat(active, BLK, axis=0), BLK, axis=1).astype(jnp.float32)
-    intensity = lax.psum(share_sum, "kern")
+    intensity = exchange_sum(share_sum, "kern")
     drive = resist_drive(intensity, target_float, pixel_active)
     kernel_index = 0
     kern_real, kern_imag, field_real, field_imag = responses[kernel_index]
@@ -129,7 +141,7 @@
     )
     back = product(back_real, col_cos) - product(back_imag, col_sin)
     frame_grad = 2.0 * weights[kernel_index] * scale / total_kernels * back
-    summed = lax.psum(frame_grad, "kern")
+    summed = exchange_sum(frame_grad, "kern")
     returned = padded(edge_pixels(summed, margin), (("tile", 1),), margin)
     mask_grad = add_returned(summed[:, margin : margin + own_cols], returned, margin)
     return mask_grad

time: 387 us -> 118 us (0.30)
  the two profiles are of different devices: /device:TPU:1 before, /device:TPU:2 now
where the time goes in v1:
time: 118 us; the launch traced here: 117 us
  waiting for transfers between devices  46.6 us (39%)
  starting transfers between devices  43.5 us (37%)
  matrix products  17.8 us (15%)
  other arithmetic  4.98 us (4%)
  local copies, waits for them, and re-layouts  3.35 us (3%)
    ppermute x10, waiting for transfers between devices, exchange_sum(): value = value + lax.ppermute(value, axis, pairs)  41.6 us
    ppermute x10, starting transfers between devices, exchange_sum(): value = value + lax.ppermute(value, axis, pairs)  31.4 us
    dot_general x36, matrix products, product(): jnp.dot(left_mat, right_mat, precision=lax.Precision.HIGHEST, preferred_e...  17.8 us
    ppermute x2, starting transfers between devices, padded(): before = lax.ppermute(last, axis, up)  9.46 us
    ppermute x2, waiting for transfers between devices, padded(): after = lax.ppermute(initial, axis, down)  5 us
    ppermute x2, starting transfers between devices, padded(): after = lax.ppermute(initial, axis, down)  2.58 us
  transfers between devices with their start and end apart: 14, of which 11 were waited for; matrix products, arithmetic and copies ran while one was open for 8% of the time, Pallas kernels for 0%

profile of v1, /device:TPU:2, one launch (start us, length us, event | category | flops | bytes accessed | tf_op | source)
XLA Modules:
  0.0 117.3 jit_solution(3225665275374364480)
XLA Ops:
  0.9 4.0 %collective-permute-start = (f32[64,64]{1,0:T(8,128)S(1)}, f32[64,64]{1,0:T(8,128)S(1)}, u32[]{:S(2)}, u32[]{:S(2)}) collective-permute-start(f32[64,64]{1,0:T(8,128)S(1)} %get-tuple-element.37), channel_id=1, source_target_pairs={{0,32},{32,64},{64,96},{96,128},{128,160},{160,192},{192,224},{224... | collective-permute-start | bytes 49160 | tf_op jit(solution)/shard_map/ppermute | solution.py:22
  18.3 1.3 %fusion.3 = f32[192,256]{1,0:T(8,128)S(1)} fusion(f32[192,256]{1,0:T(8,128)S(1)} %fusion.34, f32[192,256]{1,0:T(8,128)S(1)} %convolution_negate_fusion), kind=kOutput, calls=%fused_computation.9 | convolution fusion | flops 152010752 | bytes 589824 | tf_op jit(solution)/shard_map/dot_general | solution.py:41
  19.7 1.5 %multiply_subtract_fusion.1 = (f32[192,256]{1,0:T(8,128)S(1)}, f32[192,256]{1,0:T(8,128)S(1)}) fusion(f32[192,256]{1,0:T(8,128)S(1)} %convolution_add_fusion, f32[192,256]{1,0:T(8,128)S(1)} %fusion.3, f32[192,256]{1,0:T(8,128)S(1)} %convolution_subtract_fusion, f32[192,256]{1,0:T(8,128)S(1)} %fusion.32, f32[192,256]{1,0:T(8,128)S(1)} %fusion.58), kind=kOutput, calls=%fused_computation.42 | convolution fusion | flops 152305664 | bytes 1376256 | tf_op jit(solution)/shard_map/dot_general | solution.py:41
  23.0 1.9 %collective-permute-start.2 = (f32[64,128]{1,0:T(8,128)S(1)}, f32[64,128]{1,0:T(8,128)S(1)}, u32[]{:S(2)}, u32[]{:S(2)}) collective-permute-start(f32[64,128]{1,0:T(8,128)S(1)} %get-tuple-element.39), channel_id=1, source_target_pairs={{0,1},{1,0},{2,3},{3,2},{4,5},{5,4},{6,7},{7,6},{8,9},{9,8},{10,11... | collective-permute-start | bytes 98312 | tf_op jit(solution)/shard_map/ppermute | solution.py:35
  26.1 12.3 %collective-permute-start.3 = (f32[64,128]{1,0:T(8,128)S(1)}, f32[64,128]{1,0:T(8,128)S(1)}, u32[]{:S(2)}, u32[]{:S(2)}) collective-permute-start(f32[64,128]{1,0:T(8,128)S(1)} %add.170), channel_id=1, source_target_pairs={{0,2},{1,3},{2,0},{3,1},{4,6},{5,7},{6,4},{7,5},{8,10},{9,11},{10,... | collective-permute-start | bytes 98312 | tf_op jit(solution)/shard_map/ppermute | solution.py:35
  38.4 1.9 %collective-permute-done.3 = f32[64,128]{1,0:T(8,128)S(1)} collective-permute-done((f32[64,128]{1,0:T(8,128)S(1)}, f32[64,128]{1,0:T(8,128)S(1)}, u32[]{:S(2)}, u32[]{:S(2)}) %collective-permute-start.3) | collective-permute-done | bytes 32800 | tf_op jit(solution)/shard_map/ppermute | solution.py:35
  40.3 1.9 %collective-permute-start.4 = (f32[64,128]{1,0:T(8,128)S(1)}, f32[64,128]{1,0:T(8,128)S(1)}, u32[]{:S(2)}, u32[]{:S(2)}) collective-permute-start(f32[64,128]{1,0:T(8,128)S(1)} %add.171), channel_id=1, source_target_pairs={{0,4},{1,5},{2,6},{3,7},{4,0},{5,1},{6,2},{7,3},{8,12},{9,13},{10,... | collective-permute-start | bytes 98312 | tf_op jit(solution)/shard_map/ppermute | solution.py:35
  42.2 3.9 %collective-permute-done.4 = f32[64,128]{1,0:T(8,128)S(1)} collective-permute-done((f32[64,128]{1,0:T(8,128)S(1)}, f32[64,128]{1,0:T(8,128)S(1)}, u32[]{:S(2)}, u32[]{:S(2)}) %collective-permute-start.4) | collective-permute-done | bytes 32800 | tf_op jit(solution)/shard_map/ppermute | solution.py:35
  46.1 1.9 %collective-permute-start.5 = (f32[64,128]{1,0:T(8,128)S(1)}, f32[64,128]{1,0:T(8,128)S(1)}, u32[]{:S(2)}, u32[]{:S(2)}) collective-permute-start(f32[64,128]{1,0:T(8,128)S(1)} %add.172), channel_id=1, source_target_pairs={{0,8},{1,9},{2,10},{3,11},{4,12},{5,13},{6,14},{7,15},{8,0},{9,1},... | collective-permute-start | bytes 98312 | tf_op jit(solution)/shard_map/ppermute | solution.py:35
  48.0 5.2 %collective-permute-done.5 = f32[64,128]{1,0:T(8,128)S(1)} collective-permute-done((f32[64,128]{1,0:T(8,128)S(1)}, f32[64,128]{1,0:T(8,128)S(1)}, u32[]{:S(2)}, u32[]{:S(2)}) %collective-permute-start.5) | collective-permute-done | bytes 32800 | tf_op jit(solution)/shard_map/ppermute | solution.py:35
  53.2 1.9 %collective-permute-start.6 = (f32[64,128]{1,0:T(8,128)S(1)}, f32[64,128]{1,0:T(8,128)S(1)}, u32[]{:S(2)}, u32[]{:S(2)}) collective-permute-start(f32[64,128]{1,0:T(8,128)S(1)} %add.173), channel_id=1, source_target_pairs={{0,16},{1,17},{2,18},{3,19},{4,20},{5,21},{6,22},{7,23},{8,24},{9,... | collective-permute-start | bytes 98312 | tf_op jit(solution)/shard_map/ppermute | solution.py:35
  55.5 7.4 %collective-permute-done.6 = f32[64,128]{1,0:T(8,128)S(1)} collective-permute-done((f32[64,128]{1,0:T(8,128)S(1)}, f32[64,128]{1,0:T(8,128)S(1)}, u32[]{:S(2)}, u32[]{:S(2)}) %collective-permute-start.6) | collective-permute-done | bytes 32800 | tf_op jit(solution)/shard_map/ppermute | solution.py:35
  68.6 1.9 %collective-permute-start.7 = (f32[64,256]{1,0:T(8,128)S(1)}, f32[64,256]{1,0:T(8,128)S(1)}, u32[]{:S(2)}, u32[]{:S(2)}) collective-permute-start(f32[64,256]{1,0:T(8,128)S(1)} %fusion.6), channel_id=1, source_target_pairs={{0,1},{1,0},{2,3},{3,2},{4,5},{5,4},{6,7},{7,6},{8,9},{9,8},{10,11... | collective-permute-start | bytes 196616 | tf_op jit(solution)/shard_map/ppermute | solution.py:35
  71.8 3.8 %collective-permute-start.8 = (f32[64,256]{1,0:T(8,128)S(1)}, f32[64,256]{1,0:T(8,128)S(1)}, u32[]{:S(2)}, u32[]{:S(2)}) collective-permute-start(f32[64,256]{1,0:T(8,128)S(1)} %add.180), channel_id=1, source_target_pairs={{0,2},{1,3},{2,0},{3,1},{4,6},{5,7},{6,4},{7,5},{8,10},{9,11},{10,... | collective-permute-start | bytes 196616 | tf_op jit(solution)/shard_map/ppermute | solution.py:35
  75.5 2.4 %collective-permute-done.8 = f32[64,256]{1,0:T(8,128)S(1)} collective-permute-done((f32[64,256]{1,0:T(8,128)S(1)}, f32[64,256]{1,0:T(8,128)S(1)}, u32[]{:S(2)}, u32[]{:S(2)}) %collective-permute-start.8) | collective-permute-done | bytes 65568 | tf_op jit(solution)/shard_map/ppermute | solution.py:35
  77.9 1.9 %collective-permute-start.9 = (f32[64,256]{1,0:T(8,128)S(1)}, f32[64,256]{1,0:T(8,128)S(1)}, u32[]{:S(2)}, u32[]{:S(2)}) collective-permute-start(f32[64,256]{1,0:T(8,128)S(1)} %add.181), channel_id=1, source_target_pairs={{0,4},{1,5},{2,6},{3,7},{4,0},{5,1},{6,2},{7,3},{8,12},{9,13},{10,... | collective-permute-start | bytes 196616 | tf_op jit(solution)/shard_map/ppermute | solution.py:35
  79.9 4.2 %collective-permute-done.9 = f32[64,256]{1,0:T(8,128)S(1)} collective-permute-done((f32[64,256]{1,0:T(8,128)S(1)}, f32[64,256]{1,0:T(8,128)S(1)}, u32[]{:S(2)}, u32[]{:S(2)}) %collective-permute-start.9) | collective-permute-done | bytes 65568 | tf_op jit(solution)/shard_map/ppermute | solution.py:35
  84.1 1.9 %collective-permute-start.10 = (f32[64,256]{1,0:T(8,128)S(1)}, f32[64,256]{1,0:T(8,128)S(1)}, u32[]{:S(2)}, u32[]{:S(2)}) collective-permute-start(f32[64,256]{1,0:T(8,128)S(1)} %add.182), channel_id=1, source_target_pairs={{0,8},{1,9},{2,10},{3,11},{4,12},{5,13},{6,14},{7,15},{8,0},{9,1},... | collective-permute-start | bytes 196616 | tf_op jit(solution)/shard_map/ppermute | solution.py:35
  86.0 6.0 %collective-permute-done.10 = f32[64,256]{1,0:T(8,128)S(1)} collective-permute-done((f32[64,256]{1,0:T(8,128)S(1)}, f32[64,256]{1,0:T(8,128)S(1)}, u32[]{:S(2)}, u32[]{:S(2)}) %collective-permute-start.10) | collective-permute-done | bytes 65568 | tf_op jit(solution)/shard_map/ppermute | solution.py:35
  92.1 1.9 %collective-permute-start.11 = (f32[64,256]{1,0:T(8,128)S(1)}, f32[64,256]{1,0:T(8,128)S(1)}, u32[]{:S(2)}, u32[]{:S(2)}) collective-permute-start(f32[64,256]{1,0:T(8,128)S(1)} %add.183), channel_id=1, source_target_pairs={{0,16},{1,17},{2,18},{3,19},{4,20},{5,21},{6,22},{7,23},{8,24},{9,... | collective-permute-start | bytes 196616 | tf_op jit(solution)/shard_map/ppermute | solution.py:35
  94.0 8.1 %collective-permute-done.11 = f32[64,256]{1,0:T(8,128)S(1)} collective-permute-done((f32[64,256]{1,0:T(8,128)S(1)}, f32[64,256]{1,0:T(8,128)S(1)}, u32[]{:S(2)}, u32[]{:S(2)}) %collective-permute-start.11) | collective-permute-done | bytes 65568 | tf_op jit(solution)/shard_map/ppermute | solution.py:35
  102.3 5.4 %collective-permute-start.12 = (f32[64,64]{1,0:T(8,128)S(1)}, f32[64,64]{1,0:T(8,128)S(1)}, u32[]{:S(2)}, u32[]{:S(2)}) collective-permute-start(f32[64,64]{1,0:T(8,128)S(1)} %get-tuple-element.36), channel_id=1, source_target_pairs={{0,32},{32,64},{64,96},{96,128},{128,160},{160,192},{192,224},{224... | collective-permute-start | bytes 49160 | tf_op jit(solution)/shard_map/ppermute | solution.py:22
  110.7 5.0 %collective-permute-done.13 = f32[64,64]{1,0:T(8,128)S(1)} collective-permute-done((f32[64,64]{1,0:T(8,128)S(1)}, f32[64,64]{1,0:T(8,128)S(1)}, u32[]{:S(2)}, u32[]{:S(2)}) %collective-permute-start.13) | collective-permute-done | bytes 16416 | tf_op jit(solution)/shard_map/ppermute | solution.py:23
  115.8 1.5 %scatter-add.9 = f32[64,128]{1,0:T(8,128)} dynamic-update-slice(f32[64,128]{1,0:T(8,128)} %copy-done.2, f32[64,64]{1,0:T(8,128)S(1)} %slice_add_fusion, s32[]{:T(128)} %constant.95.clone.1, s32[]{:T(128)} %constant.107.clone.1) | dynamic-update-slice | bytes 32772 | tf_op jit(solution)/shard_map/scatter-add | solution.py:75
  (79 shorter events, 26.8 us)
Async XLA Ops:
  0.9 14.0 %collective-permute-start = (f32[64,64]{1,0:T(8,128)S(1)}, f32[64,64]{1,0:T(8,128)S(1)}, u32[]{:S(2)}, u32[]{:S(2)}) collective-permute-start(f32[64,64]{1,0:T(8,128)S(1)} %get-tuple-element.37), channel_id=1, source_target_pairs={{0,32},{32,64},{64,96},{96,128},{128,160},{160,192},{192,224},{224... | collective-permute-start | bytes 49160 | tf_op jit(solution)/shard_map/ppermute | solution.py:22
  4.9 10.0 %collective-permute-start.1 = (f32[64,64]{1,0:T(8,128)S(1)}, f32[64,64]{1,0:T(8,128)S(1)}, u32[]{:S(2)}, u32[]{:S(2)}) collective-permute-start(f32[64,64]{1,0:T(8,128)S(1)} %get-tuple-element.38), channel_id=1, source_target_pairs={{32,0},{64,32},{96,64},{128,96},{160,128},{192,160},{224,192},{256... | collective-permute-start | bytes 49160 | tf_op jit(solution)/shard_map/ppermute | solution.py:23
  7.8 2.0 %copy-start.1 = (f32[1,2,129,129]{3,1,2,0:T(2,128)S(1)}, f32[1,2,129,129]{3,1,2,0:T(2,128)}, u32[]{:S(2)}) copy-start(f32[1,2,129,129]{3,1,2,0:T(2,128)} %param.10) | copy-start | bytes 399388
  13.7 1.2 %copy-start = (f32[64,128]{1,0:T(8,128)S(1)}, f32[64,128]{1,0:T(8,128)}, u32[]{:S(2)}) copy-start(f32[64,128]{1,0:T(8,128)} %param.9) | copy-start | bytes 98308
  23.0 3.1 %collective-permute-start.2 = (f32[64,128]{1,0:T(8,128)S(1)}, f32[64,128]{1,0:T(8,128)S(1)}, u32[]{:S(2)}, u32[]{:S(2)}) collective-permute-start(f32[64,128]{1,0:T(8,128)S(1)} %get-tuple-element.39), channel_id=1, source_target_pairs={{0,1},{1,0},{2,3},{3,2},{4,5},{5,4},{6,7},{7,6},{8,9},{9,8},{10,11... | collective-permute-start | bytes 98312 | tf_op jit(solution)/shard_map/ppermute | solution.py:35
  26.1 14.2 %collective-permute-start.3 = (f32[64,128]{1,0:T(8,128)S(1)}, f32[64,128]{1,0:T(8,128)S(1)}, u32[]{:S(2)}, u32[]{:S(2)}) collective-permute-start(f32[64,128]{1,0:T(8,128)S(1)} %add.170), channel_id=1, source_target_pairs={{0,2},{1,3},{2,0},{3,1},{4,6},{5,7},{6,4},{7,5},{8,10},{9,11},{10,... | collective-permute-start | bytes 98312 | tf_op jit(solution)/shard_map/ppermute | solution.py:35
  40.3 5.8 %collective-permute-start.4 = (f32[64,128]{1,0:T(8,128)S(1)}, f32[64,128]{1,0:T(8,128)S(1)}, u32[]{:S(2)}, u32[]{:S(2)}) collective-permute-start(f32[64,128]{1,0:T(8,128)S(1)} %add.171), channel_id=1, source_target_pairs={{0,4},{1,5},{2,6},{3,7},{4,0},{5,1},{6,2},{7,3},{8,12},{9,13},{10,... | collective-permute-start | bytes 98312 | tf_op jit(solution)/shard_map/ppermute | solution.py:35
  46.1 9.0 %copy-start.4 = (s32[2,4]{1,0:T(2,128)S(1)}, s32[2,4]{1,0:T(2,128)}, u32[]{:S(2)}) copy-start(s32[2,4]{1,0:T(2,128)} %param.13) | copy-start | bytes 100
  46.1 7.1 %collective-permute-start.5 = (f32[64,128]{1,0:T(8,128)S(1)}, f32[64,128]{1,0:T(8,128)S(1)}, u32[]{:S(2)}, u32[]{:S(2)}) collective-permute-start(f32[64,128]{1,0:T(8,128)S(1)} %add.172), channel_id=1, source_target_pairs={{0,8},{1,9},{2,10},{3,11},{4,12},{5,13},{6,14},{7,15},{8,0},{9,1},... | collective-permute-start | bytes 98312 | tf_op jit(solution)/shard_map/ppermute | solution.py:35
  53.2 9.7 %collective-permute-start.6 = (f32[64,128]{1,0:T(8,128)S(1)}, f32[64,128]{1,0:T(8,128)S(1)}, u32[]{:S(2)}, u32[]{:S(2)}) collective-permute-start(f32[64,128]{1,0:T(8,128)S(1)} %add.173), channel_id=1, source_target_pairs={{0,16},{1,17},{2,18},{3,19},{4,20},{5,21},{6,22},{7,23},{8,24},{9,... | collective-permute-start | bytes 98312 | tf_op jit(solution)/shard_map/ppermute | solution.py:35
  55.4 7.5 %copy-start.3 = (s32[64,128]{1,0:T(8,128)S(1)}, s32[64,128]{1,0:T(8,128)}, u32[]{:S(2)}) copy-start(s32[64,128]{1,0:T(8,128)} %param.12) | copy-start | bytes 98308
  68.6 3.1 %collective-permute-start.7 = (f32[64,256]{1,0:T(8,128)S(1)}, f32[64,256]{1,0:T(8,128)S(1)}, u32[]{:S(2)}, u32[]{:S(2)}) collective-permute-start(f32[64,256]{1,0:T(8,128)S(1)} %fusion.6), channel_id=1, source_target_pairs={{0,1},{1,0},{2,3},{3,2},{4,5},{5,4},{6,7},{7,6},{8,9},{9,8},{10,11... | collective-permute-start | bytes 196616 | tf_op jit(solution)/shard_map/ppermute | solution.py:35
  71.8 6.2 %collective-permute-start.8 = (f32[64,256]{1,0:T(8,128)S(1)}, f32[64,256]{1,0:T(8,128)S(1)}, u32[]{:S(2)}, u32[]{:S(2)}) collective-permute-start(f32[64,256]{1,0:T(8,128)S(1)} %add.180), channel_id=1, source_target_pairs={{0,2},{1,3},{2,0},{3,1},{4,6},{5,7},{6,4},{7,5},{8,10},{9,11},{10,... | collective-permute-start | bytes 196616 | tf_op jit(solution)/shard_map/ppermute | solution.py:35
  77.9 6.2 %collective-permute-start.9 = (f32[64,256]{1,0:T(8,128)S(1)}, f32[64,256]{1,0:T(8,128)S(1)}, u32[]{:S(2)}, u32[]{:S(2)}) collective-permute-start(f32[64,256]{1,0:T(8,128)S(1)} %add.181), channel_id=1, source_target_pairs={{0,4},{1,5},{2,6},{3,7},{4,0},{5,1},{6,2},{7,3},{8,12},{9,13},{10,... | collective-permute-start | bytes 196616 | tf_op jit(solution)/shard_map/ppermute | solution.py:35
  84.1 8.0 %collective-permute-start.10 = (f32[64,256]{1,0:T(8,128)S(1)}, f32[64,256]{1,0:T(8,128)S(1)}, u32[]{:S(2)}, u32[]{:S(2)}) collective-permute-start(f32[64,256]{1,0:T(8,128)S(1)} %add.182), channel_id=1, source_target_pairs={{0,8},{1,9},{2,10},{3,11},{4,12},{5,13},{6,14},{7,15},{8,0},{9,1},... | collective-permute-start | bytes 196616 | tf_op jit(solution)/shard_map/ppermute | solution.py:35
  92.1 10.1 %collective-permute-start.11 = (f32[64,256]{1,0:T(8,128)S(1)}, f32[64,256]{1,0:T(8,128)S(1)}, u32[]{:S(2)}, u32[]{:S(2)}) collective-permute-start(f32[64,256]{1,0:T(8,128)S(1)} %add.183), channel_id=1, source_target_pairs={{0,16},{1,17},{2,18},{3,19},{4,20},{5,21},{6,22},{7,23},{8,24},{9,... | collective-permute-start | bytes 196616 | tf_op jit(solution)/shard_map/ppermute | solution.py:35
  102.3 7.5 %collective-permute-start.12 = (f32[64,64]{1,0:T(8,128)S(1)}, f32[64,64]{1,0:T(8,128)S(1)}, u32[]{:S(2)}, u32[]{:S(2)}) collective-permute-start(f32[64,64]{1,0:T(8,128)S(1)} %get-tuple-element.36), channel_id=1, source_target_pairs={{0,32},{32,64},{64,96},{96,128},{128,160},{160,192},{192,224},{224... | collective-permute-start | bytes 49160 | tf_op jit(solution)/shard_map/ppermute | solution.py:22
  108.4 7.3 %collective-permute-start.13 = (f32[64,64]{1,0:T(8,128)S(1)}, f32[64,64]{1,0:T(8,128)S(1)}, u32[]{:S(2)}, u32[]{:S(2)}) collective-permute-start(f32[64,64]{1,0:T(8,128)S(1)} %get-tuple-element.35), channel_id=1, source_target_pairs={{32,0},{64,32},{96,64},{128,96},{160,128},{192,160},{224,192},{256... | collective-permute-start | bytes 49160 | tf_op jit(solution)/shard_map/ppermute | solution.py:23
  110.7 5.1 %copy-start.2 = (f32[64,128]{1,0:T(8,128)}, f32[64,128]{1,0:T(8,128)S(1)}, u32[]{:S(2)}) copy-start(f32[64,128]{1,0:T(8,128)S(1)} %scatter-add.6) | copy-start | bytes 98308

commit v2 on v1

--- a/solution.py
+++ b/solution.py
@@ -91,9 +91,15 @@
     row_cos, row_sin = twiddle(frame_rows)
     col_cos, col_sin = twiddle(frame_cols)
     extended = padded(mask, (("tile", 1),), margin)
-    spec_real = product(row_cos[:, margin : margin + band], extended)
-    spec_imag = -product(row_sin[:, margin : margin + band], extended)
-    spec_real, spec_imag = apply_right(spec_real, spec_imag, col_cos, col_sin, -1.0)
+    cols_real = product(extended, col_cos)
+    cols_imag = -product(extended, col_sin)
+    spec_real, spec_imag = apply_left(
+        row_cos[:, margin : margin + band],
+        row_sin[:, margin : margin + band],
+        -1.0,
+        cols_real,
+        cols_imag,
+    )
     kernel_index = 0
     kern_real, kern_imag = apply_left(
         row_cos[:, :width],
@@ -124,11 +130,11 @@
     drive = resist_drive(intensity, target_float, pixel_active)
     kernel_index = 0
     kern_real, kern_imag, field_real, field_imag = responses[kernel_index]
+    source_real, source_imag = apply_right(
+        drive * field_real, drive * field_imag, col_cos[:own_cols, :], col_sin[:own_cols, :], -1.0
+    )
     source_real, source_imag = apply_left(
-        row_cos[:, :band], row_sin[:, :band], -1.0, drive * field_real, drive * field_imag
-    )
-    source_real, source_imag = apply_right(
-        source_real, source_imag, col_cos[:own_cols, :], col_sin[:own_cols, :], -1.0
+        row_cos[:, :band], row_sin[:, :band], -1.0, source_real, source_imag
     )
     quot_real = source_real * kern_real + source_imag * kern_imag
     quot_imag = source_imag * kern_real - source_real * kern_imag
@@ -139,12 +145,16 @@
         quot_real,
         quot_imag,
     )
-    back = product(back_real, col_cos) - product(back_imag, col_sin)
-    frame_grad = 2.0 * weights[kernel_index] * scale / total_kernels * back
-    summed = exchange_sum(frame_grad, "kern")
-    returned = padded(edge_pixels(summed, margin), (("tile", 1),), margin)
-    mask_grad = add_returned(summed[:, margin : margin + own_cols], returned, margin)
-    return mask_grad
+    grad_scale = 2.0 * weights[kernel_index] * scale / total_kernels
+    edge_cos = edge_pixels(col_cos, margin)
+    edge_sin = edge_pixels(col_sin, margin)
+    edges = grad_scale * (product(back_real, edge_cos) - product(back_imag, edge_sin))
+    returned = padded(edges, (("tile", 1),), margin)
+    centre_cos = col_cos[:, margin : margin + own_cols]
+    centre_sin = col_sin[:, margin : margin + own_cols]
+    centre = grad_scale * (product(back_real, centre_cos) - product(back_imag, centre_sin))
+    own_grad = add_returned(centre, returned, margin)
+    return exchange_sum(own_grad, "kern")
 
 
 def solution(mesh):

time: 118 us -> 111 us (0.941)
  matrix products: 17.8 us -> 14.1 us
  waiting for transfers between devices: 46.6 us -> 43.4 us
    dot_general x36 -> x38, matrix products: 17.8 us -> 14.1 us  [product(): jnp.dot(left_mat, right_mat, precision=lax.Precision.HIGHEST, preferred_e...]
    ppermute x10, waiting for transfers between devices: 41.6 us -> 38.4 us  [exchange_sum(): value = value + lax.ppermute(value, axis, pairs)]
  transfers between devices with their start and end apart: 14 -> 14, of which waited for: 11 -> 11; matrix products, arithmetic and copies ran while one was open for 8% -> 9% of each run, Pallas kernels for 0% -> 0%
where the time goes in v2:
time: 111 us
  starting transfers between devices  44.3 us (40%)
  waiting for transfers between devices  43.4 us (39%)
  matrix products  14.1 us (13%)
  other arithmetic  5.53 us (5%)
  local copies, waits for them, and re-layouts  2.42 us (2%)
  between operations  1.16 us (1%)
    ppermute x10, waiting for transfers between devices, exchange_sum(): value = value + lax.ppermute(value, axis, pairs)  38.4 us
    ppermute x10, starting transfers between devices, exchange_sum(): value = value + lax.ppermute(value, axis, pairs)  32.2 us
    dot_general x38, matrix products, product(): jnp.dot(left_mat, right_mat, precision=lax.Precision.HIGHEST, preferred_e...  14.1 us
    ppermute x2, starting transfers between devices, padded(): before = lax.ppermute(last, axis, up)  9.46 us
    ppermute x2, waiting for transfers between devices, padded(): after = lax.ppermute(initial, axis, down)  5.04 us
    ppermute x2, starting transfers between devices, padded(): after = lax.ppermute(initial, axis, down)  2.58 us
  transfers between devices with their start and end apart: 14, of which 11 were waited for; matrix products, arithmetic and copies ran while one was open for 9% of the time, Pallas kernels for 0%

profile of v2, /device:TPU:2, one launch (start us, length us, event | category | flops | bytes accessed | tf_op | source)
XLA Modules:
  0.0 110.9 jit_solution(16610598305490331837)
XLA Ops:
  0.9 4.0 %collective-permute-start = (f32[64,64]{1,0:T(8,128)S(1)}, f32[64,64]{1,0:T(8,128)S(1)}, u32[]{:S(2)}, u32[]{:S(2)}) collective-permute-start(f32[64,64]{1,0:T(8,128)S(1)} %get-tuple-element.41), channel_id=1, source_target_pairs={{0,32},{32,64},{64,96},{96,128},{128,160},{160,192},{192,224},{224... | collective-permute-start | bytes 49160 | tf_op jit(solution)/shard_map/ppermute | solution.py:22
  4.9 1.3 %collective-permute-start.1 = (f32[64,64]{1,0:T(8,128)S(1)}, f32[64,64]{1,0:T(8,128)S(1)}, u32[]{:S(2)}, u32[]{:S(2)}) collective-permute-start(f32[64,64]{1,0:T(8,128)S(1)} %get-tuple-element.42), channel_id=1, source_target_pairs={{32,0},{64,32},{96,64},{128,96},{160,128},{192,160},{224,192},{256... | collective-permute-start | bytes 49160 | tf_op jit(solution)/shard_map/ppermute | solution.py:23
  14.9 1.3 %convolution_negate_fusion = f32[64,256]{1,0:T(8,128)S(1)} fusion(f32[64,64]{1,0:T(8,128)S(1)} %collective-permute-done.1, f32[64,128]{1,0:T(8,128)S(1)} %copy-done.1, f32[64,64]{1,0:T(8,128)S(1)} %collective-permute-done), kind=kOutput, calls=%fused_computation.20 | convolution fusion | flops 51298304 | bytes 131072 | tf_op jit(solution)/shard_map/dot_general | solution.py:41
  20.8 2.1 %collective-permute-start.2 = (f32[64,128]{1,0:T(8,128)S(1)}, f32[64,128]{1,0:T(8,128)S(1)}, u32[]{:S(2)}, u32[]{:S(2)}) collective-permute-start(f32[64,128]{1,0:T(8,128)S(1)} %get-tuple-element.43), channel_id=1, source_target_pairs={{0,1},{1,0},{2,3},{3,2},{4,5},{5,4},{6,7},{7,6},{8,9},{9,8},{10,11... | collective-permute-start | bytes 98312 | tf_op jit(solution)/shard_map/ppermute | solution.py:35
  23.9 12.3 %collective-permute-start.3 = (f32[64,128]{1,0:T(8,128)S(1)}, f32[64,128]{1,0:T(8,128)S(1)}, u32[]{:S(2)}, u32[]{:S(2)}) collective-permute-start(f32[64,128]{1,0:T(8,128)S(1)} %add.178), channel_id=1, source_target_pairs={{0,2},{1,3},{2,0},{3,1},{4,6},{5,7},{6,4},{7,5},{8,10},{9,11},{10,... | collective-permute-start | bytes 98312 | tf_op jit(solution)/shard_map/ppermute | solution.py:35
  36.2 1.9 %collective-permute-done.3 = f32[64,128]{1,0:T(8,128)S(1)} collective-permute-done((f32[64,128]{1,0:T(8,128)S(1)}, f32[64,128]{1,0:T(8,128)S(1)}, u32[]{:S(2)}, u32[]{:S(2)}) %collective-permute-start.3) | collective-permute-done | bytes 32800 | tf_op jit(solution)/shard_map/ppermute | solution.py:35
  38.1 1.9 %collective-permute-start.4 = (f32[64,128]{1,0:T(8,128)S(1)}, f32[64,128]{1,0:T(8,128)S(1)}, u32[]{:S(2)}, u32[]{:S(2)}) collective-permute-start(f32[64,128]{1,0:T(8,128)S(1)} %add.179), channel_id=1, source_target_pairs={{0,4},{1,5},{2,6},{3,7},{4,0},{5,1},{6,2},{7,3},{8,12},{9,13},{10,... | collective-permute-start | bytes 98312 | tf_op jit(solution)/shard_map/ppermute | solution.py:35
  40.0 3.9 %collective-permute-done.4 = f32[64,128]{1,0:T(8,128)S(1)} collective-permute-done((f32[64,128]{1,0:T(8,128)S(1)}, f32[64,128]{1,0:T(8,128)S(1)}, u32[]{:S(2)}, u32[]{:S(2)}) %collective-permute-start.4) | collective-permute-done | bytes 32800 | tf_op jit(solution)/shard_map/ppermute | solution.py:35
  43.9 1.9 %collective-permute-start.5 = (f32[64,128]{1,0:T(8,128)S(1)}, f32[64,128]{1,0:T(8,128)S(1)}, u32[]{:S(2)}, u32[]{:S(2)}) collective-permute-start(f32[64,128]{1,0:T(8,128)S(1)} %add.180), channel_id=1, source_target_pairs={{0,8},{1,9},{2,10},{3,11},{4,12},{5,13},{6,14},{7,15},{8,0},{9,1},... | collective-permute-start | bytes 98312 | tf_op jit(solution)/shard_map/ppermute | solution.py:35
  45.9 5.1 %collective-permute-done.5 = f32[64,128]{1,0:T(8,128)S(1)} collective-permute-done((f32[64,128]{1,0:T(8,128)S(1)}, f32[64,128]{1,0:T(8,128)S(1)}, u32[]{:S(2)}, u32[]{:S(2)}) %collective-permute-start.5) | collective-permute-done | bytes 32800 | tf_op jit(solution)/shard_map/ppermute | solution.py:35
  51.0 1.9 %collective-permute-start.6 = (f32[64,128]{1,0:T(8,128)S(1)}, f32[64,128]{1,0:T(8,128)S(1)}, u32[]{:S(2)}, u32[]{:S(2)}) collective-permute-start(f32[64,128]{1,0:T(8,128)S(1)} %add.181), channel_id=1, source_target_pairs={{0,16},{1,17},{2,18},{3,19},{4,20},{5,21},{6,22},{7,23},{8,24},{9,... | collective-permute-start | bytes 98312 | tf_op jit(solution)/shard_map/ppermute | solution.py:35
  54.0 6.7 %collective-permute-done.6 = f32[64,128]{1,0:T(8,128)S(1)} collective-permute-done((f32[64,128]{1,0:T(8,128)S(1)}, f32[64,128]{1,0:T(8,128)S(1)}, u32[]{:S(2)}, u32[]{:S(2)}) %collective-permute-start.6) | collective-permute-done | bytes 32800 | tf_op jit(solution)/shard_map/ppermute | solution.py:35
  64.7 5.4 %collective-permute-start.7 = (f32[64,64]{1,0:T(8,128)S(1)}, f32[64,64]{1,0:T(8,128)S(1)}, u32[]{:S(2)}, u32[]{:S(2)}) collective-permute-start(f32[64,64]{1,0:T(8,128)S(1)} %get-tuple-element.40), channel_id=1, source_target_pairs={{0,32},{32,64},{64,96},{96,128},{128,160},{160,192},{192,224},{224... | collective-permute-start | bytes 49160 | tf_op jit(solution)/shard_map/ppermute | solution.py:22
  70.5 1.3 %collective-permute-start.8 = (f32[64,64]{1,0:T(8,128)S(1)}, f32[64,64]{1,0:T(8,128)S(1)}, u32[]{:S(2)}, u32[]{:S(2)}) collective-permute-start(f32[64,64]{1,0:T(8,128)S(1)} %get-tuple-element.39), channel_id=1, source_target_pairs={{32,0},{64,32},{96,64},{128,96},{160,128},{192,160},{224,192},{256... | collective-permute-start | bytes 49160 | tf_op jit(solution)/shard_map/ppermute | solution.py:23
  72.7 5.0 %collective-permute-done.8 = f32[64,64]{1,0:T(8,128)S(1)} collective-permute-done((f32[64,64]{1,0:T(8,128)S(1)}, f32[64,64]{1,0:T(8,128)S(1)}, u32[]{:S(2)}, u32[]{:S(2)}) %collective-permute-start.8) | collective-permute-done | bytes 16416 | tf_op jit(solution)/shard_map/ppermute | solution.py:23
  78.3 1.9 %collective-permute-start.9 = (f32[64,128]{1,0:T(8,128)S(1)}, f32[64,128]{1,0:T(8,128)S(1)}, u32[]{:S(2)}, u32[]{:S(2)}) collective-permute-start(f32[64,128]{1,0:T(8,128)S(1)} %scatter-add.9), channel_id=1, source_target_pairs={{0,1},{1,0},{2,3},{3,2},{4,5},{5,4},{6,7},{7,6},{8,9},{9,8},{10,11... | collective-permute-start | bytes 98312 | tf_op jit(solution)/shard_map/ppermute | solution.py:35
  81.4 4.4 %collective-permute-start.10 = (f32[64,128]{1,0:T(8,128)S(1)}, f32[64,128]{1,0:T(8,128)S(1)}, u32[]{:S(2)}, u32[]{:S(2)}) collective-permute-start(f32[64,128]{1,0:T(8,128)S(1)} %add.190), channel_id=1, source_target_pairs={{0,2},{1,3},{2,0},{3,1},{4,6},{5,7},{6,4},{7,5},{8,10},{9,11},{10,... | collective-permute-start | bytes 98312 | tf_op jit(solution)/shard_map/ppermute | solution.py:35
  85.8 1.9 %collective-permute-done.10 = f32[64,128]{1,0:T(8,128)S(1)} collective-permute-done((f32[64,128]{1,0:T(8,128)S(1)}, f32[64,128]{1,0:T(8,128)S(1)}, u32[]{:S(2)}, u32[]{:S(2)}) %collective-permute-start.10) | collective-permute-done | bytes 32800 | tf_op jit(solution)/shard_map/ppermute | solution.py:35
  87.7 1.9 %collective-permute-start.11 = (f32[64,128]{1,0:T(8,128)S(1)}, f32[64,128]{1,0:T(8,128)S(1)}, u32[]{:S(2)}, u32[]{:S(2)}) collective-permute-start(f32[64,128]{1,0:T(8,128)S(1)} %add.191), channel_id=1, source_target_pairs={{0,4},{1,5},{2,6},{3,7},{4,0},{5,1},{6,2},{7,3},{8,12},{9,13},{10,... | collective-permute-start | bytes 98312 | tf_op jit(solution)/shard_map/ppermute | solution.py:35
  89.6 3.9 %collective-permute-done.11 = f32[64,128]{1,0:T(8,128)S(1)} collective-permute-done((f32[64,128]{1,0:T(8,128)S(1)}, f32[64,128]{1,0:T(8,128)S(1)}, u32[]{:S(2)}, u32[]{:S(2)}) %collective-permute-start.11) | collective-permute-done | bytes 32800 | tf_op jit(solution)/shard_map/ppermute | solution.py:35
  93.5 1.9 %collective-permute-start.12 = (f32[64,128]{1,0:T(8,128)S(1)}, f32[64,128]{1,0:T(8,128)S(1)}, u32[]{:S(2)}, u32[]{:S(2)}) collective-permute-start(f32[64,128]{1,0:T(8,128)S(1)} %add.192), channel_id=1, source_target_pairs={{0,8},{1,9},{2,10},{3,11},{4,12},{5,13},{6,14},{7,15},{8,0},{9,1},... | collective-permute-start | bytes 98312 | tf_op jit(solution)/shard_map/ppermute | solution.py:35
  95.4 5.2 %collective-permute-done.12 = f32[64,128]{1,0:T(8,128)S(1)} collective-permute-done((f32[64,128]{1,0:T(8,128)S(1)}, f32[64,128]{1,0:T(8,128)S(1)}, u32[]{:S(2)}, u32[]{:S(2)}) %collective-permute-start.12) | collective-permute-done | bytes 32800 | tf_op jit(solution)/shard_map/ppermute | solution.py:35
  100.6 1.9 %collective-permute-start.13 = (f32[64,128]{1,0:T(8,128)S(1)}, f32[64,128]{1,0:T(8,128)S(1)}, u32[]{:S(2)}, u32[]{:S(2)}) collective-permute-start(f32[64,128]{1,0:T(8,128)S(1)} %add.193), channel_id=1, source_target_pairs={{0,16},{1,17},{2,18},{3,19},{4,20},{5,21},{6,22},{7,23},{8,24},{9,... | collective-permute-start | bytes 98312 | tf_op jit(solution)/shard_map/ppermute | solution.py:35
  102.5 7.8 %collective-permute-done.13 = f32[64,128]{1,0:T(8,128)S(1)} collective-permute-done((f32[64,128]{1,0:T(8,128)S(1)}, f32[64,128]{1,0:T(8,128)S(1)}, u32[]{:S(2)}, u32[]{:S(2)}) %collective-permute-start.13) | collective-permute-done | bytes 32800 | tf_op jit(solution)/shard_map/ppermute | solution.py:35
  (80 shorter events, 23.0 us)
Async XLA Ops:
  0.9 14.0 %collective-permute-start = (f32[64,64]{1,0:T(8,128)S(1)}, f32[64,64]{1,0:T(8,128)S(1)}, u32[]{:S(2)}, u32[]{:S(2)}) collective-permute-start(f32[64,64]{1,0:T(8,128)S(1)} %get-tuple-element.41), channel_id=1, source_target_pairs={{0,32},{32,64},{64,96},{96,128},{128,160},{160,192},{192,224},{224... | collective-permute-start | bytes 49160 | tf_op jit(solution)/shard_map/ppermute | solution.py:22
  4.9 10.0 %collective-permute-start.1 = (f32[64,64]{1,0:T(8,128)S(1)}, f32[64,64]{1,0:T(8,128)S(1)}, u32[]{:S(2)}, u32[]{:S(2)}) collective-permute-start(f32[64,64]{1,0:T(8,128)S(1)} %get-tuple-element.42), channel_id=1, source_target_pairs={{32,0},{64,32},{96,64},{128,96},{160,128},{192,160},{224,192},{256... | collective-permute-start | bytes 49160 | tf_op jit(solution)/shard_map/ppermute | solution.py:23
  7.8 2.0 %copy-start = (f32[1,2,129,129]{3,1,2,0:T(2,128)S(1)}, f32[1,2,129,129]{3,1,2,0:T(2,128)}, u32[]{:S(2)}) copy-start(f32[1,2,129,129]{3,1,2,0:T(2,128)} %param.10) | copy-start | bytes 399388
  13.7 1.2 %copy-start.1 = (f32[64,128]{1,0:T(8,128)S(1)}, f32[64,128]{1,0:T(8,128)}, u32[]{:S(2)}) copy-start(f32[64,128]{1,0:T(8,128)} %param.9) | copy-start | bytes 98308
  20.8 3.1 %collective-permute-start.2 = (f32[64,128]{1,0:T(8,128)S(1)}, f32[64,128]{1,0:T(8,128)S(1)}, u32[]{:S(2)}, u32[]{:S(2)}) collective-permute-start(f32[64,128]{1,0:T(8,128)S(1)} %get-tuple-element.43), channel_id=1, source_target_pairs={{0,1},{1,0},{2,3},{3,2},{4,5},{5,4},{6,7},{7,6},{8,9},{9,8},{10,11... | collective-permute-start | bytes 98312 | tf_op jit(solution)/shard_map/ppermute | solution.py:35
  23.9 14.2 %collective-permute-start.3 = (f32[64,128]{1,0:T(8,128)S(1)}, f32[64,128]{1,0:T(8,128)S(1)}, u32[]{:S(2)}, u32[]{:S(2)}) collective-permute-start(f32[64,128]{1,0:T(8,128)S(1)} %add.178), channel_id=1, source_target_pairs={{0,2},{1,3},{2,0},{3,1},{4,6},{5,7},{6,4},{7,5},{8,10},{9,11},{10,... | collective-permute-start | bytes 98312 | tf_op jit(solution)/shard_map/ppermute | solution.py:35
  38.1 5.8 %collective-permute-start.4 = (f32[64,128]{1,0:T(8,128)S(1)}, f32[64,128]{1,0:T(8,128)S(1)}, u32[]{:S(2)}, u32[]{:S(2)}) collective-permute-start(f32[64,128]{1,0:T(8,128)S(1)} %add.179), channel_id=1, source_target_pairs={{0,4},{1,5},{2,6},{3,7},{4,0},{5,1},{6,2},{7,3},{8,12},{9,13},{10,... | collective-permute-start | bytes 98312 | tf_op jit(solution)/shard_map/ppermute | solution.py:35
  43.9 7.1 %collective-permute-start.5 = (f32[64,128]{1,0:T(8,128)S(1)}, f32[64,128]{1,0:T(8,128)S(1)}, u32[]{:S(2)}, u32[]{:S(2)}) collective-permute-start(f32[64,128]{1,0:T(8,128)S(1)} %add.180), channel_id=1, source_target_pairs={{0,8},{1,9},{2,10},{3,11},{4,12},{5,13},{6,14},{7,15},{8,0},{9,1},... | collective-permute-start | bytes 98312 | tf_op jit(solution)/shard_map/ppermute | solution.py:35
  51.0 2.0 %copy-start.3 = (s32[2,4]{1,0:T(2,128)S(1)}, s32[2,4]{1,0:T(2,128)}, u32[]{:S(2)}) copy-start(s32[2,4]{1,0:T(2,128)} %param.13) | copy-start | bytes 100
  51.0 9.7 %collective-permute-start.6 = (f32[64,128]{1,0:T(8,128)S(1)}, f32[64,128]{1,0:T(8,128)S(1)}, u32[]{:S(2)}, u32[]{:S(2)}) collective-permute-start(f32[64,128]{1,0:T(8,128)S(1)} %add.181), channel_id=1, source_target_pairs={{0,16},{1,17},{2,18},{3,19},{4,20},{5,21},{6,22},{7,23},{8,24},{9,... | collective-permute-start | bytes 98312 | tf_op jit(solution)/shard_map/ppermute | solution.py:35
  53.3 7.4 %copy-start.2 = (s32[64,128]{1,0:T(8,128)S(1)}, s32[64,128]{1,0:T(8,128)}, u32[]{:S(2)}) copy-start(s32[64,128]{1,0:T(8,128)} %param.12) | copy-start | bytes 98308
  64.7 7.1 %collective-permute-start.7 = (f32[64,64]{1,0:T(8,128)S(1)}, f32[64,64]{1,0:T(8,128)S(1)}, u32[]{:S(2)}, u32[]{:S(2)}) collective-permute-start(f32[64,64]{1,0:T(8,128)S(1)} %get-tuple-element.40), channel_id=1, source_target_pairs={{0,32},{32,64},{64,96},{96,128},{128,160},{160,192},{192,224},{224... | collective-permute-start | bytes 49160 | tf_op jit(solution)/shard_map/ppermute | solution.py:22
  70.5 7.3 %collective-permute-start.8 = (f32[64,64]{1,0:T(8,128)S(1)}, f32[64,64]{1,0:T(8,128)S(1)}, u32[]{:S(2)}, u32[]{:S(2)}) collective-permute-start(f32[64,64]{1,0:T(8,128)S(1)} %get-tuple-element.39), channel_id=1, source_target_pairs={{32,0},{64,32},{96,64},{128,96},{160,128},{192,160},{224,192},{256... | collective-permute-start | bytes 49160 | tf_op jit(solution)/shard_map/ppermute | solution.py:23
  78.3 3.1 %collective-permute-start.9 = (f32[64,128]{1,0:T(8,128)S(1)}, f32[64,128]{1,0:T(8,128)S(1)}, u32[]{:S(2)}, u32[]{:S(2)}) collective-permute-start(f32[64,128]{1,0:T(8,128)S(1)} %scatter-add.9), channel_id=1, source_target_pairs={{0,1},{1,0},{2,3},{3,2},{4,5},{5,4},{6,7},{7,6},{8,9},{9,8},{10,11... | collective-permute-start | bytes 98312 | tf_op jit(solution)/shard_map/ppermute | solution.py:35
  81.4 6.3 %collective-permute-start.10 = (f32[64,128]{1,0:T(8,128)S(1)}, f32[64,128]{1,0:T(8,128)S(1)}, u32[]{:S(2)}, u32[]{:S(2)}) collective-permute-start(f32[64,128]{1,0:T(8,128)S(1)} %add.190), channel_id=1, source_target_pairs={{0,2},{1,3},{2,0},{3,1},{4,6},{5,7},{6,4},{7,5},{8,10},{9,11},{10,... | collective-permute-start | bytes 98312 | tf_op jit(solution)/shard_map/ppermute | solution.py:35
  87.7 5.8 %collective-permute-start.11 = (f32[64,128]{1,0:T(8,128)S(1)}, f32[64,128]{1,0:T(8,128)S(1)}, u32[]{:S(2)}, u32[]{:S(2)}) collective-permute-start(f32[64,128]{1,0:T(8,128)S(1)} %add.191), channel_id=1, source_target_pairs={{0,4},{1,5},{2,6},{3,7},{4,0},{5,1},{6,2},{7,3},{8,12},{9,13},{10,... | collective-permute-start | bytes 98312 | tf_op jit(solution)/shard_map/ppermute | solution.py:35
  93.5 7.1 %collective-permute-start.12 = (f32[64,128]{1,0:T(8,128)S(1)}, f32[64,128]{1,0:T(8,128)S(1)}, u32[]{:S(2)}, u32[]{:S(2)}) collective-permute-start(f32[64,128]{1,0:T(8,128)S(1)} %add.192), channel_id=1, source_target_pairs={{0,8},{1,9},{2,10},{3,11},{4,12},{5,13},{6,14},{7,15},{8,0},{9,1},... | collective-permute-start | bytes 98312 | tf_op jit(solution)/shard_map/ppermute | solution.py:35
  100.6 9.7 %collective-permute-start.13 = (f32[64,128]{1,0:T(8,128)S(1)}, f32[64,128]{1,0:T(8,128)S(1)}, u32[]{:S(2)}, u32[]{:S(2)}) collective-permute-start(f32[64,128]{1,0:T(8,128)S(1)} %add.193), channel_id=1, source_target_pairs={{0,16},{1,17},{2,18},{3,19},{4,20},{5,21},{6,22},{7,23},{8,24},{9,... | collective-permute-start | bytes 98312 | tf_op jit(solution)/shard_map/ppermute | solution.py:35

commit v3 on v2

--- a/solution.py
+++ b/solution.py
@@ -27,14 +27,14 @@
 
 def exchange_sum(value, axis):
     peers = lax.axis_size(axis)
-    if peers & (peers - 1):
+    rows, cols = value.shape
+    if (rows * cols) % peers:
         return lax.psum(value, axis)
-    stride = 1
-    while stride < peers:
-        pairs = [(i, i ^ stride) for i in range(peers)]
-        value = value + lax.ppermute(value, axis, pairs)
-        stride *= 2
-    return value
+    parts = value.reshape(peers, rows * cols // peers)
+    parts = lax.all_to_all(parts, axis, 0, 0, tiled=True)
+    total = jnp.sum(parts, axis=0, keepdims=True)
+    gathered = lax.all_to_all(jnp.broadcast_to(total, parts.shape), axis, 0, 0, tiled=True)
+    return gathered.reshape(rows, cols)
 
 
 def product(left_mat, right_mat):

time: 111 us -> 100 us (0.901)
  the two profiles are of different devices: /device:TPU:2 before, /device:TPU:1 now
where the time goes in v3:
time: 100 us; the launch traced here: 99.7 us
  starting transfers between devices  31.3 us (31%)
  blocking collectives  24 us (24%)
  waiting for transfers between devices  18.6 us (19%)
  matrix products  14.7 us (15%)
  local copies, waits for them, and re-layouts  5.01 us (5%)
  other arithmetic  5.01 us (5%)
  between operations  1.1 us (1%)
    dot_general x38, matrix products, product(): jnp.dot(left_mat, right_mat, precision=lax.Precision.HIGHEST, preferred_e...  14.7 us
    all_to_all x1, starting transfers between devices, exchange_sum(): parts = lax.all_to_all(parts, axis, 0, 0, tiled=True)  13.6 us
    all_to_all x1, blocking collectives, exchange_sum(): parts = lax.all_to_all(parts, axis, 0, 0, tiled=True)  12.7 us
    all_to_all x1, blocking collectives, exchange_sum(): lax.all_to_all(jnp.broadcast_to(total, parts.shape), axis, 0, 0, tiled=True)  11.3 us
    ppermute x2, starting transfers between devices, padded(): before = lax.ppermute(last, axis, up)  11.2 us
    all_to_all x1, waiting for transfers between devices, exchange_sum(): parts = lax.all_to_all(parts, axis, 0, 0, tiled=True)  8.16 us
    all_to_all x1, waiting for transfers between devices, exchange_sum(): lax.all_to_all(jnp.broadcast_to(total, parts.shape), axis, 0, 0, tiled=True)  6.51 us
    ppermute x2, waiting for transfers between devices, padded(): after = lax.ppermute(initial, axis, down)  3.91 us
  transfers between devices with their start and end apart: 6, of which 3 were waited for; matrix products, arithmetic and copies ran while one was open for 10% of the time, Pallas kernels for 0%

profile of v3, /device:TPU:1, one launch (start us, length us, event | category | flops | bytes accessed | tf_op | source)
XLA Modules:
  0.0 99.7 jit_solution(8031882194847422405)
XLA Ops:
  0.0 0.9 fusion.103
  0.9 5.5 %collective-permute-start = (f32[64,64]{1,0:T(8,128)S(1)}, f32[64,64]{1,0:T(8,128)S(1)}, u32[]{:S(2)}, u32[]{:S(2)}) collective-permute-start(f32[64,64]{1,0:T(8,128)S(1)} %get-tuple-element.41), channel_id=1, source_target_pairs={{0,32},{32,64},{64,96},{96,128},{128,160},{160,192},{192,224},{224... | collective-permute-start | bytes 49160 | tf_op jit(solution)/shard_map/ppermute | solution.py:22
  6.4 1.3 %collective-permute-start.1 = (f32[64,64]{1,0:T(8,128)S(1)}, f32[64,64]{1,0:T(8,128)S(1)}, u32[]{:S(2)}, u32[]{:S(2)}) collective-permute-start(f32[64,64]{1,0:T(8,128)S(1)} %get-tuple-element.42), channel_id=1, source_target_pairs={{32,0},{64,32},{96,64},{128,96},{160,128},{192,160},{224,192},{256... | collective-permute-start | bytes 49160 | tf_op jit(solution)/shard_map/ppermute | solution.py:23
  7.7 0.8 fusion.17
  8.4 0.8 fusion.16
  9.2 1.0 fusion.36
  10.2 1.0 fusion.35
  16.4 1.3 %convolution_negate_fusion = f32[64,256]{1,0:T(8,128)S(1)} fusion(f32[64,64]{1,0:T(8,128)S(1)} %collective-permute-done.1, f32[64,128]{1,0:T(8,128)S(1)} %copy-done.1, f32[64,64]{1,0:T(8,128)S(1)} %collective-permute-done), kind=kOutput, calls=%fused_computation.20 | convolution fusion | flops 51298304 | bytes 131072 | tf_op jit(solution)/shard_map/dot_general | solution.py:41
  18.0 1.2 %fusion.55 = f32[64,256]{1,0:T(8,128)S(1)} fusion(f32[64,64]{1,0:T(8,128)S(1)} %collective-permute-done.1, f32[64,128]{1,0:T(8,128)S(1)} %copy-done.1, f32[64,64]{1,0:T(8,128)S(1)} %collective-permute-done), kind=kOutput, calls=%fused_computation.89 | convolution fusion | flops 51281920 | bytes 131072 | tf_op jit(solution)/shard_map/dot_general | solution.py:41
  22.0 0.8 multiply_multiply_fusion
  22.8 13.6 %all-to-all-start = ((f32[32,1,256]{2,1,0:T(1,128)}), f32[32,1,256]{2,1,0:T(1,128)S(1)}, u32[]{:S(2)}, u32[]{:S(2)}) async-start(f32[32,1,256]{2,1,0:T(1,128)} %bitcast.3), calls=%async_computation | async-start | bytes 65536 | tf_op jit(solution)/shard_map/all_to_all | solution.py:34
  36.5 8.2 %all-to-all-done = f32[32,1,256]{2,1,0:T(1,128)S(1)} async-done(((f32[32,1,256]{2,1,0:T(1,128)}), f32[32,1,256]{2,1,0:T(1,128)S(1)}, u32[]{:S(2)}, u32[]{:S(2)}) %all-to-all-start) | async-done | bytes 32800 | tf_op jit(solution)/shard_map/all_to_all | solution.py:34
  44.7 0.6 broadcast_in_dim.8
  45.4 3.9 %all-to-all-start.1 = ((f32[32,1,256]{2,1,0:T(1,128)}), f32[32,1,256]{2,1,0:T(1,128)S(1)}, u32[]{:S(2)}, u32[]{:S(2)}) async-start(f32[32,1,256]{2,1,0:T(1,128)} %broadcast_in_dim.8), calls=%async_computation.1 | async-start | bytes 65536 | tf_op jit(solution)/shard_map/all_to_all | solution.py:36
  50.3 0.7 compare_reduce_fusion
  51.0 6.5 %all-to-all-done.1 = f32[32,1,256]{2,1,0:T(1,128)S(1)} async-done(((f32[32,1,256]{2,1,0:T(1,128)}), f32[32,1,256]{2,1,0:T(1,128)S(1)}, u32[]{:S(2)}, u32[]{:S(2)}) %all-to-all-start.1) | async-done | bytes 32800 | tf_op jit(solution)/shard_map/all_to_all | solution.py:36
  57.6 0.7 copy-done.2
  62.3 5.8 %collective-permute-start.2 = (f32[64,64]{1,0:T(8,128)S(1)}, f32[64,64]{1,0:T(8,128)S(1)}, u32[]{:S(2)}, u32[]{:S(2)}) collective-permute-start(f32[64,64]{1,0:T(8,128)S(1)} %get-tuple-element.40), channel_id=1, source_target_pairs={{0,32},{32,64},{64,96},{96,128},{128,160},{160,192},{192,224},{224... | collective-permute-start | bytes 49160 | tf_op jit(solution)/shard_map/ppermute | solution.py:22
  68.4 1.3 %collective-permute-start.3 = (f32[64,64]{1,0:T(8,128)S(1)}, f32[64,64]{1,0:T(8,128)S(1)}, u32[]{:S(2)}, u32[]{:S(2)}) collective-permute-start(f32[64,64]{1,0:T(8,128)S(1)} %get-tuple-element.39), channel_id=1, source_target_pairs={{32,0},{64,32},{96,64},{128,96},{160,128},{192,160},{224,192},{256... | collective-permute-start | bytes 49160 | tf_op jit(solution)/shard_map/ppermute | solution.py:23
  69.7 0.6 add_select_fusion.2
  70.7 3.9 %collective-permute-done.3 = f32[64,64]{1,0:T(8,128)S(1)} collective-permute-done((f32[64,64]{1,0:T(8,128)S(1)}, f32[64,64]{1,0:T(8,128)S(1)}, u32[]{:S(2)}, u32[]{:S(2)}) %collective-permute-start.3) | collective-permute-done | bytes 16416 | tf_op jit(solution)/shard_map/ppermute | solution.py:23
  75.1 12.7 %all_to_all.30 = f32[32,1,256]{2,1,0:T(1,128)S(1)} all-to-all(f32[32,1,256]{2,1,0:T(1,128)S(1)} %bitcast.47), channel_id=1, replica_groups=mesh['tile'=32,'kern'=32] {'kern'}, dimensions={0} | all-to-all | bytes 65536 | tf_op jit(solution)/shard_map/all_to_all | solution.py:34
  87.9 11.3 %all_to_all.31 = f32[32,1,256]{2,1,0:T(1,128)S(1)} all-to-all(f32[32,1,256]{2,1,0:T(1,128)S(1)} %broadcast_in_dim.11), channel_id=1, replica_groups=mesh['tile'=32,'kern'=32] {'kern'}, dimensions={0} | all-to-all | bytes 65536 | tf_op jit(solution)/shard_map/all_to_all | solution.py:36
  99.1 0.6 copy.46
  (64 shorter events, 13.7 us)
Async XLA Ops:
  0.9 15.4 %collective-permute-start = (f32[64,64]{1,0:T(8,128)S(1)}, f32[64,64]{1,0:T(8,128)S(1)}, u32[]{:S(2)}, u32[]{:S(2)}) collective-permute-start(f32[64,64]{1,0:T(8,128)S(1)} %get-tuple-element.41), channel_id=1, source_target_pairs={{0,32},{32,64},{64,96},{96,128},{128,160},{160,192},{192,224},{224... | collective-permute-start | bytes 49160 | tf_op jit(solution)/shard_map/ppermute | solution.py:22
  6.4 10.0 %collective-permute-start.1 = (f32[64,64]{1,0:T(8,128)S(1)}, f32[64,64]{1,0:T(8,128)S(1)}, u32[]{:S(2)}, u32[]{:S(2)}) collective-permute-start(f32[64,64]{1,0:T(8,128)S(1)} %get-tuple-element.42), channel_id=1, source_target_pairs={{32,0},{64,32},{96,64},{128,96},{160,128},{192,160},{224,192},{256... | collective-permute-start | bytes 49160 | tf_op jit(solution)/shard_map/ppermute | solution.py:23
  9.2 2.0 %copy-start = (f32[1,2,129,129]{3,1,2,0:T(2,128)S(1)}, f32[1,2,129,129]{3,1,2,0:T(2,128)}, u32[]{:S(2)}) copy-start(f32[1,2,129,129]{3,1,2,0:T(2,128)} %param.10) | copy-start | bytes 399388
  15.1 1.2 %copy-start.1 = (f32[64,128]{1,0:T(8,128)S(1)}, f32[64,128]{1,0:T(8,128)}, u32[]{:S(2)}) copy-start(f32[64,128]{1,0:T(8,128)} %param.9) | copy-start | bytes 98308
  22.8 21.9 %all-to-all-start = ((f32[32,1,256]{2,1,0:T(1,128)}), f32[32,1,256]{2,1,0:T(1,128)S(1)}, u32[]{:S(2)}, u32[]{:S(2)}) async-start(f32[32,1,256]{2,1,0:T(1,128)} %bitcast.3), calls=%async_computation | async-start | bytes 65536 | tf_op jit(solution)/shard_map/all_to_all | solution.py:34
  45.4 12.2 %all-to-all-start.1 = ((f32[32,1,256]{2,1,0:T(1,128)}), f32[32,1,256]{2,1,0:T(1,128)S(1)}, u32[]{:S(2)}, u32[]{:S(2)}) async-start(f32[32,1,256]{2,1,0:T(1,128)} %broadcast_in_dim.8), calls=%async_computation.1 | async-start | bytes 65536 | tf_op jit(solution)/shard_map/all_to_all | solution.py:36
  49.3 0.7 copy-start.3
  57.6 0.8 copy-start.2
  62.3 7.4 %collective-permute-start.2 = (f32[64,64]{1,0:T(8,128)S(1)}, f32[64,64]{1,0:T(8,128)S(1)}, u32[]{:S(2)}, u32[]{:S(2)}) collective-permute-start(f32[64,64]{1,0:T(8,128)S(1)} %get-tuple-element.40), channel_id=1, source_target_pairs={{0,32},{32,64},{64,96},{96,128},{128,160},{160,192},{192,224},{224... | collective-permute-start | bytes 49160 | tf_op jit(solution)/shard_map/ppermute | solution.py:22
  68.4 6.2 %collective-permute-start.3 = (f32[64,64]{1,0:T(8,128)S(1)}, f32[64,64]{1,0:T(8,128)S(1)}, u32[]{:S(2)}, u32[]{:S(2)}) collective-permute-start(f32[64,64]{1,0:T(8,128)S(1)} %get-tuple-element.39), channel_id=1, source_target_pairs={{32,0},{64,32},{96,64},{128,96},{160,128},{192,160},{224,192},{256... | collective-permute-start | bytes 49160 | tf_op jit(solution)/shard_map/ppermute | solution.py:23

commit v4 on v3

--- a/solution.py
+++ b/solution.py
@@ -1,6 +1,7 @@
 import math
 
 import jax
+import numpy as np
 import jax.numpy as jnp
 from jax import lax
 from jax.sharding import PartitionSpec as P
@@ -44,10 +45,9 @@
 
 
 def twiddle(length):
-    series = jnp.arange(length, dtype=jnp.int32)
-    phase = series[:, None] * series[None, :] % length
-    angle = phase.astype(jnp.float32) * (2.0 * math.pi / length)
-    return (jnp.cos(angle), jnp.sin(angle))
+    series = np.arange(length, dtype=np.int64)
+    angle = (series[:, None] * series[None, :] % length) * (2.0 * math.pi / length)
+    return (jnp.asarray(np.cos(angle), jnp.float32), jnp.asarray(np.sin(angle), jnp.float32))
 
 
 def apply_left(cosine, sine, sign, real_part, imag_part):
@@ -90,6 +90,7 @@
     scale = 1.0 / (frame_rows * frame_cols)
     row_cos, row_sin = twiddle(frame_rows)
     col_cos, col_sin = twiddle(frame_cols)
+    row_cos, row_sin, col_cos, col_sin = lax.optimization_barrier((row_cos, row_sin, col_cos, col_sin))
     extended = padded(mask, (("tile", 1),), margin)
     cols_real = product(extended, col_cos)
     cols_imag = -product(extended, col_sin)

time: 100 us -> 96.4 us (0.964)
  blocking collectives: 24 us -> 48.9 us
  starting transfers between devices: 31.3 us -> 14.3 us
  waiting for transfers between devices: 18.6 us -> 10.4 us
  other arithmetic: 5.01 us -> 1.57 us
  matrix products: 14.7 us -> 12.2 us
  local copies, waits for them, and re-layouts: 5.01 us -> 7.21 us
    all_to_all x1 -> x2, blocking collectives: 12.7 us -> 37.6 us  [exchange_sum(): parts = lax.all_to_all(parts, axis, 0, 0, tiled=True)]
    all_to_all x1 -> x0, starting transfers between devices: 13.6 us -> none  [exchange_sum(): parts = lax.all_to_all(parts, axis, 0, 0, tiled=True)]
    all_to_all x1 -> x0, waiting for transfers between devices: 8.16 us -> none  [exchange_sum(): parts = lax.all_to_all(parts, axis, 0, 0, tiled=True)]
    ppermute x2, starting transfers between devices: 11.2 us -> 7.87 us  [padded(): before = lax.ppermute(last, axis, up)]
    dot_general x38, matrix products: 14.7 us -> 12.2 us  [product(): jnp.dot(left_mat, right_mat, precision=lax.Precision.HIGHEST, preferred_e...]
    sin x2 -> x0, other arithmetic: 1.73 us -> none  [twiddle(): return (jnp.cos(angle), jnp.sin(angle))]
    cos x2 -> x0, other arithmetic: 1.72 us -> none  [twiddle(): return (jnp.cos(angle), jnp.sin(angle))]
    unnamed x9 -> x15, local copies, waits for them, and re-layouts: 1.94 us -> 3.14 us
  transfers between devices with their start and end apart: 6 -> 5, of which waited for: 3 -> 2; matrix products, arithmetic and copies ran while one was open for 10% -> 8% of each run, Pallas kernels for 0% -> 0%
where the time goes in v4:
time: 96.4 us; the launch traced here: 95.7 us
  blocking collectives  48.9 us (51%)
  starting transfers between devices  14.3 us (15%)
  matrix products  12.2 us (13%)
  waiting for transfers between devices  10.4 us (11%)
  local copies, waits for them, and re-layouts  7.21 us (7%)
  other arithmetic  1.57 us (2%)
  between operations  1.08 us (1%)
    all_to_all x2, blocking collectives, exchange_sum(): parts = lax.all_to_all(parts, axis, 0, 0, tiled=True)  37.6 us
    dot_general x38, matrix products, product(): jnp.dot(left_mat, right_mat, precision=lax.Precision.HIGHEST, preferred_e...  12.2 us
    all_to_all x1, blocking collectives, exchange_sum(): lax.all_to_all(jnp.broadcast_to(total, parts.shape), axis, 0, 0, tiled=True)  11.3 us
    ppermute x2, starting transfers between devices, padded(): before = lax.ppermute(last, axis, up)  7.87 us
    all_to_all x1, waiting for transfers between devices, exchange_sum(): lax.all_to_all(jnp.broadcast_to(total, parts.shape), axis, 0, 0, tiled=True)  6.51 us
    ppermute x2, waiting for transfers between devices, padded(): after = lax.ppermute(initial, axis, down)  3.91 us
    all_to_all x1, starting transfers between devices, exchange_sum(): lax.all_to_all(jnp.broadcast_to(total, parts.shape), axis, 0, 0, tiled=True)  3.9 us
    unnamed x15, local copies, waits for them, and re-layouts  3.14 us
  transfers between devices with their start and end apart: 5, of which 2 were waited for; matrix products, arithmetic and copies ran while one was open for 8% of the time, Pallas kernels for 0%

profile of v4, /device:TPU:1, one launch (start us, length us, event | category | flops | bytes accessed | tf_op | source)
XLA Modules:
  0.0 95.7 jit_solution(6670559266074190768)
XLA Ops:
  0.0 0.9 fusion.78
  0.9 1.3 %collective-permute-start.1 = (f32[64,64]{1,0:T(8,128)S(1)}, f32[64,64]{1,0:T(8,128)S(1)}, u32[]{:S(2)}, u32[]{:S(2)}) collective-permute-start(f32[64,64]{1,0:T(8,128)S(1)} %get-tuple-element.50), channel_id=1, source_target_pairs={{32,0},{64,32},{96,64},{128,96},{160,128},{192,160},{224,192},{256... | collective-permute-start | bytes 49160 | tf_op jit(solution)/shard_map/ppermute | solution.py:24
  2.2 6.2 %collective-permute-start = (f32[64,64]{1,0:T(8,128)S(1)}, f32[64,64]{1,0:T(8,128)S(1)}, u32[]{:S(2)}, u32[]{:S(2)}) collective-permute-start(f32[64,64]{1,0:T(8,128)S(1)} %get-tuple-element.49), channel_id=1, source_target_pairs={{0,32},{32,64},{64,96},{96,128},{128,160},{160,192},{192,224},{224... | collective-permute-start | bytes 49160 | tf_op jit(solution)/shard_map/ppermute | solution.py:23
  8.4 1.3 %fusion.74 = (f32[1,1,129,129]{3,1,2,0:T(1,128)S(1)}, f32[1,1,129,129]{3,1,2,0:T(1,128)S(1)}) fusion(f32[1,2,129,129]{3,1,2,0:T(2,128)} %param.14), kind=kLoop, calls=%fused_computation.110 | loop fusion | bytes 266256 | tf_op jit(solution)/shard_map/slice | solution.py:110
  9.7 0.5 fusion.8
  11.7 0.5 convolution_subtract_fusion.3
  12.6 0.5 fusion.24
  13.2 0.5 fusion.26
  14.2 0.5 convolution_add_fusion.2
  14.7 0.6 convolution_subtract_fusion.2
  19.9 24.9 %all_to_all.30 = f32[32,1,256]{2,1,0:T(1,128)S(1)} all-to-all(f32[32,1,256]{2,1,0:T(1,128)S(1)} %bitcast.51), channel_id=1, replica_groups=mesh['tile'=32,'kern'=32] {'kern'}, dimensions={0} | all-to-all | bytes 65536 | tf_op jit(solution)/shard_map/all_to_all | solution.py:35
  44.9 0.6 broadcast_in_dim.8
  45.5 3.9 %all-to-all-start.1 = ((f32[32,1,256]{2,1,0:T(1,128)}), f32[32,1,256]{2,1,0:T(1,128)S(1)}, u32[]{:S(2)}, u32[]{:S(2)}) async-start(f32[32,1,256]{2,1,0:T(1,128)} %broadcast_in_dim.8), calls=%async_computation.1 | async-start | bytes 65536 | tf_op jit(solution)/shard_map/all_to_all | solution.py:37
  49.6 0.5 copy-done.6
  50.4 0.7 compare_reduce_fusion
  51.2 6.5 %all-to-all-done.1 = f32[32,1,256]{2,1,0:T(1,128)S(1)} async-done(((f32[32,1,256]{2,1,0:T(1,128)}), f32[32,1,256]{2,1,0:T(1,128)S(1)}, u32[]{:S(2)}, u32[]{:S(2)}) %all-to-all-start.1) | async-done | bytes 32800 | tf_op jit(solution)/shard_map/all_to_all | solution.py:37
  57.7 0.7 copy-done.5
  62.5 1.6 %collective-permute-start.2 = (f32[64,64]{1,0:T(8,128)S(1)}, f32[64,64]{1,0:T(8,128)S(1)}, u32[]{:S(2)}, u32[]{:S(2)}) collective-permute-start(f32[64,64]{1,0:T(8,128)S(1)} %get-tuple-element.48), channel_id=1, source_target_pairs={{0,32},{32,64},{64,96},{96,128},{128,160},{160,192},{192,224},{224... | collective-permute-start | bytes 49160 | tf_op jit(solution)/shard_map/ppermute | solution.py:23
  64.4 1.3 %collective-permute-start.3 = (f32[64,64]{1,0:T(8,128)S(1)}, f32[64,64]{1,0:T(8,128)S(1)}, u32[]{:S(2)}, u32[]{:S(2)}) collective-permute-start(f32[64,64]{1,0:T(8,128)S(1)} %get-tuple-element.47), channel_id=1, source_target_pairs={{32,0},{64,32},{96,64},{128,96},{160,128},{192,160},{224,192},{256... | collective-permute-start | bytes 49160 | tf_op jit(solution)/shard_map/ppermute | solution.py:24
  65.7 0.6 add_select_fusion
  66.7 3.9 %collective-permute-done.3 = f32[64,64]{1,0:T(8,128)S(1)} collective-permute-done((f32[64,64]{1,0:T(8,128)S(1)}, f32[64,64]{1,0:T(8,128)S(1)}, u32[]{:S(2)}, u32[]{:S(2)}) %collective-permute-start.3) | collective-permute-done | bytes 16416 | tf_op jit(solution)/shard_map/ppermute | solution.py:24
  71.1 12.7 %all_to_all.31 = f32[32,1,256]{2,1,0:T(1,128)S(1)} all-to-all(f32[32,1,256]{2,1,0:T(1,128)S(1)} %bitcast.49), channel_id=1, replica_groups=mesh['tile'=32,'kern'=32] {'kern'}, dimensions={0} | all-to-all | bytes 65536 | tf_op jit(solution)/shard_map/all_to_all | solution.py:35
  83.9 11.3 %all_to_all.32 = f32[32,1,256]{2,1,0:T(1,128)S(1)} all-to-all(f32[32,1,256]{2,1,0:T(1,128)S(1)} %broadcast_in_dim.21), channel_id=1, replica_groups=mesh['tile'=32,'kern'=32] {'kern'}, dimensions={0} | all-to-all | bytes 65536 | tf_op jit(solution)/shard_map/all_to_all | solution.py:37
  95.1 0.6 copy.50
  (64 shorter events, 11.7 us)
Async XLA Ops:
  0.9 15.0 %collective-permute-start.1 = (f32[64,64]{1,0:T(8,128)S(1)}, f32[64,64]{1,0:T(8,128)S(1)}, u32[]{:S(2)}, u32[]{:S(2)}) collective-permute-start(f32[64,64]{1,0:T(8,128)S(1)} %get-tuple-element.50), channel_id=1, source_target_pairs={{32,0},{64,32},{96,64},{128,96},{160,128},{192,160},{224,192},{256... | collective-permute-start | bytes 49160 | tf_op jit(solution)/shard_map/ppermute | solution.py:24
  2.2 7.5 %copy-start.3 = (f32[192,192]{1,0:T(8,128)S(1)}, f32[192,192]{1,0:T(8,128)}, u32[]{:S(2)}) copy-start(f32[192,192]{1,0:T(8,128)} %constant.90.clone) | copy-start | bytes 442372
  2.2 13.7 %collective-permute-start = (f32[64,64]{1,0:T(8,128)S(1)}, f32[64,64]{1,0:T(8,128)S(1)}, u32[]{:S(2)}, u32[]{:S(2)}) collective-permute-start(f32[64,64]{1,0:T(8,128)S(1)} %get-tuple-element.49), channel_id=1, source_target_pairs={{0,32},{32,64},{64,96},{96,128},{128,160},{160,192},{192,224},{224... | collective-permute-start | bytes 49160 | tf_op jit(solution)/shard_map/ppermute | solution.py:23
  10.2 0.9 copy-start.2
  11.7 1.0 copy-start.1
  13.2 1.0 copy-start
  14.7 1.2 %copy-start.4 = (f32[64,128]{1,0:T(8,128)S(1)}, f32[64,128]{1,0:T(8,128)}, u32[]{:S(2)}) copy-start(f32[64,128]{1,0:T(8,128)} %param.13) | copy-start | bytes 98308
  45.5 12.2 %all-to-all-start.1 = ((f32[32,1,256]{2,1,0:T(1,128)}), f32[32,1,256]{2,1,0:T(1,128)S(1)}, u32[]{:S(2)}, u32[]{:S(2)}) async-start(f32[32,1,256]{2,1,0:T(1,128)} %broadcast_in_dim.8), calls=%async_computation.1 | async-start | bytes 65536 | tf_op jit(solution)/shard_map/all_to_all | solution.py:37
  49.4 0.7 copy-start.6
  57.7 0.8 copy-start.5
  62.5 3.3 %collective-permute-start.2 = (f32[64,64]{1,0:T(8,128)S(1)}, f32[64,64]{1,0:T(8,128)S(1)}, u32[]{:S(2)}, u32[]{:S(2)}) collective-permute-start(f32[64,64]{1,0:T(8,128)S(1)} %get-tuple-element.48), channel_id=1, source_target_pairs={{0,32},{32,64},{64,96},{96,128},{128,160},{160,192},{192,224},{224... | collective-permute-start | bytes 49160 | tf_op jit(solution)/shard_map/ppermute | solution.py:23
  64.4 6.2 %collective-permute-start.3 = (f32[64,64]{1,0:T(8,128)S(1)}, f32[64,64]{1,0:T(8,128)S(1)}, u32[]{:S(2)}, u32[]{:S(2)}) collective-permute-start(f32[64,64]{1,0:T(8,128)S(1)} %get-tuple-element.47), channel_id=1, source_target_pairs={{32,0},{64,32},{96,64},{128,96},{160,128},{192,160},{224,192},{256... | collective-permute-start | bytes 49160 | tf_op jit(solution)/shard_map/ppermute | solution.py:24

commit v5 on v4

--- a/solution.py
+++ b/solution.py
@@ -84,14 +84,19 @@
     band, own_cols = mask.shape
     width = kernels.shape[-1]
     margin = (width - 1) // 2
+    reach = 2 * margin
+    field_cols = own_cols + reach
     frame_rows = band + 2 * margin
-    frame_cols = own_cols + 2 * margin
+    frame_cols = own_cols + 2 * reach
     total_kernels = kernels.shape[0] * lax.axis_size("kern")
     scale = 1.0 / (frame_rows * frame_cols)
     row_cos, row_sin = twiddle(frame_rows)
     col_cos, col_sin = twiddle(frame_cols)
     row_cos, row_sin, col_cos, col_sin = lax.optimization_barrier((row_cos, row_sin, col_cos, col_sin))
-    extended = padded(mask, (("tile", 1),), margin)
+    extended = padded(mask, (("tile", 1),), reach)
+    block_cols = own_cols // active.shape[1]
+    target_ext = padded(target.astype(jnp.float32), (("tile", 1),), margin)
+    active_ext = padded(active.astype(jnp.float32), (("tile", 1),), margin // block_cols)
     cols_real = product(extended, col_cos)
     cols_imag = -product(extended, col_sin)
     spec_real, spec_imag = apply_left(
@@ -118,21 +123,21 @@
         row_cos[:band, :], row_sin[:band, :], 1.0, prod_real, prod_imag
     )
     field_real, field_imag = apply_right(
-        field_real, field_imag, col_cos[:, :own_cols], col_sin[:, :own_cols], 1.0
+        field_real, field_imag, col_cos[:, :field_cols], col_sin[:, :field_cols], 1.0
     )
     field_real = field_real * scale
     field_imag = field_imag * scale
-    responses = [(kern_real, kern_imag, field_real, field_imag)]
     share_sum = weights[kernel_index] * (field_real * field_real + field_imag * field_imag)
     share_sum = share_sum / total_kernels
-    target_float = target.astype(jnp.float32)
-    pixel_active = jnp.repeat(jnp.repeat(active, BLK, axis=0), BLK, axis=1).astype(jnp.float32)
+    pixel_active = jnp.repeat(jnp.repeat(active_ext, BLK, axis=0), block_cols, axis=1)
     intensity = exchange_sum(share_sum, "kern")
-    drive = resist_drive(intensity, target_float, pixel_active)
-    kernel_index = 0
-    kern_real, kern_imag, field_real, field_imag = responses[kernel_index]
+    drive = resist_drive(intensity, target_ext, pixel_active)
     source_real, source_imag = apply_right(
-        drive * field_real, drive * field_imag, col_cos[:own_cols, :], col_sin[:own_cols, :], -1.0
+        drive * field_real,
+        drive * field_imag,
+        col_cos[:field_cols, :],
+        col_sin[:field_cols, :],
+        -1.0,
     )
     source_real, source_imag = apply_left(
         row_cos[:, :band], row_sin[:, :band], -1.0, source_real, source_imag
@@ -147,14 +152,9 @@
         quot_imag,
     )
     grad_scale = 2.0 * weights[kernel_index] * scale / total_kernels
-    edge_cos = edge_pixels(col_cos, margin)
-    edge_sin = edge_pixels(col_sin, margin)
-    edges = grad_scale * (product(back_real, edge_cos) - product(back_imag, edge_sin))
-    returned = padded(edges, (("tile", 1),), margin)
-    centre_cos = col_cos[:, margin : margin + own_cols]
-    centre_sin = col_sin[:, margin : margin + own_cols]
-    centre = grad_scale * (product(back_real, centre_cos) - product(back_imag, centre_sin))
-    own_grad = add_returned(centre, returned, margin)
+    own_cos = col_cos[:, reach : reach + own_cols]
+    own_sin = col_sin[:, reach : reach + own_cols]
+    own_grad = grad_scale * (product(back_real, own_cos) - product(back_imag, own_sin))
     return exchange_sum(own_grad, "kern")
 
 

time: 96.4 us -> 100 us (1.037)
  the two profiles are of different devices: /device:TPU:1 before, /device:TPU:453 now
where the time goes in v5:
time: 100 us; the launch traced here: 99.8 us
  starting transfers between devices  43.5 us (44%)
  blocking collectives  29.5 us (30%)
  matrix products  14.6 us (15%)
  waiting for transfers between devices  5.66 us (6%)
  local copies, waits for them, and re-layouts  4.96 us (5%)
  between operations  1.12 us (1%)
    ppermute x3, starting transfers between devices, padded(): before = lax.ppermute(last, axis, up)  18.6 us
    all_to_all x1, blocking collectives, exchange_sum(): parts = lax.all_to_all(parts, axis, 0, 0, tiled=True)  18.2 us
    dot_general x36, matrix products, product(): jnp.dot(left_mat, right_mat, precision=lax.Precision.HIGHEST, preferred_e...  14.6 us
    all_to_all x1, blocking collectives, exchange_sum(): lax.all_to_all(jnp.broadcast_to(total, parts.shape), axis, 0, 0, tiled=True)  11.3 us
    all_to_all x1, starting transfers between devices, exchange_sum(): parts = lax.all_to_all(parts, axis, 0, 0, tiled=True)  9.87 us
    all_to_all x1, starting transfers between devices, exchange_sum(): lax.all_to_all(jnp.broadcast_to(total, parts.shape), axis, 0, 0, tiled=True)  9.15 us
    ppermute x3, starting transfers between devices, padded(): after = lax.ppermute(initial, axis, down)  5.94 us
    ppermute x3, waiting for transfers between devices, padded(): after = lax.ppermute(initial, axis, down)  5.65 us
  transfers between devices with their start and end apart: 8, of which 1 were waited for; matrix products, arithmetic and copies ran while one was open for 7% of the time, Pallas kernels for 0%

profile of v5, /device:TPU:453, one launch (start us, length us, event | category | flops | bytes accessed | tf_op | source)
XLA Modules:
  0.0 99.8 jit_solution(13362321753514691494)
XLA Ops:
  0.0 5.3 %collective-permute-start = (f32[64,128]{1,0:T(8,128)}, f32[64,128]{1,0:T(8,128)S(1)}, u32[]{:S(2)}, u32[]{:S(2)}) collective-permute-start(f32[64,128]{1,0:T(8,128)} %param.9), channel_id=1, source_target_pairs={{0,32},{32,64},{64,96},{96,128},{128,160},{160,192},{192,224},{224... | collective-permute-start | bytes 98312 | tf_op jit(solution)/shard_map/ppermute | solution.py:23
  5.3 1.9 %collective-permute-start.1 = (f32[64,128]{1,0:T(8,128)}, f32[64,128]{1,0:T(8,128)S(1)}, u32[]{:S(2)}, u32[]{:S(2)}) collective-permute-start(f32[64,128]{1,0:T(8,128)} %param.9), channel_id=1, source_target_pairs={{32,0},{64,32},{96,64},{128,96},{160,128},{192,160},{224,192},{256... | collective-permute-start | bytes 98312 | tf_op jit(solution)/shard_map/ppermute | solution.py:24
  7.2 1.3 %fusion.70 = (f32[1,1,129,129]{3,1,2,0:T(1,128)S(1)}, f32[1,1,129,129]{3,1,2,0:T(1,128)S(1)}) fusion(f32[1,2,129,129]{3,1,2,0:T(2,128)} %param.10), kind=kLoop, calls=%fused_computation.103 | loop fusion | bytes 266256 | tf_op jit(solution)/shard_map/slice | solution.py:115
  9.0 0.5 fusion.28
  9.9 0.5 convolution_subtract_fusion.1
  10.5 0.5 convolution_add_fusion.1
  11.0 0.6 fusion.24
  11.6 0.6 fusion.22
  12.3 0.6 convolution_subtract_fusion
  12.9 0.6 convolution_add_fusion
  14.3 0.7 copy-done.4
  17.3 0.5 multiply_subtract_fusion.1
  20.5 0.7 all_to_all.26
  21.2 9.9 %all-to-all-start = ((f32[32,1,512]{2,1,0:T(1,128)}), f32[32,1,512]{2,1,0:T(1,128)S(1)}, u32[]{:S(2)}, u32[]{:S(2)}) async-start(f32[32,1,512]{2,1,0:T(1,128)} %all_to_all.26), calls=%async_computation | async-start | bytes 131072 | tf_op jit(solution)/shard_map/all_to_all | solution.py:35
  31.1 6.7 %collective-permute-start.4 = (f32[2,2]{1,0:T(2,128)S(1)}, f32[2,2]{1,0:T(2,128)S(1)}, u32[]{:S(2)}, u32[]{:S(2)}) collective-permute-start(f32[2,2]{1,0:T(2,128)S(1)} %get-tuple-element.21), channel_id=1, source_target_pairs={{0,32},{32,64},{64,96},{96,128},{128,160},{160,192},{192,224},{224... | collective-permute-start | bytes 56 | tf_op jit(solution)/shard_map/ppermute | solution.py:23
  37.8 1.9 %collective-permute-start.5 = (f32[2,2]{1,0:T(2,128)S(1)}, f32[2,2]{1,0:T(2,128)S(1)}, u32[]{:S(2)}, u32[]{:S(2)}) collective-permute-start(f32[2,2]{1,0:T(2,128)S(1)} %get-tuple-element.22), channel_id=1, source_target_pairs={{32,0},{64,32},{96,64},{128,96},{160,128},{192,160},{224,192},{256... | collective-permute-start | bytes 56 | tf_op jit(solution)/shard_map/ppermute | solution.py:24
  39.8 0.7 broadcast_in_dim.8
  40.5 9.2 %all-to-all-start.1 = ((f32[32,1,512]{2,1,0:T(1,128)}), f32[32,1,512]{2,1,0:T(1,128)S(1)}, u32[]{:S(2)}, u32[]{:S(2)}) async-start(f32[32,1,512]{2,1,0:T(1,128)} %broadcast_in_dim.8), calls=%async_computation.1 | async-start | bytes 131072 | tf_op jit(solution)/shard_map/all_to_all | solution.py:37
  49.7 6.6 %collective-permute-start.2 = (f32[64,64]{1,0:T(8,128)S(1)}, f32[64,64]{1,0:T(8,128)S(1)}, u32[]{:S(2)}, u32[]{:S(2)}) collective-permute-start(f32[64,64]{1,0:T(8,128)S(1)} %get-tuple-element.19), channel_id=1, source_target_pairs={{0,32},{32,64},{64,96},{96,128},{128,160},{160,192},{192,224},{224... | collective-permute-start | bytes 49160 | tf_op jit(solution)/shard_map/ppermute | solution.py:23
  56.4 2.1 %collective-permute-start.3 = (f32[64,64]{1,0:T(8,128)S(1)}, f32[64,64]{1,0:T(8,128)S(1)}, u32[]{:S(2)}, u32[]{:S(2)}) collective-permute-start(f32[64,64]{1,0:T(8,128)S(1)} %get-tuple-element.20), channel_id=1, source_target_pairs={{32,0},{64,32},{96,64},{128,96},{160,128},{192,160},{224,192},{256... | collective-permute-start | bytes 49160 | tf_op jit(solution)/shard_map/ppermute | solution.py:24
  59.0 5.6 %collective-permute-done.3 = f32[64,64]{1,0:T(8,128)S(1)} collective-permute-done((f32[64,64]{1,0:T(8,128)S(1)}, f32[64,64]{1,0:T(8,128)S(1)}, u32[]{:S(2)}, u32[]{:S(2)}) %collective-permute-start.3) | collective-permute-done | bytes 16416 | tf_op jit(solution)/shard_map/ppermute | solution.py:24
  69.6 18.2 %all_to_all.31 = f32[32,1,256]{2,1,0:T(1,128)S(1)} all-to-all(f32[32,1,256]{2,1,0:T(1,128)S(1)} %bitcast.50), channel_id=1, replica_groups=mesh['tile'=32,'kern'=32] {'kern'}, dimensions={0} | all-to-all | bytes 65536 | tf_op jit(solution)/shard_map/all_to_all | solution.py:35
  87.9 11.3 %all_to_all.32 = f32[32,1,256]{2,1,0:T(1,128)S(1)} all-to-all(f32[32,1,256]{2,1,0:T(1,128)S(1)} %broadcast_in_dim.21), channel_id=1, replica_groups=mesh['tile'=32,'kern'=32] {'kern'}, dimensions={0} | all-to-all | bytes 65536 | tf_op jit(solution)/shard_map/all_to_all | solution.py:37
  99.1 0.6 copy.50
  (67 shorter events, 11.4 us)
Async XLA Ops:
  0.0 8.5 %copy-start.2 = (f32[192,192]{1,0:T(8,128)S(1)}, f32[192,192]{1,0:T(8,128)}, u32[]{:S(2)}) copy-start(f32[192,192]{1,0:T(8,128)} %constant.34.clone) | copy-start | bytes 442372
  0.0 14.2 %collective-permute-start = (f32[64,128]{1,0:T(8,128)}, f32[64,128]{1,0:T(8,128)S(1)}, u32[]{:S(2)}, u32[]{:S(2)}) collective-permute-start(f32[64,128]{1,0:T(8,128)} %param.9), channel_id=1, source_target_pairs={{0,32},{32,64},{64,96},{96,128},{128,160},{160,192},{192,224},{224... | collective-permute-start | bytes 98312 | tf_op jit(solution)/shard_map/ppermute | solution.py:23
  5.3 9.7 %collective-permute-start.1 = (f32[64,128]{1,0:T(8,128)}, f32[64,128]{1,0:T(8,128)S(1)}, u32[]{:S(2)}, u32[]{:S(2)}) collective-permute-start(f32[64,128]{1,0:T(8,128)} %param.9), channel_id=1, source_target_pairs={{32,0},{64,32},{96,64},{128,96},{160,128},{192,160},{224,192},{256... | collective-permute-start | bytes 98312 | tf_op jit(solution)/shard_map/ppermute | solution.py:24
  9.0 0.9 copy-start.3
  9.9 1.1 %copy-start.1 = (f32[384,384]{1,0:T(8,128)S(1)}, f32[384,384]{1,0:T(8,128)}, u32[]{:S(2)}) copy-start(f32[384,384]{1,0:T(8,128)} %constant.36.clone) | copy-start | bytes 1769476
  11.0 1.3 %copy-start = (f32[384,384]{1,0:T(8,128)S(1)}, f32[384,384]{1,0:T(8,128)}, u32[]{:S(2)}) copy-start(f32[384,384]{1,0:T(8,128)} %constant.37.clone) | copy-start | bytes 1769476
  13.5 0.7 copy-start.6
  14.2 0.8 copy-start.4
  21.2 18.5 %copy-start.5 = (s32[64,128]{1,0:T(8,128)S(1)}, s32[64,128]{1,0:T(8,128)}, u32[]{:S(2)}) copy-start(s32[64,128]{1,0:T(8,128)} %param.12) | copy-start | bytes 98308
  21.2 18.6 %all-to-all-start = ((f32[32,1,512]{2,1,0:T(1,128)}), f32[32,1,512]{2,1,0:T(1,128)S(1)}, u32[]{:S(2)}, u32[]{:S(2)}) async-start(f32[32,1,512]{2,1,0:T(1,128)} %all_to_all.26), calls=%async_computation | async-start | bytes 131072 | tf_op jit(solution)/shard_map/all_to_all | solution.py:35
  31.1 27.4 %collective-permute-start.4 = (f32[2,2]{1,0:T(2,128)S(1)}, f32[2,2]{1,0:T(2,128)S(1)}, u32[]{:S(2)}, u32[]{:S(2)}) collective-permute-start(f32[2,2]{1,0:T(2,128)S(1)} %get-tuple-element.21), channel_id=1, source_target_pairs={{0,32},{32,64},{64,96},{96,128},{128,160},{160,192},{192,224},{224... | collective-permute-start | bytes 56 | tf_op jit(solution)/shard_map/ppermute | solution.py:23
  37.8 20.7 %collective-permute-start.5 = (f32[2,2]{1,0:T(2,128)S(1)}, f32[2,2]{1,0:T(2,128)S(1)}, u32[]{:S(2)}, u32[]{:S(2)}) collective-permute-start(f32[2,2]{1,0:T(2,128)S(1)} %get-tuple-element.22), channel_id=1, source_target_pairs={{32,0},{64,32},{96,64},{128,96},{160,128},{192,160},{224,192},{256... | collective-permute-start | bytes 56 | tf_op jit(solution)/shard_map/ppermute | solution.py:24
  40.5 18.4 %all-to-all-start.1 = ((f32[32,1,512]{2,1,0:T(1,128)}), f32[32,1,512]{2,1,0:T(1,128)S(1)}, u32[]{:S(2)}, u32[]{:S(2)}) async-start(f32[32,1,512]{2,1,0:T(1,128)} %broadcast_in_dim.8), calls=%async_computation.1 | async-start | bytes 131072 | tf_op jit(solution)/shard_map/all_to_all | solution.py:37
  49.7 9.3 %collective-permute-start.2 = (f32[64,64]{1,0:T(8,128)S(1)}, f32[64,64]{1,0:T(8,128)S(1)}, u32[]{:S(2)}, u32[]{:S(2)}) collective-permute-start(f32[64,64]{1,0:T(8,128)S(1)} %get-tuple-element.19), channel_id=1, source_target_pairs={{0,32},{32,64},{64,96},{96,128},{128,160},{160,192},{192,224},{224... | collective-permute-start | bytes 49160 | tf_op jit(solution)/shard_map/ppermute | solution.py:23
  56.4 8.3 %collective-permute-start.3 = (f32[64,64]{1,0:T(8,128)S(1)}, f32[64,64]{1,0:T(8,128)S(1)}, u32[]{:S(2)}, u32[]{:S(2)}) collective-permute-start(f32[64,64]{1,0:T(8,128)S(1)} %get-tuple-element.20), channel_id=1, source_target_pairs={{32,0},{64,32},{96,64},{128,96},{160,128},{192,160},{224,192},{256... | collective-permute-start | bytes 49160 | tf_op jit(solution)/shard_map/ppermute | solution.py:24

commit v6 on v5

--- a/solution.py
+++ b/solution.py
@@ -93,10 +93,16 @@
     row_cos, row_sin = twiddle(frame_rows)
     col_cos, col_sin = twiddle(frame_cols)
     row_cos, row_sin, col_cos, col_sin = lax.optimization_barrier((row_cos, row_sin, col_cos, col_sin))
-    extended = padded(mask, (("tile", 1),), reach)
+    block_rows = band // active.shape[0]
     block_cols = own_cols // active.shape[1]
-    target_ext = padded(target.astype(jnp.float32), (("tile", 1),), margin)
-    active_ext = padded(active.astype(jnp.float32), (("tile", 1),), margin // block_cols)
+    own_active = jnp.repeat(jnp.repeat(active, block_rows, axis=0), block_cols, axis=1)
+    stacked = jnp.concatenate(
+        [mask, target.astype(jnp.float32), own_active.astype(jnp.float32)], axis=0
+    )
+    stacked = padded(stacked, (("tile", 1),), reach)
+    extended = stacked[:band]
+    target_ext = stacked[band : 2 * band, margin : margin + field_cols]
+    pixel_active = stacked[2 * band :, margin : margin + field_cols]
     cols_real = product(extended, col_cos)
     cols_imag = -product(extended, col_sin)
     spec_real, spec_imag = apply_left(
@@ -129,7 +135,6 @@
     field_imag = field_imag * scale
     share_sum = weights[kernel_index] * (field_real * field_real + field_imag * field_imag)
     share_sum = share_sum / total_kernels
-    pixel_active = jnp.repeat(jnp.repeat(active_ext, BLK, axis=0), block_cols, axis=1)
     intensity = exchange_sum(share_sum, "kern")
     drive = resist_drive(intensity, target_ext, pixel_active)
     source_real, source_imag = apply_right(

time: 100 us -> 85.1 us (0.85)
  the two profiles are of different devices: /device:TPU:453 before, /device:TPU:1 now
where the time goes in v6:
time: 85.1 us; the launch traced here: 84.2 us
  blocking collectives  43.5 us (51%)
  matrix products  14.6 us (17%)
  starting transfers between devices  10.8 us (13%)
  waiting for transfers between devices  8.4 us (10%)
  local copies, waits for them, and re-layouts  4.86 us (6%)
  other arithmetic  1 us (1%)
  between operations  1 us (1%)
    all_to_all x2, blocking collectives, exchange_sum(): parts = lax.all_to_all(parts, axis, 0, 0, tiled=True)  32.2 us
    dot_general x36, matrix products, product(): jnp.dot(left_mat, right_mat, precision=lax.Precision.HIGHEST, preferred_e...  14.6 us
    all_to_all x1, blocking collectives, exchange_sum(): lax.all_to_all(jnp.broadcast_to(total, parts.shape), axis, 0, 0, tiled=True)  11.3 us
    all_to_all x1, waiting for transfers between devices, exchange_sum(): lax.all_to_all(jnp.broadcast_to(total, parts.shape), axis, 0, 0, tiled=True)  8.4 us
    ppermute x1, starting transfers between devices, padded(): before = lax.ppermute(last, axis, up)  5.6 us
    all_to_all x1, starting transfers between devices, exchange_sum(): lax.all_to_all(jnp.broadcast_to(total, parts.shape), axis, 0, 0, tiled=True)  3.91 us
    unnamed x13, local copies, waits for them, and re-layouts  2.51 us
  transfers between devices with their start and end apart: 3, of which 1 were waited for; matrix products, arithmetic and copies ran while one was open for 7% of the time, Pallas kernels for 0%

profile of v6, /device:TPU:1, one launch (start us, length us, event | category | flops | bytes accessed | tf_op | source)
XLA Modules:
  0.0 84.2 jit_solution(17391225396031723872)
XLA Ops:
  0.0 0.7 convert_element_type.15
  1.0 0.7 copy-done.5
  1.7 0.8 copy-done.4
  2.5 5.6 %collective-permute-start = (f32[192,128]{1,0:T(8,128)S(1)}, f32[192,128]{1,0:T(8,128)S(1)}, u32[]{:S(2)}, u32[]{:S(2)}) collective-permute-start(f32[192,128]{1,0:T(8,128)S(1)} %pad_maximum_fusion.1), channel_id=1, source_target_pairs={{0,32},{32,64},{64,96},{96,128},{128,160},{160,192},{192,224},{224... | collective-permute-start | bytes 294920 | tf_op jit(solution)/shard_map/ppermute | solution.py:23
  8.1 1.3 %collective-permute-start.1 = (f32[192,128]{1,0:T(8,128)S(1)}, f32[192,128]{1,0:T(8,128)S(1)}, u32[]{:S(2)}, u32[]{:S(2)}) collective-permute-start(f32[192,128]{1,0:T(8,128)S(1)} %pad_maximum_fusion.1), channel_id=1, source_target_pairs={{32,0},{64,32},{96,64},{128,96},{160,128},{192,160},{224,192},{256... | collective-permute-start | bytes 294920 | tf_op jit(solution)/shard_map/ppermute | solution.py:24
  9.4 1.3 %fusion.72 = (f32[1,1,129,129]{3,1,2,0:T(1,128)S(1)}, f32[1,1,129,129]{3,1,2,0:T(1,128)S(1)}) fusion(f32[1,2,129,129]{3,1,2,0:T(2,128)} %param.10), kind=kLoop, calls=%fused_computation.104 | loop fusion | bytes 266256 | tf_op jit(solution)/shard_map/slice | solution.py:121
  10.7 0.5 fusion.30
  11.2 0.5 fusion.28
  12.1 0.5 convolution_subtract_fusion.1
  12.6 0.5 convolution_add_fusion.1
  13.2 0.6 fusion.24
  13.8 0.6 fusion.22
  14.4 0.6 convolution_subtract_fusion
  15.1 0.6 convolution_add_fusion
  16.9 0.5 convolution_negate_fusion
  18.7 0.5 multiply_subtract_fusion.1
  21.9 21.0 %all_to_all.31 = f32[32,1,512]{2,1,0:T(1,128)S(1)} all-to-all(f32[32,1,512]{2,1,0:T(1,128)S(1)} %all_to_all.26), channel_id=1, replica_groups=mesh['tile'=32,'kern'=32] {'kern'}, dimensions={0} | all-to-all | bytes 131072 | tf_op jit(solution)/shard_map/all_to_all | solution.py:35
  43.0 0.7 broadcast_in_dim.20
  43.6 3.9 %all-to-all-start.1 = ((f32[32,1,512]{2,1,0:T(1,128)}), f32[32,1,512]{2,1,0:T(1,128)S(1)}, u32[]{:S(2)}, u32[]{:S(2)}) async-start(f32[32,1,512]{2,1,0:T(1,128)} %broadcast_in_dim.20), calls=%async_computation.1 | async-start | bytes 131072 | tf_op jit(solution)/shard_map/all_to_all | solution.py:37
  47.6 8.4 %all-to-all-done.1 = f32[32,1,512]{2,1,0:T(1,128)S(1)} async-done(((f32[32,1,512]{2,1,0:T(1,128)}), f32[32,1,512]{2,1,0:T(1,128)S(1)}, u32[]{:S(2)}, u32[]{:S(2)}) %all-to-all-start.1) | async-done | bytes 65568 | tf_op jit(solution)/shard_map/all_to_all | solution.py:37
  58.7 0.5 multiply_subtract_fusion
  61.0 11.3 %all_to_all.32 = f32[32,1,256]{2,1,0:T(1,128)S(1)} all-to-all(f32[32,1,256]{2,1,0:T(1,128)S(1)} %bitcast.48), channel_id=1, replica_groups=mesh['tile'=32,'kern'=32] {'kern'}, dimensions={0} | all-to-all | bytes 65536 | tf_op jit(solution)/shard_map/all_to_all | solution.py:35
  72.3 11.3 %all_to_all.33 = f32[32,1,256]{2,1,0:T(1,128)S(1)} all-to-all(f32[32,1,256]{2,1,0:T(1,128)S(1)} %broadcast_in_dim.21), channel_id=1, replica_groups=mesh['tile'=32,'kern'=32] {'kern'}, dimensions={0} | all-to-all | bytes 65536 | tf_op jit(solution)/shard_map/all_to_all | solution.py:37
  83.6 0.6 copy.48
  (52 shorter events, 9.9 us)
Async XLA Ops:
  0.9 0.8 copy-start.5
  1.7 0.8 copy-start.4
  2.5 8.2 %copy-start.2 = (f32[192,192]{1,0:T(8,128)S(1)}, f32[192,192]{1,0:T(8,128)}, u32[]{:S(2)}) copy-start(f32[192,192]{1,0:T(8,128)} %constant.34.clone) | copy-start | bytes 442372
  2.5 13.9 %collective-permute-start = (f32[192,128]{1,0:T(8,128)S(1)}, f32[192,128]{1,0:T(8,128)S(1)}, u32[]{:S(2)}, u32[]{:S(2)}) collective-permute-start(f32[192,128]{1,0:T(8,128)S(1)} %pad_maximum_fusion.1), channel_id=1, source_target_pairs={{0,32},{32,64},{64,96},{96,128},{128,160},{160,192},{192,224},{224... | collective-permute-start | bytes 294920 | tf_op jit(solution)/shard_map/ppermute | solution.py:23
  8.1 8.3 %collective-permute-start.1 = (f32[192,128]{1,0:T(8,128)S(1)}, f32[192,128]{1,0:T(8,128)S(1)}, u32[]{:S(2)}, u32[]{:S(2)}) collective-permute-start(f32[192,128]{1,0:T(8,128)S(1)} %pad_maximum_fusion.1), channel_id=1, source_target_pairs={{32,0},{64,32},{96,64},{128,96},{160,128},{192,160},{224,192},{256... | collective-permute-start | bytes 294920 | tf_op jit(solution)/shard_map/ppermute | solution.py:24
  11.2 0.9 %copy-start.3 = (f32[192,192]{1,0:T(8,128)S(1)}, f32[192,192]{1,0:T(8,128)}, u32[]{:S(2)}) copy-start(f32[192,192]{1,0:T(8,128)} %constant.35.clone) | copy-start | bytes 442372
  12.1 1.1 %copy-start.1 = (f32[384,384]{1,0:T(8,128)S(1)}, f32[384,384]{1,0:T(8,128)}, u32[]{:S(2)}) copy-start(f32[384,384]{1,0:T(8,128)} %constant.36.clone) | copy-start | bytes 1769476
  13.2 1.3 %copy-start = (f32[384,384]{1,0:T(8,128)S(1)}, f32[384,384]{1,0:T(8,128)}, u32[]{:S(2)}) copy-start(f32[384,384]{1,0:T(8,128)} %constant.37.clone) | copy-start | bytes 1769476
  43.6 12.3 %all-to-all-start.1 = ((f32[32,1,512]{2,1,0:T(1,128)}), f32[32,1,512]{2,1,0:T(1,128)S(1)}, u32[]{:S(2)}, u32[]{:S(2)}) async-start(f32[32,1,512]{2,1,0:T(1,128)} %broadcast_in_dim.20), calls=%async_computation.1 | async-start | bytes 131072 | tf_op jit(solution)/shard_map/all_to_all | solution.py:37

commit v7 on v6

--- a/solution.py
+++ b/solution.py
@@ -51,16 +51,24 @@
 
 
 def apply_left(cosine, sine, sign, real_part, imag_part):
+    width = real_part.shape[1]
+    both = jnp.concatenate([real_part, imag_part], axis=1)
+    by_cos = product(cosine, both)
+    by_sin = product(sine, both)
     return (
-        product(cosine, real_part) - sign * product(sine, imag_part),
-        product(cosine, imag_part) + sign * product(sine, real_part),
+        by_cos[:, :width] - sign * by_sin[:, width:],
+        by_cos[:, width:] + sign * by_sin[:, :width],
     )
 
 
 def apply_right(real_part, imag_part, cosine, sine, sign):
+    height = real_part.shape[0]
+    both = jnp.concatenate([real_part, imag_part], axis=0)
+    by_cos = product(both, cosine)
+    by_sin = product(both, sine)
     return (
-        product(real_part, cosine) - sign * product(imag_part, sine),
-        product(imag_part, cosine) + sign * product(real_part, sine),
+        by_cos[:height] - sign * by_sin[height:],
+        by_cos[height:] + sign * by_sin[:height],
     )
 
 

time: 85.1 us -> 83.2 us (0.978)
  matrix products: 14.6 us -> 10.9 us
  local copies, waits for them, and re-layouts: 4.86 us -> 6.49 us
    dot_general x36 -> x20, matrix products: 14.6 us -> 10.9 us  [product(): jnp.dot(left_mat, right_mat, precision=lax.Precision.HIGHEST, preferred_e...]
    unnamed x13, local copies, waits for them, and re-layouts: 2.51 us -> 4.1 us
  transfers between devices with their start and end apart: 3 -> 3, of which waited for: 1 -> 1; matrix products, arithmetic and copies ran while one was open for 7% -> 6% of each run, Pallas kernels for 0% -> 0%
where the time goes in v7:
time: 83.2 us; the launch traced here: 82.3 us
  blocking collectives  43.5 us (52%)
  matrix products  10.9 us (13%)
  starting transfers between devices  10.6 us (13%)
  waiting for transfers between devices  8.41 us (10%)
  local copies, waits for them, and re-layouts  6.49 us (8%)
  other arithmetic  1.48 us (2%)
  between operations  0.97 us (1%)
    all_to_all x2, blocking collectives, exchange_sum(): parts = lax.all_to_all(parts, axis, 0, 0, tiled=True)  32.2 us
    all_to_all x1, blocking collectives, exchange_sum(): lax.all_to_all(jnp.broadcast_to(total, parts.shape), axis, 0, 0, tiled=True)  11.3 us
    dot_general x20, matrix products, product(): jnp.dot(left_mat, right_mat, precision=lax.Precision.HIGHEST, preferred_e...  10.9 us
    all_to_all x1, waiting for transfers between devices, exchange_sum(): lax.all_to_all(jnp.broadcast_to(total, parts.shape), axis, 0, 0, tiled=True)  8.4 us
    ppermute x1, starting transfers between devices, padded(): before = lax.ppermute(last, axis, up)  5.47 us
    unnamed x13, local copies, waits for them, and re-layouts  4.1 us
    all_to_all x1, starting transfers between devices, exchange_sum(): lax.all_to_all(jnp.broadcast_to(total, parts.shape), axis, 0, 0, tiled=True)  3.87 us
  transfers between devices with their start and end apart: 3, of which 1 were waited for; matrix products, arithmetic and copies ran while one was open for 6% of the time, Pallas kernels for 0%

profile of v7, /device:TPU:1, one launch (start us, length us, event | category | flops | bytes accessed | tf_op | source)
XLA Modules:
  0.0 82.3 jit_solution(9617856195615263671)
XLA Ops:
  0.0 0.7 convert_element_type.15
  1.0 0.7 copy-done.5
  1.7 0.8 copy-done.4
  2.5 5.5 %collective-permute-start = (f32[192,128]{1,0:T(8,128)S(1)}, f32[192,128]{1,0:T(8,128)S(1)}, u32[]{:S(2)}, u32[]{:S(2)}) collective-permute-start(f32[192,128]{1,0:T(8,128)S(1)} %pad_maximum_fusion.25), channel_id=1, source_target_pairs={{0,32},{32,64},{64,96},{96,128},{128,160},{160,192},{192,224},{224... | collective-permute-start | bytes 294920 | tf_op jit(solution)/shard_map/ppermute | solution.py:23
  7.9 1.3 %collective-permute-start.1 = (f32[192,128]{1,0:T(8,128)S(1)}, f32[192,128]{1,0:T(8,128)S(1)}, u32[]{:S(2)}, u32[]{:S(2)}) collective-permute-start(f32[192,128]{1,0:T(8,128)S(1)} %pad_maximum_fusion.25), channel_id=1, source_target_pairs={{32,0},{64,32},{96,64},{128,96},{160,128},{192,160},{224,192},{256... | collective-permute-start | bytes 294920 | tf_op jit(solution)/shard_map/ppermute | solution.py:24
  9.2 1.3 %fusion.77 = (f32[1,1,129,129]{3,1,2,0:T(1,128)S(1)}, f32[1,1,129,129]{3,1,2,0:T(1,128)S(1)}) fusion(f32[1,2,129,129]{3,1,2,0:T(2,128)} %param.10), kind=kLoop, calls=%fused_computation.114 | loop fusion | bytes 266256 | tf_op jit(solution)/shard_map/slice | solution.py:128
  10.6 0.9 %copy-done.2 = f32[192,192]{1,0:T(8,128)S(1)} copy-done((f32[192,192]{1,0:T(8,128)S(1)}, f32[192,192]{1,0:T(8,128)}, u32[]{:S(2)}) %copy-start.2) | copy-done | bytes 147480
  11.4 0.8 fusion.24
  12.4 0.8 fusion.26
  13.2 1.0 %copy-done.1 = f32[384,384]{1,0:T(8,128)S(1)} copy-done((f32[384,384]{1,0:T(8,128)S(1)}, f32[384,384]{1,0:T(8,128)}, u32[]{:S(2)}) %copy-start.1) | copy-done | bytes 589848
  14.2 0.9 %fusion.19 = f32[384,384]{1,0:T(8,128)S(1)} fusion(f32[384,384]{1,0:T(8,128)S(1)} %copy-done.1, f32[192,129]{0,1:T(8,128)S(1)} %get-tuple-element.21, f32[192,129]{0,1:T(8,128)S(1)} %get-tuple-element.20), kind=kOutput, calls=%fused_computation.36 | convolution fusion | flops 228311424 | bytes 1077248 | tf_op jit(solution)/shard_map/dot_general | solution.py:42
  15.2 0.9 %fusion.17 = f32[384,384]{1,0:T(8,128)S(1)} fusion(f32[384,384]{1,0:T(8,128)S(1)} %copy-done, f32[192,129]{0,1:T(8,128)S(1)} %get-tuple-element.21, f32[192,129]{0,1:T(8,128)S(1)} %get-tuple-element.20), kind=kOutput, calls=%fused_computation.34 | convolution fusion | flops 228311424 | bytes 1077248 | tf_op jit(solution)/shard_map/dot_general | solution.py:42
  17.7 0.7 fusion.31
  18.4 0.7 fusion.30
  19.8 0.5 fusion.3
  21.2 21.0 %all_to_all.31 = f32[32,1,512]{2,1,0:T(1,128)S(1)} all-to-all(f32[32,1,512]{2,1,0:T(1,128)S(1)} %all_to_all.26), channel_id=1, replica_groups=mesh['tile'=32,'kern'=32] {'kern'}, dimensions={0} | all-to-all | bytes 131072 | tf_op jit(solution)/shard_map/all_to_all | solution.py:35
  42.2 0.7 broadcast_in_dim.20
  42.9 3.9 %all-to-all-start.1 = ((f32[32,1,512]{2,1,0:T(1,128)}), f32[32,1,512]{2,1,0:T(1,128)S(1)}, u32[]{:S(2)}, u32[]{:S(2)}) async-start(f32[32,1,512]{2,1,0:T(1,128)} %broadcast_in_dim.20), calls=%async_computation.1 | async-start | bytes 131072 | tf_op jit(solution)/shard_map/all_to_all | solution.py:37
  46.8 8.4 %all-to-all-done.1 = f32[32,1,512]{2,1,0:T(1,128)S(1)} async-done(((f32[32,1,512]{2,1,0:T(1,128)}), f32[32,1,512]{2,1,0:T(1,128)S(1)}, u32[]{:S(2)}, u32[]{:S(2)}) %all-to-all-start.1) | async-done | bytes 65568 | tf_op jit(solution)/shard_map/all_to_all | solution.py:37
  56.2 0.6 fusion.29
  56.9 0.6 fusion.28
  59.1 11.3 %all_to_all.32 = f32[32,1,256]{2,1,0:T(1,128)S(1)} all-to-all(f32[32,1,256]{2,1,0:T(1,128)S(1)} %bitcast.17), channel_id=1, replica_groups=mesh['tile'=32,'kern'=32] {'kern'}, dimensions={0} | all-to-all | bytes 65536 | tf_op jit(solution)/shard_map/all_to_all | solution.py:35
  70.5 11.3 %all_to_all.33 = f32[32,1,256]{2,1,0:T(1,128)S(1)} all-to-all(f32[32,1,256]{2,1,0:T(1,128)S(1)} %broadcast_in_dim.21), channel_id=1, replica_groups=mesh['tile'=32,'kern'=32] {'kern'}, dimensions={0} | all-to-all | bytes 65536 | tf_op jit(solution)/shard_map/all_to_all | solution.py:37
  81.7 0.6 copy.45
  (45 shorter events, 5.9 us)
Async XLA Ops:
  0.9 0.8 copy-start.5
  1.7 0.8 copy-start.4
  2.5 14.3 %collective-permute-start = (f32[192,128]{1,0:T(8,128)S(1)}, f32[192,128]{1,0:T(8,128)S(1)}, u32[]{:S(2)}, u32[]{:S(2)}) collective-permute-start(f32[192,128]{1,0:T(8,128)S(1)} %pad_maximum_fusion.25), channel_id=1, source_target_pairs={{0,32},{32,64},{64,96},{96,128},{128,160},{160,192},{192,224},{224... | collective-permute-start | bytes 294920 | tf_op jit(solution)/shard_map/ppermute | solution.py:23
  7.9 8.8 %collective-permute-start.1 = (f32[192,128]{1,0:T(8,128)S(1)}, f32[192,128]{1,0:T(8,128)S(1)}, u32[]{:S(2)}, u32[]{:S(2)}) collective-permute-start(f32[192,128]{1,0:T(8,128)S(1)} %pad_maximum_fusion.25), channel_id=1, source_target_pairs={{32,0},{64,32},{96,64},{128,96},{160,128},{192,160},{224,192},{256... | collective-permute-start | bytes 294920 | tf_op jit(solution)/shard_map/ppermute | solution.py:24
  10.5 0.9 %copy-start.2 = (f32[192,192]{1,0:T(8,128)S(1)}, f32[192,192]{1,0:T(8,128)}, u32[]{:S(2)}) copy-start(f32[192,192]{1,0:T(8,128)} %constant.35.clone) | copy-start | bytes 442372
  11.4 0.9 %copy-start.3 = (f32[192,192]{1,0:T(8,128)S(1)}, f32[192,192]{1,0:T(8,128)}, u32[]{:S(2)}) copy-start(f32[192,192]{1,0:T(8,128)} %constant.34.clone) | copy-start | bytes 442372
  13.2 1.1 %copy-start.1 = (f32[384,384]{1,0:T(8,128)S(1)}, f32[384,384]{1,0:T(8,128)}, u32[]{:S(2)}) copy-start(f32[384,384]{1,0:T(8,128)} %constant.36.clone) | copy-start | bytes 1769476
  13.2 1.9 %copy-start = (f32[384,384]{1,0:T(8,128)S(1)}, f32[384,384]{1,0:T(8,128)}, u32[]{:S(2)}) copy-start(f32[384,384]{1,0:T(8,128)} %constant.37.clone) | copy-start | bytes 1769476
  42.9 12.3 %all-to-all-start.1 = ((f32[32,1,512]{2,1,0:T(1,128)}), f32[32,1,512]{2,1,0:T(1,128)S(1)}, u32[]{:S(2)}, u32[]{:S(2)}) async-start(f32[32,1,512]{2,1,0:T(1,128)} %broadcast_in_dim.20), calls=%async_computation.1 | async-start | bytes 131072 | tf_op jit(solution)/shard_map/all_to_all | solution.py:37

commit v8 on v7

--- a/solution.py
+++ b/solution.py
@@ -72,6 +72,26 @@
     )
 
 
+def left_stacked(stack, sign, real_part, imag_part):
+    height = stack.shape[0] // 2
+    width = real_part.shape[1]
+    full = product(stack, jnp.concatenate([real_part, imag_part], axis=1))
+    return (
+        full[:height, :width] - sign * full[height:, width:],
+        full[:height, width:] + sign * full[height:, :width],
+    )
+
+
+def right_stacked(real_part, imag_part, stack, sign):
+    height = real_part.shape[0]
+    width = stack.shape[1] // 2
+    full = product(jnp.concatenate([real_part, imag_part], axis=0), stack)
+    return (
+        full[:height, :width] - sign * full[height:, width:],
+        full[height:, :width] + sign * full[:height, width:],
+    )
+
+
 def edge_pixels(frame, margin):
     return jnp.concatenate([frame[:, :margin], frame[:, frame.shape[1] - margin :]], axis=1)
 
@@ -100,7 +120,11 @@
     scale = 1.0 / (frame_rows * frame_cols)
     row_cos, row_sin = twiddle(frame_rows)
     col_cos, col_sin = twiddle(frame_cols)
-    row_cos, row_sin, col_cos, col_sin = lax.optimization_barrier((row_cos, row_sin, col_cos, col_sin))
+    row_stack = jnp.concatenate([row_cos, row_sin], axis=0)
+    col_stack = jnp.concatenate([col_cos, col_sin], axis=1)
+    row_stack, col_stack = lax.optimization_barrier((row_stack, col_stack))
+    row_cos, row_sin = row_stack[:frame_rows], row_stack[frame_rows:]
+    col_cos, col_sin = col_stack[:, :frame_cols], col_stack[:, frame_cols:]
     block_rows = band // active.shape[0]
     block_cols = own_cols // active.shape[1]
     own_active = jnp.repeat(jnp.repeat(active, block_rows, axis=0), block_cols, axis=1)
@@ -111,26 +135,17 @@
     extended = stacked[:band]
     target_ext = stacked[band : 2 * band, margin : margin + field_cols]
     pixel_active = stacked[2 * band :, margin : margin + field_cols]
-    cols_real = product(extended, col_cos)
-    cols_imag = -product(extended, col_sin)
-    spec_real, spec_imag = apply_left(
-        row_cos[:, margin : margin + band],
-        row_sin[:, margin : margin + band],
-        -1.0,
-        cols_real,
-        cols_imag,
+    by_cols = product(extended, col_stack)
+    cols_real = by_cols[:, :frame_cols]
+    cols_imag = -by_cols[:, frame_cols:]
+    spec_real, spec_imag = left_stacked(
+        row_stack[:, margin : margin + band], -1.0, cols_real, cols_imag
     )
     kernel_index = 0
-    kern_real, kern_imag = apply_left(
-        row_cos[:, :width],
-        row_sin[:, :width],
-        1.0,
-        kernels[kernel_index, 0],
-        kernels[kernel_index, 1],
+    kern_real, kern_imag = left_stacked(
+        row_stack[:, :width], 1.0, kernels[kernel_index, 0], kernels[kernel_index, 1]
     )
-    kern_real, kern_imag = apply_right(
-        kern_real, kern_imag, col_cos[:width, :], col_sin[:width, :], 1.0
-    )
+    kern_real, kern_imag = right_stacked(kern_real, kern_imag, col_stack[:width, :], 1.0)
     prod_real = spec_real * kern_real - spec_imag * kern_imag
     prod_imag = spec_real * kern_imag + spec_imag * kern_real
     field_real, field_imag = apply_left(
@@ -145,15 +160,11 @@
     share_sum = share_sum / total_kernels
     intensity = exchange_sum(share_sum, "kern")
     drive = resist_drive(intensity, target_ext, pixel_active)
-    source_real, source_imag = apply_right(
-        drive * field_real,
-        drive * field_imag,
-        col_cos[:field_cols, :],
-        col_sin[:field_cols, :],
-        -1.0,
+    source_real, source_imag = right_stacked(
+        drive * field_real, drive * field_imag, col_stack[:field_cols, :], -1.0
     )
-    source_real, source_imag = apply_left(
-        row_cos[:, :band], row_sin[:, :band], -1.0, source_real, source_imag
+    source_real, source_imag = left_stacked(
+        row_stack[:, :band], -1.0, source_real, source_imag
     )
     quot_real = source_real * kern_real + source_imag * kern_imag
     quot_imag = source_imag * kern_real - source_real * kern_imag

time: 83.2 us -> 81.6 us (0.981)
  local copies, waits for them, and re-layouts: 6.49 us -> 3.16 us
  matrix products: 10.9 us -> 9.01 us
  other arithmetic: 1.48 us -> 3.17 us
  waiting for transfers between devices: 8.41 us -> 9.52 us
  blocking collectives: 43.5 us -> 44.6 us
    unnamed x13 -> x7, local copies, waits for them, and re-layouts: 4.1 us -> 0.78 us
    dot_general x20 -> x14, matrix products: 10.9 us -> 9.01 us  [product(): jnp.dot(left_mat, right_mat, precision=lax.Precision.HIGHEST, preferred_e...]
    all_to_all x2, blocking collectives: 32.2 us -> 33.4 us  [exchange_sum(): parts = lax.all_to_all(parts, axis, 0, 0, tiled=True)]
    ppermute x1, waiting for transfers between devices: 0.01 us -> 1.11 us  [padded(): after = lax.ppermute(initial, axis, down)]
  transfers between devices with their start and end apart: 3 -> 3, of which waited for: 1 -> 2; matrix products, arithmetic and copies ran while one was open for 6% -> 4% of each run, Pallas kernels for 0% -> 0%
where the time goes in v8:
time: 81.6 us; the launch traced here: 81 us
  blocking collectives  44.6 us (55%)
  starting transfers between devices  10.6 us (13%)
  waiting for transfers between devices  9.52 us (12%)
  matrix products  9.01 us (11%)
  other arithmetic  3.17 us (4%)
  local copies, waits for them, and re-layouts  3.16 us (4%)
  between operations  0.91 us (1%)
    all_to_all x2, blocking collectives, exchange_sum(): parts = lax.all_to_all(parts, axis, 0, 0, tiled=True)  33.4 us
    all_to_all x1, blocking collectives, exchange_sum(): lax.all_to_all(jnp.broadcast_to(total, parts.shape), axis, 0, 0, tiled=True)  11.3 us
    dot_general x14, matrix products, product(): jnp.dot(left_mat, right_mat, precision=lax.Precision.HIGHEST, preferred_e...  9.01 us
    all_to_all x1, waiting for transfers between devices, exchange_sum(): lax.all_to_all(jnp.broadcast_to(total, parts.shape), axis, 0, 0, tiled=True)  8.4 us
    ppermute x1, starting transfers between devices, padded(): before = lax.ppermute(last, axis, up)  5.46 us
    all_to_all x1, starting transfers between devices, exchange_sum(): lax.all_to_all(jnp.broadcast_to(total, parts.shape), axis, 0, 0, tiled=True)  3.89 us
  transfers between devices with their start and end apart: 3, of which 2 were waited for; matrix products, arithmetic and copies ran while one was open for 4% of the time, Pallas kernels for 0%

profile of v8, /device:TPU:1, one launch (start us, length us, event | category | flops | bytes accessed | tf_op | source)
XLA Modules:
  0.0 81.0 jit_solution(16546654948835866888)
XLA Ops:
  0.0 0.7 convert_element_type.15
  1.1 0.8 convert_element_type.14
  1.8 0.8 pad_maximum_fusion.10
  2.6 5.5 %collective-permute-start = (f32[192,128]{1,0:T(8,128)S(1)}, f32[192,128]{1,0:T(8,128)S(1)}, u32[]{:S(2)}, u32[]{:S(2)}) collective-permute-start(f32[192,128]{1,0:T(8,128)S(1)} %pad_maximum_fusion.10), channel_id=1, source_target_pairs={{0,32},{32,64},{64,96},{96,128},{128,160},{160,192},{192,224},{224... | collective-permute-start | bytes 294920 | tf_op jit(solution)/shard_map/ppermute | solution.py:23
  8.1 1.3 %collective-permute-start.1 = (f32[192,128]{1,0:T(8,128)S(1)}, f32[192,128]{1,0:T(8,128)S(1)}, u32[]{:S(2)}, u32[]{:S(2)}) collective-permute-start(f32[192,128]{1,0:T(8,128)S(1)} %pad_maximum_fusion.10), channel_id=1, source_target_pairs={{32,0},{64,32},{96,64},{128,96},{160,128},{192,160},{224,192},{256... | collective-permute-start | bytes 294920 | tf_op jit(solution)/shard_map/ppermute | solution.py:24
  9.4 1.3 %fusion.76 = (f32[1,1,129,129]{3,1,2,0:T(1,128)S(1)}, f32[1,1,129,129]{3,1,2,0:T(1,128)S(1)}) fusion(f32[1,2,129,129]{3,1,2,0:T(2,128)} %param.10), kind=kLoop, calls=%fused_computation.108 | loop fusion | bytes 266256 | tf_op jit(solution)/shard_map/slice | solution.py:146
  10.7 0.9 %fusion.13 = f32[384,258]{0,1:T(8,128)S(1)} fusion(f32[384,192]{1,0:T(8,128)S(1)} %copy-done.1, f32[129,129]{1,0:T(8,128)S(1)} %get-tuple-element.26, f32[129,129]{1,0:T(8,128)S(1)} %get-tuple-element.27), kind=kOutput, calls=%fused_computation.16 | convolution fusion | flops 153396736 | bytes 824328 | tf_op jit(solution)/shard_map/dot_general | solution.py:42
  11.9 1.2 %fusion.7 = f32[384,768]{1,0:T(8,128)S(1)} fusion(f32[384,768]{1,0:T(8,128)S(1)} %copy-done, f32[192,129]{0,1:T(8,128)S(1)} %get-tuple-element.17, f32[192,129]{0,1:T(8,128)S(1)} %get-tuple-element.16), kind=kOutput, calls=%fused_computation.10 | convolution fusion | flops 456573312 | bytes 1875968 | tf_op jit(solution)/shard_map/dot_general | solution.py:42
  13.8 1.1 %collective-permute-done.1 = f32[192,128]{1,0:T(8,128)S(1)} collective-permute-done((f32[192,128]{1,0:T(8,128)S(1)}, f32[192,128]{1,0:T(8,128)S(1)}, u32[]{:S(2)}, u32[]{:S(2)}) %collective-permute-start.1) | collective-permute-done | bytes 98336 | tf_op jit(solution)/shard_map/ppermute | solution.py:24
  15.0 0.8 %fusion.45 = f32[64,768]{1,0:T(8,128)S(1)} fusion(f32[384,768]{1,0:T(8,128)S(1)} %copy-done, f32[192,384]{1,0:T(8,128)S(1)} %pad_maximum_fusion.6), kind=kOutput, calls=%fused_computation.71 | convolution fusion | flops 226492416 | bytes 1474560 | tf_op jit(solution)/shard_map/dot_general | solution.py:42
  15.8 1.1 %fusion.25 = f32[384,768]{1,0:T(8,128)S(1)} fusion(f32[64,384]{1,0:T(8,128)S(1)} %get-tuple-element.25, f32[64,384]{1,0:T(8,128)S(1)} %get-tuple-element.24, f32[384,192]{1,0:T(8,128)S(1)} %copy-done.1), kind=kOutput, calls=%fused_computation.39 | convolution fusion | flops 226541568 | bytes 1572864 | tf_op jit(solution)/shard_map/dot_general | solution.py:42
  17.2 0.5 fusion.6
  17.7 0.5 fusion.5
  19.1 22.1 %all_to_all.31 = f32[32,1,512]{2,1,0:T(1,128)S(1)} all-to-all(f32[32,1,512]{2,1,0:T(1,128)S(1)} %all_to_all.26), channel_id=1, replica_groups=mesh['tile'=32,'kern'=32] {'kern'}, dimensions={0} | all-to-all | bytes 131072 | tf_op jit(solution)/shard_map/all_to_all | solution.py:35
  41.3 0.7 broadcast_in_dim.20
  42.0 3.9 %all-to-all-start.1 = ((f32[32,1,512]{2,1,0:T(1,128)}), f32[32,1,512]{2,1,0:T(1,128)S(1)}, u32[]{:S(2)}, u32[]{:S(2)}) async-start(f32[32,1,512]{2,1,0:T(1,128)} %broadcast_in_dim.20), calls=%async_computation.1 | async-start | bytes 131072 | tf_op jit(solution)/shard_map/all_to_all | solution.py:37
  45.9 8.4 %all-to-all-done.1 = f32[32,1,512]{2,1,0:T(1,128)S(1)} async-done(((f32[32,1,512]{2,1,0:T(1,128)}), f32[32,1,512]{2,1,0:T(1,128)S(1)}, u32[]{:S(2)}, u32[]{:S(2)}) %all-to-all-start.1) | async-done | bytes 65568 | tf_op jit(solution)/shard_map/all_to_all | solution.py:37
  54.5 0.6 fusion.1
  55.1 1.1 %fusion.29 = f32[384,768]{1,0:T(8,128)S(1)} fusion(f32[64,384]{1,0:T(8,128)S(1)} %get-tuple-element.19, f32[64,384]{1,0:T(8,128)S(1)} %get-tuple-element.18, f32[384,192]{1,0:T(8,128)S(1)} %copy-done.1), kind=kOutput, calls=%fused_computation.44 | convolution fusion | flops 226541568 | bytes 1572864 | tf_op jit(solution)/shard_map/dot_general | solution.py:42
  56.3 0.5 fusion.4
  56.8 0.5 fusion.3
  57.8 11.3 %all_to_all.32 = f32[32,1,256]{2,1,0:T(1,128)S(1)} all-to-all(f32[32,1,256]{2,1,0:T(1,128)S(1)} %bitcast.16), channel_id=1, replica_groups=mesh['tile'=32,'kern'=32] {'kern'}, dimensions={0} | all-to-all | bytes 65536 | tf_op jit(solution)/shard_map/all_to_all | solution.py:35
  69.2 11.3 %all_to_all.33 = f32[32,1,256]{2,1,0:T(1,128)S(1)} all-to-all(f32[32,1,256]{2,1,0:T(1,128)S(1)} %broadcast_in_dim.21), channel_id=1, replica_groups=mesh['tile'=32,'kern'=32] {'kern'}, dimensions={0} | all-to-all | bytes 65536 | tf_op jit(solution)/shard_map/all_to_all | solution.py:37
  80.4 0.6 copy.45
  (34 shorter events, 2.8 us)
Async XLA Ops:
  0.0 10.7 %copy-start.1 = (f32[384,192]{1,0:T(8,128)S(1)}, f32[384,192]{1,0:T(8,128)}, u32[]{:S(2)}) copy-start(f32[384,192]{1,0:T(8,128)} %constant.41) | copy-start | bytes 884740
  2.6 11.2 %collective-permute-start = (f32[192,128]{1,0:T(8,128)S(1)}, f32[192,128]{1,0:T(8,128)S(1)}, u32[]{:S(2)}, u32[]{:S(2)}) collective-permute-start(f32[192,128]{1,0:T(8,128)S(1)} %pad_maximum_fusion.10), channel_id=1, source_target_pairs={{0,32},{32,64},{64,96},{96,128},{128,160},{160,192},{192,224},{224... | collective-permute-start | bytes 294920 | tf_op jit(solution)/shard_map/ppermute | solution.py:23
  8.1 6.9 %collective-permute-start.1 = (f32[192,128]{1,0:T(8,128)S(1)}, f32[192,128]{1,0:T(8,128)S(1)}, u32[]{:S(2)}, u32[]{:S(2)}) collective-permute-start(f32[192,128]{1,0:T(8,128)S(1)} %pad_maximum_fusion.10), channel_id=1, source_target_pairs={{32,0},{64,32},{96,64},{128,96},{160,128},{192,160},{224,192},{256... | collective-permute-start | bytes 294920 | tf_op jit(solution)/shard_map/ppermute | solution.py:24
  10.6 1.3 %copy-start = (f32[384,768]{1,0:T(8,128)S(1)}, f32[384,768]{1,0:T(8,128)}, u32[]{:S(2)}) copy-start(f32[384,768]{1,0:T(8,128)} %constant.42) | copy-start | bytes 3538948
  11.6 3.3 %copy-start.2 = (f32[64,128]{1,0:T(8,128)S(1)}, f32[64,128]{1,0:T(8,128)}, u32[]{:S(2)}) copy-start(f32[64,128]{1,0:T(8,128)} %param.9) | copy-start | bytes 98308
  42.0 12.3 %all-to-all-start.1 = ((f32[32,1,512]{2,1,0:T(1,128)}), f32[32,1,512]{2,1,0:T(1,128)S(1)}, u32[]{:S(2)}, u32[]{:S(2)}) async-start(f32[32,1,512]{2,1,0:T(1,128)} %broadcast_in_dim.20), calls=%async_computation.1 | async-start | bytes 131072 | tf_op jit(solution)/shard_map/all_to_all | solution.py:37

commit v9 on v8

--- a/solution.py
+++ b/solution.py
@@ -125,16 +125,25 @@
     row_stack, col_stack = lax.optimization_barrier((row_stack, col_stack))
     row_cos, row_sin = row_stack[:frame_rows], row_stack[frame_rows:]
     col_cos, col_sin = col_stack[:, :frame_cols], col_stack[:, frame_cols:]
-    block_rows = band // active.shape[0]
-    block_cols = own_cols // active.shape[1]
-    own_active = jnp.repeat(jnp.repeat(active, block_rows, axis=0), block_cols, axis=1)
-    stacked = jnp.concatenate(
-        [mask, target.astype(jnp.float32), own_active.astype(jnp.float32)], axis=0
-    )
+    block_grid, blocks = active.shape
+    block_rows = band // block_grid
+    block_cols = own_cols // blocks
+    reach_blocks = margin // block_cols
+    active_rows = jnp.pad(active.astype(jnp.float32), ((0, 0), (0, own_cols - blocks)))
+    stacked = jnp.concatenate([mask, target.astype(jnp.float32), active_rows], axis=0)
     stacked = padded(stacked, (("tile", 1),), reach)
     extended = stacked[:band]
     target_ext = stacked[band : 2 * band, margin : margin + field_cols]
-    pixel_active = stacked[2 * band :, margin : margin + field_cols]
+    active_row = stacked[2 * band :]
+    active_ext = jnp.concatenate(
+        [
+            active_row[:, blocks - reach_blocks : blocks],
+            active_row[:, own_cols : own_cols + blocks],
+            active_row[:, 2 * own_cols : 2 * own_cols + reach_blocks],
+        ],
+        axis=1,
+    )
+    pixel_active = jnp.repeat(jnp.repeat(active_ext, block_rows, axis=0), block_cols, axis=1)
     by_cols = product(extended, col_stack)
     cols_real = by_cols[:, :frame_cols]
     cols_imag = -by_cols[:, frame_cols:]

time: 81.6 us -> 80.8 us (level)
  transfers between devices with their start and end apart: 3 -> 3, of which waited for: 2 -> 2; matrix products, arithmetic and copies ran while one was open for 4% -> 5% of each run, Pallas kernels for 0% -> 0%
where the time goes in v9:
time: 80.8 us; the launch traced here: 80.3 us
  blocking collectives  44.6 us (55%)
  starting transfers between devices  10.6 us (13%)
  matrix products  9.02 us (11%)
  waiting for transfers between devices  8.71 us (11%)
  local copies, waits for them, and re-layouts  3.25 us (4%)
  other arithmetic  3.18 us (4%)
  between operations  0.92 us (1%)
    all_to_all x2, blocking collectives, exchange_sum(): parts = lax.all_to_all(parts, axis, 0, 0, tiled=True)  33.4 us
    all_to_all x1, blocking collectives, exchange_sum(): lax.all_to_all(jnp.broadcast_to(total, parts.shape), axis, 0, 0, tiled=True)  11.3 us
    dot_general x14, matrix products, product(): jnp.dot(left_mat, right_mat, precision=lax.Precision.HIGHEST, preferred_e...  9.02 us
    all_to_all x1, waiting for transfers between devices, exchange_sum(): lax.all_to_all(jnp.broadcast_to(total, parts.shape), axis, 0, 0, tiled=True)  7.9 us
    ppermute x1, starting transfers between devices, padded(): before = lax.ppermute(last, axis, up)  5.46 us
    all_to_all x1, starting transfers between devices, exchange_sum(): lax.all_to_all(jnp.broadcast_to(total, parts.shape), axis, 0, 0, tiled=True)  3.89 us
  transfers between devices with their start and end apart: 3, of which 2 were waited for; matrix products, arithmetic and copies ran while one was open for 5% of the time, Pallas kernels for 0%

profile of v9, /device:TPU:1, one launch (start us, length us, event | category | flops | bytes accessed | tf_op | source)
XLA Modules:
  0.0 80.3 jit_solution(3515561291221757526)
XLA Ops:
  0.0 0.7 convert_element_type.9
  0.7 0.8 convert_element_type.8
  1.5 0.8 pad_maximum_fusion.9
  2.3 5.5 %collective-permute-start = (f32[130,128]{1,0:T(8,128)S(1)}, f32[130,128]{1,0:T(8,128)S(1)}, u32[]{:S(2)}, u32[]{:S(2)}) collective-permute-start(f32[130,128]{1,0:T(8,128)S(1)} %pad_maximum_fusion.9), channel_id=1, source_target_pairs={{0,32},{32,64},{64,96},{96,128},{128,160},{160,192},{192,224},{224... | collective-permute-start | bytes 199688 | tf_op jit(solution)/shard_map/ppermute | solution.py:23
  7.7 1.3 %collective-permute-start.1 = (f32[130,128]{1,0:T(8,128)S(1)}, f32[130,128]{1,0:T(8,128)S(1)}, u32[]{:S(2)}, u32[]{:S(2)}) collective-permute-start(f32[130,128]{1,0:T(8,128)S(1)} %pad_maximum_fusion.9), channel_id=1, source_target_pairs={{32,0},{64,32},{96,64},{128,96},{160,128},{192,160},{224,192},{256... | collective-permute-start | bytes 199688 | tf_op jit(solution)/shard_map/ppermute | solution.py:24
  9.0 1.3 %fusion.87 = (f32[1,1,129,129]{3,1,2,0:T(1,128)S(1)}, f32[1,1,129,129]{3,1,2,0:T(1,128)S(1)}) fusion(f32[1,2,129,129]{3,1,2,0:T(2,128)} %param.10), kind=kLoop, calls=%fused_computation.121 | loop fusion | bytes 266256 | tf_op jit(solution)/shard_map/slice | solution.py:155
  10.3 0.9 %fusion.13 = f32[384,258]{0,1:T(8,128)S(1)} fusion(f32[384,192]{1,0:T(8,128)S(1)} %copy-done.1, f32[129,129]{1,0:T(8,128)S(1)} %get-tuple-element.26, f32[129,129]{1,0:T(8,128)S(1)} %get-tuple-element.27), kind=kOutput, calls=%fused_computation.16 | convolution fusion | flops 153396736 | bytes 824328 | tf_op jit(solution)/shard_map/dot_general | solution.py:42
  11.6 1.3 %fusion.7 = f32[384,768]{1,0:T(8,128)S(1)} fusion(f32[384,768]{1,0:T(8,128)S(1)} %copy-done, f32[192,129]{0,1:T(8,128)S(1)} %get-tuple-element.17, f32[192,129]{0,1:T(8,128)S(1)} %get-tuple-element.16), kind=kOutput, calls=%fused_computation.10 | convolution fusion | flops 456573312 | bytes 1875968 | tf_op jit(solution)/shard_map/dot_general | solution.py:42
  13.5 0.8 collective-permute-done.1
  14.3 0.8 %fusion.45 = f32[64,768]{1,0:T(8,128)S(1)} fusion(f32[384,768]{1,0:T(8,128)S(1)} %copy-done, f32[130,128]{1,0:T(8,128)S(1)} %collective-permute-done.1, f32[130,128]{1,0:T(8,128)S(1)} %collective-permute-done, f32[2,128]{1,0:T(2,128)S(1)} %pad.4, f32[64,128]{1,0:T(8,128)S(1)} %convert_element_type.8, f32[64,128]{1,0:T(8,128)S(1)} %copy-done.2), kind=kOutput, calls=%fused_computation.70 | convolution fusion | flops 226590720 | bytes 1575936 | tf_op jit(solution)/shard_map/dot_general | solution.py:42
  15.2 1.1 %fusion.25 = f32[384,768]{1,0:T(8,128)S(1)} fusion(f32[64,384]{1,0:T(8,128)S(1)} %get-tuple-element.25, f32[64,384]{1,0:T(8,128)S(1)} %get-tuple-element.24, f32[384,192]{1,0:T(8,128)S(1)} %copy-done.1), kind=kOutput, calls=%fused_computation.38 | convolution fusion | flops 226541568 | bytes 1572864 | tf_op jit(solution)/shard_map/dot_general | solution.py:42
  16.6 0.5 fusion.6
  17.0 0.5 fusion.5
  18.5 22.1 %all_to_all.31 = f32[32,1,512]{2,1,0:T(1,128)S(1)} all-to-all(f32[32,1,512]{2,1,0:T(1,128)S(1)} %all_to_all.26), channel_id=1, replica_groups=mesh['tile'=32,'kern'=32] {'kern'}, dimensions={0} | all-to-all | bytes 131072 | tf_op jit(solution)/shard_map/all_to_all | solution.py:35
  40.6 0.7 broadcast_in_dim.8
  41.3 3.9 %all-to-all-start.1 = ((f32[32,1,512]{2,1,0:T(1,128)}), f32[32,1,512]{2,1,0:T(1,128)S(1)}, u32[]{:S(2)}, u32[]{:S(2)}) async-start(f32[32,1,512]{2,1,0:T(1,128)} %broadcast_in_dim.8), calls=%async_computation.1 | async-start | bytes 131072 | tf_op jit(solution)/shard_map/all_to_all | solution.py:37
  45.7 7.9 %all-to-all-done.1 = f32[32,1,512]{2,1,0:T(1,128)S(1)} async-done(((f32[32,1,512]{2,1,0:T(1,128)}), f32[32,1,512]{2,1,0:T(1,128)S(1)}, u32[]{:S(2)}, u32[]{:S(2)}) %all-to-all-start.1) | async-done | bytes 65568 | tf_op jit(solution)/shard_map/all_to_all | solution.py:37
  53.8 0.6 fusion.1
  54.4 1.1 %fusion.29 = f32[384,768]{1,0:T(8,128)S(1)} fusion(f32[64,384]{1,0:T(8,128)S(1)} %get-tuple-element.19, f32[64,384]{1,0:T(8,128)S(1)} %get-tuple-element.18, f32[384,192]{1,0:T(8,128)S(1)} %copy-done.1), kind=kOutput, calls=%fused_computation.43 | convolution fusion | flops 226541568 | bytes 1572864 | tf_op jit(solution)/shard_map/dot_general | solution.py:42
  55.6 0.5 fusion.4
  56.1 0.5 fusion.3
  57.1 11.3 %all_to_all.32 = f32[32,1,256]{2,1,0:T(1,128)S(1)} all-to-all(f32[32,1,256]{2,1,0:T(1,128)S(1)} %bitcast.16), channel_id=1, replica_groups=mesh['tile'=32,'kern'=32] {'kern'}, dimensions={0} | all-to-all | bytes 65536 | tf_op jit(solution)/shard_map/all_to_all | solution.py:35
  68.5 11.3 %all_to_all.33 = f32[32,1,256]{2,1,0:T(1,128)S(1)} all-to-all(f32[32,1,256]{2,1,0:T(1,128)S(1)} %broadcast_in_dim.21), channel_id=1, replica_groups=mesh['tile'=32,'kern'=32] {'kern'}, dimensions={0} | all-to-all | bytes 65536 | tf_op jit(solution)/shard_map/all_to_all | solution.py:37
  79.7 0.6 copy.45
  (37 shorter events, 2.9 us)
Async XLA Ops:
  0.0 10.3 %copy-start.1 = (f32[384,192]{1,0:T(8,128)S(1)}, f32[384,192]{1,0:T(8,128)}, u32[]{:S(2)}) copy-start(f32[384,192]{1,0:T(8,128)} %constant.45) | copy-start | bytes 884740
  2.3 11.2 %collective-permute-start = (f32[130,128]{1,0:T(8,128)S(1)}, f32[130,128]{1,0:T(8,128)S(1)}, u32[]{:S(2)}, u32[]{:S(2)}) collective-permute-start(f32[130,128]{1,0:T(8,128)S(1)} %pad_maximum_fusion.9), channel_id=1, source_target_pairs={{0,32},{32,64},{64,96},{96,128},{128,160},{160,192},{192,224},{224... | collective-permute-start | bytes 199688 | tf_op jit(solution)/shard_map/ppermute | solution.py:23
  7.7 6.6 %collective-permute-start.1 = (f32[130,128]{1,0:T(8,128)S(1)}, f32[130,128]{1,0:T(8,128)S(1)}, u32[]{:S(2)}, u32[]{:S(2)}) collective-permute-start(f32[130,128]{1,0:T(8,128)S(1)} %pad_maximum_fusion.9), channel_id=1, source_target_pairs={{32,0},{64,32},{96,64},{128,96},{160,128},{192,160},{224,192},{256... | collective-permute-start | bytes 199688 | tf_op jit(solution)/shard_map/ppermute | solution.py:24
  10.3 1.3 %copy-start = (f32[384,768]{1,0:T(8,128)S(1)}, f32[384,768]{1,0:T(8,128)}, u32[]{:S(2)}) copy-start(f32[384,768]{1,0:T(8,128)} %constant.46) | copy-start | bytes 3538948
  11.3 3.0 %copy-start.2 = (f32[64,128]{1,0:T(8,128)S(1)}, f32[64,128]{1,0:T(8,128)}, u32[]{:S(2)}) copy-start(f32[64,128]{1,0:T(8,128)} %param.9) | copy-start | bytes 98308
  41.3 12.3 %all-to-all-start.1 = ((f32[32,1,512]{2,1,0:T(1,128)}), f32[32,1,512]{2,1,0:T(1,128)S(1)}, u32[]{:S(2)}, u32[]{:S(2)}) async-start(f32[32,1,512]{2,1,0:T(1,128)} %broadcast_in_dim.8), calls=%async_computation.1 | async-start | bytes 131072 | tf_op jit(solution)/shard_map/all_to_all | solution.py:37

commit v10 on v9

--- a/solution.py
+++ b/solution.py
@@ -130,11 +130,11 @@
     block_cols = own_cols // blocks
     reach_blocks = margin // block_cols
     active_rows = jnp.pad(active.astype(jnp.float32), ((0, 0), (0, own_cols - blocks)))
-    stacked = jnp.concatenate([mask, target.astype(jnp.float32), active_rows], axis=0)
-    stacked = padded(stacked, (("tile", 1),), reach)
-    extended = stacked[:band]
-    target_ext = stacked[band : 2 * band, margin : margin + field_cols]
-    active_row = stacked[2 * band :]
+    extended = padded(mask, (("tile", 1),), reach)
+    sides = jnp.concatenate([target.astype(jnp.float32), active_rows], axis=0)
+    sides = padded(sides, (("tile", 1),), reach)
+    target_ext = sides[:band, margin : margin + field_cols]
+    active_row = sides[band:]
     active_ext = jnp.concatenate(
         [
             active_row[:, blocks - reach_blocks : blocks],
@@ -166,7 +166,7 @@
     field_real = field_real * scale
     field_imag = field_imag * scale
     share_sum = weights[kernel_index] * (field_real * field_real + field_imag * field_imag)
-    share_sum = share_sum / total_kernels
+    share_sum = share_sum / total_kernels + 0.0 * target_ext
     intensity = exchange_sum(share_sum, "kern")
     drive = resist_drive(intensity, target_ext, pixel_active)
     source_real, source_imag = right_stacked(

time: 80.8 us -> 86.5 us (1.071)
  starting transfers between devices: 10.6 us -> 17.5 us
    ppermute x1 -> x2, starting transfers between devices: 5.46 us -> 11.1 us  [padded(): before = lax.ppermute(last, axis, up)]
    ppermute x1 -> x2, starting transfers between devices: 1.29 us -> 2.58 us  [padded(): after = lax.ppermute(initial, axis, down)]
  transfers between devices with their start and end apart: 3 -> 5, of which waited for: 2 -> 1; matrix products, arithmetic and copies ran while one was open for 5% -> 11% of each run, Pallas kernels for 0% -> 0%
where the time goes in v10:
time: 86.5 us; the launch traced here: 85.2 us
  blocking collectives  44 us (51%)
  starting transfers between devices  17.5 us (20%)
  matrix products  9.01 us (10%)
  waiting for transfers between devices  7.92 us (9%)
  local copies, waits for them, and re-layouts  3.26 us (4%)
  other arithmetic  2.45 us (3%)
  between operations  0.97 us (1%)
    all_to_all x2, blocking collectives, exchange_sum(): parts = lax.all_to_all(parts, axis, 0, 0, tiled=True)  32.8 us
    all_to_all x1, blocking collectives, exchange_sum(): lax.all_to_all(jnp.broadcast_to(total, parts.shape), axis, 0, 0, tiled=True)  11.3 us
    ppermute x2, starting transfers between devices, padded(): before = lax.ppermute(last, axis, up)  11.1 us
    dot_general x14, matrix products, product(): jnp.dot(left_mat, right_mat, precision=lax.Precision.HIGHEST, preferred_e...  9.01 us
    all_to_all x1, waiting for transfers between devices, exchange_sum(): lax.all_to_all(jnp.broadcast_to(total, parts.shape), axis, 0, 0, tiled=True)  7.9 us
    all_to_all x1, starting transfers between devices, exchange_sum(): lax.all_to_all(jnp.broadcast_to(total, parts.shape), axis, 0, 0, tiled=True)  3.87 us
    ppermute x2, starting transfers between devices, padded(): after = lax.ppermute(initial, axis, down)  2.58 us
  transfers between devices with their start and end apart: 5, of which 1 were waited for; matrix products, arithmetic and copies ran while one was open for 11% of the time, Pallas kernels for 0%

profile of v10, /device:TPU:1, one launch (start us, length us, event | category | flops | bytes accessed | tf_op | source)
XLA Modules:
  0.0 85.2 jit_solution(10002895297678522889)
XLA Ops:
  0.0 5.6 %collective-permute-start = (f32[64,128]{1,0:T(8,128)}, f32[64,128]{1,0:T(8,128)S(1)}, u32[]{:S(2)}, u32[]{:S(2)}) collective-permute-start(f32[64,128]{1,0:T(8,128)} %param.9), channel_id=1, source_target_pairs={{0,32},{32,64},{64,96},{96,128},{128,160},{160,192},{192,224},{224... | collective-permute-start | bytes 98312 | tf_op jit(solution)/shard_map/ppermute | solution.py:23
  5.6 1.3 %collective-permute-start.1 = (f32[64,128]{1,0:T(8,128)}, f32[64,128]{1,0:T(8,128)S(1)}, u32[]{:S(2)}, u32[]{:S(2)}) collective-permute-start(f32[64,128]{1,0:T(8,128)} %param.9), channel_id=1, source_target_pairs={{32,0},{64,32},{96,64},{128,96},{160,128},{192,160},{224,192},{256... | collective-permute-start | bytes 98312 | tf_op jit(solution)/shard_map/ppermute | solution.py:24
  6.9 0.7 convert_element_type.9
  7.6 0.8 convert_element_type.8
  8.4 5.5 %collective-permute-start.2 = (f32[66,128]{1,0:T(8,128)S(1)}, f32[66,128]{1,0:T(8,128)S(1)}, u32[]{:S(2)}, u32[]{:S(2)}) collective-permute-start(f32[66,128]{1,0:T(8,128)S(1)} %pad_maximum_fusion.12), channel_id=1, source_target_pairs={{0,32},{32,64},{64,96},{96,128},{128,160},{160,192},{192,224},{224... | collective-permute-start | bytes 101384 | tf_op jit(solution)/shard_map/ppermute | solution.py:23
  13.9 1.3 %collective-permute-start.3 = (f32[66,128]{1,0:T(8,128)S(1)}, f32[66,128]{1,0:T(8,128)S(1)}, u32[]{:S(2)}, u32[]{:S(2)}) collective-permute-start(f32[66,128]{1,0:T(8,128)S(1)} %pad_maximum_fusion.12), channel_id=1, source_target_pairs={{32,0},{64,32},{96,64},{128,96},{160,128},{192,160},{224,192},{256... | collective-permute-start | bytes 101384 | tf_op jit(solution)/shard_map/ppermute | solution.py:24
  15.2 1.3 %fusion.76 = (f32[1,1,129,129]{3,1,2,0:T(1,128)S(1)}, f32[1,1,129,129]{3,1,2,0:T(1,128)S(1)}) fusion(f32[1,2,129,129]{3,1,2,0:T(2,128)} %param.10), kind=kLoop, calls=%fused_computation.111 | loop fusion | bytes 266256 | tf_op jit(solution)/shard_map/slice | solution.py:155
  16.5 0.9 %fusion.13 = f32[384,258]{0,1:T(8,128)S(1)} fusion(f32[384,192]{1,0:T(8,128)S(1)} %copy-done.1, f32[129,129]{1,0:T(8,128)S(1)} %get-tuple-element.26, f32[129,129]{1,0:T(8,128)S(1)} %get-tuple-element.27), kind=kOutput, calls=%fused_computation.16 | convolution fusion | flops 153396736 | bytes 824328 | tf_op jit(solution)/shard_map/dot_general | solution.py:42
  17.7 1.3 %fusion.7 = f32[384,768]{1,0:T(8,128)S(1)} fusion(f32[384,768]{1,0:T(8,128)S(1)} %copy-done, f32[192,129]{0,1:T(8,128)S(1)} %get-tuple-element.17, f32[192,129]{0,1:T(8,128)S(1)} %get-tuple-element.16), kind=kOutput, calls=%fused_computation.10 | convolution fusion | flops 456573312 | bytes 1875968 | tf_op jit(solution)/shard_map/dot_general | solution.py:42
  19.6 0.8 fusion.45
  20.5 1.1 %fusion.25 = f32[384,768]{1,0:T(8,128)S(1)} fusion(f32[64,384]{1,0:T(8,128)S(1)} %get-tuple-element.25, f32[64,384]{1,0:T(8,128)S(1)} %get-tuple-element.24, f32[384,192]{1,0:T(8,128)S(1)} %copy-done.1), kind=kOutput, calls=%fused_computation.38 | convolution fusion | flops 226541568 | bytes 1572864 | tf_op jit(solution)/shard_map/dot_general | solution.py:42
  21.9 0.5 fusion.6
  22.4 0.5 fusion.5
  23.9 21.5 %all_to_all.31 = f32[32,1,512]{2,1,0:T(1,128)S(1)} all-to-all(f32[32,1,512]{2,1,0:T(1,128)S(1)} %all_to_all.26), channel_id=1, replica_groups=mesh['tile'=32,'kern'=32] {'kern'}, dimensions={0} | all-to-all | bytes 131072 | tf_op jit(solution)/shard_map/all_to_all | solution.py:35
  45.5 0.7 broadcast_in_dim.8
  46.2 3.9 %all-to-all-start.1 = ((f32[32,1,512]{2,1,0:T(1,128)}), f32[32,1,512]{2,1,0:T(1,128)S(1)}, u32[]{:S(2)}, u32[]{:S(2)}) async-start(f32[32,1,512]{2,1,0:T(1,128)} %broadcast_in_dim.8), calls=%async_computation.1 | async-start | bytes 131072 | tf_op jit(solution)/shard_map/all_to_all | solution.py:37
  50.5 7.9 %all-to-all-done.1 = f32[32,1,512]{2,1,0:T(1,128)S(1)} async-done(((f32[32,1,512]{2,1,0:T(1,128)}), f32[32,1,512]{2,1,0:T(1,128)S(1)}, u32[]{:S(2)}, u32[]{:S(2)}) %all-to-all-start.1) | async-done | bytes 65568 | tf_op jit(solution)/shard_map/all_to_all | solution.py:37
  58.6 0.6 fusion.1
  59.2 1.1 %fusion.29 = f32[384,768]{1,0:T(8,128)S(1)} fusion(f32[64,384]{1,0:T(8,128)S(1)} %get-tuple-element.19, f32[64,384]{1,0:T(8,128)S(1)} %get-tuple-element.18, f32[384,192]{1,0:T(8,128)S(1)} %copy-done.1), kind=kOutput, calls=%fused_computation.43 | convolution fusion | flops 226541568 | bytes 1572864 | tf_op jit(solution)/shard_map/dot_general | solution.py:42
  60.4 0.5 fusion.4
  60.9 0.5 fusion.3
  62.0 11.3 %all_to_all.32 = f32[32,1,256]{2,1,0:T(1,128)S(1)} all-to-all(f32[32,1,256]{2,1,0:T(1,128)S(1)} %bitcast.16), channel_id=1, replica_groups=mesh['tile'=32,'kern'=32] {'kern'}, dimensions={0} | all-to-all | bytes 65536 | tf_op jit(solution)/shard_map/all_to_all | solution.py:35
  73.3 11.3 %all_to_all.33 = f32[32,1,256]{2,1,0:T(1,128)S(1)} all-to-all(f32[32,1,256]{2,1,0:T(1,128)S(1)} %broadcast_in_dim.21), channel_id=1, replica_groups=mesh['tile'=32,'kern'=32] {'kern'}, dimensions={0} | all-to-all | bytes 65536 | tf_op jit(solution)/shard_map/all_to_all | solution.py:37
  84.6 0.6 copy.45
  (41 shorter events, 3.0 us)
Async XLA Ops:
  0.0 16.5 %copy-start.1 = (f32[384,192]{1,0:T(8,128)S(1)}, f32[384,192]{1,0:T(8,128)}, u32[]{:S(2)}) copy-start(f32[384,192]{1,0:T(8,128)} %constant.46) | copy-start | bytes 884740
  0.0 19.6 %collective-permute-start = (f32[64,128]{1,0:T(8,128)}, f32[64,128]{1,0:T(8,128)S(1)}, u32[]{:S(2)}, u32[]{:S(2)}) collective-permute-start(f32[64,128]{1,0:T(8,128)} %param.9), channel_id=1, source_target_pairs={{0,32},{32,64},{64,96},{96,128},{128,160},{160,192},{192,224},{224... | collective-permute-start | bytes 98312 | tf_op jit(solution)/shard_map/ppermute | solution.py:23
  5.6 14.0 %collective-permute-start.1 = (f32[64,128]{1,0:T(8,128)}, f32[64,128]{1,0:T(8,128)S(1)}, u32[]{:S(2)}, u32[]{:S(2)}) collective-permute-start(f32[64,128]{1,0:T(8,128)} %param.9), channel_id=1, source_target_pairs={{32,0},{64,32},{96,64},{128,96},{160,128},{192,160},{224,192},{256... | collective-permute-start | bytes 98312 | tf_op jit(solution)/shard_map/ppermute | solution.py:24
  8.4 15.3 %collective-permute-start.2 = (f32[66,128]{1,0:T(8,128)S(1)}, f32[66,128]{1,0:T(8,128)S(1)}, u32[]{:S(2)}, u32[]{:S(2)}) collective-permute-start(f32[66,128]{1,0:T(8,128)S(1)} %pad_maximum_fusion.12), channel_id=1, source_target_pairs={{0,32},{32,64},{64,96},{96,128},{128,160},{160,192},{192,224},{224... | collective-permute-start | bytes 101384 | tf_op jit(solution)/shard_map/ppermute | solution.py:23
  13.9 9.9 %collective-permute-start.3 = (f32[66,128]{1,0:T(8,128)S(1)}, f32[66,128]{1,0:T(8,128)S(1)}, u32[]{:S(2)}, u32[]{:S(2)}) collective-permute-start(f32[66,128]{1,0:T(8,128)S(1)} %pad_maximum_fusion.12), channel_id=1, source_target_pairs={{32,0},{64,32},{96,64},{128,96},{160,128},{192,160},{224,192},{256... | collective-permute-start | bytes 101384 | tf_op jit(solution)/shard_map/ppermute | solution.py:24
  16.4 1.3 %copy-start = (f32[384,768]{1,0:T(8,128)S(1)}, f32[384,768]{1,0:T(8,128)}, u32[]{:S(2)}) copy-start(f32[384,768]{1,0:T(8,128)} %constant.47) | copy-start | bytes 3538948
  17.4 2.2 %copy-start.2 = (f32[64,128]{1,0:T(8,128)S(1)}, f32[64,128]{1,0:T(8,128)}, u32[]{:S(2)}) copy-start(f32[64,128]{1,0:T(8,128)} %param.9) | copy-start | bytes 98308
  46.2 12.3 %all-to-all-start.1 = ((f32[32,1,512]{2,1,0:T(1,128)}), f32[32,1,512]{2,1,0:T(1,128)S(1)}, u32[]{:S(2)}, u32[]{:S(2)}) async-start(f32[32,1,512]{2,1,0:T(1,128)} %broadcast_in_dim.8), calls=%async_computation.1 | async-start | bytes 131072 | tf_op jit(solution)/shard_map/all_to_all | solution.py:37

commit v11 on v9

--- a/solution.py
+++ b/solution.py
@@ -129,8 +129,9 @@
     block_rows = band // block_grid
     block_cols = own_cols // blocks
     reach_blocks = margin // block_cols
-    active_rows = jnp.pad(active.astype(jnp.float32), ((0, 0), (0, own_cols - blocks)))
-    stacked = jnp.concatenate([mask, target.astype(jnp.float32), active_rows], axis=0)
+    active_rows = jnp.pad(active, ((0, 0), (0, own_cols - blocks)))
+    whole = jnp.concatenate([target, active_rows], axis=0).astype(jnp.float32)
+    stacked = jnp.concatenate([mask, whole], axis=0)
     stacked = padded(stacked, (("tile", 1),), reach)
     extended = stacked[:band]
     target_ext = stacked[band : 2 * band, margin : margin + field_cols]

time: 80.8 us -> 80.1 us (level)
  no operation moved by 1% of the time
where the time goes in v11:
time: 80.1 us; the launch traced here: 79.7 us
  blocking collectives  44.6 us (56%)
  starting transfers between devices  10.6 us (13%)
  matrix products  9.01 us (11%)
  waiting for transfers between devices  8.7 us (11%)
  local copies, waits for them, and re-layouts  3.25 us (4%)
  other arithmetic  2.52 us (3%)
  between operations  0.93 us (1%)
    all_to_all x2, blocking collectives, exchange_sum(): parts = lax.all_to_all(parts, axis, 0, 0, tiled=True)  33.4 us
    all_to_all x1, blocking collectives, exchange_sum(): lax.all_to_all(jnp.broadcast_to(total, parts.shape), axis, 0, 0, tiled=True)  11.3 us
    dot_general x14, matrix products, product(): jnp.dot(left_mat, right_mat, precision=lax.Precision.HIGHEST, preferred_e...  9.01 us
    all_to_all x1, waiting for transfers between devices, exchange_sum(): lax.all_to_all(jnp.broadcast_to(total, parts.shape), axis, 0, 0, tiled=True)  7.89 us
    ppermute x1, starting transfers between devices, padded(): before = lax.ppermute(last, axis, up)  5.46 us
    all_to_all x1, starting transfers between devices, exchange_sum(): lax.all_to_all(jnp.broadcast_to(total, parts.shape), axis, 0, 0, tiled=True)  3.88 us
  transfers between devices with their start and end apart: 3, of which 2 were waited for; matrix products, arithmetic and copies ran while one was open for 5% of the time, Pallas kernels for 0%

profile of v11, /device:TPU:1, one launch (start us, length us, event | category | flops | bytes accessed | tf_op | source)
XLA Modules:
  0.0 79.7 jit_solution(24591886120014061)
XLA Ops:
  0.0 0.8 %fusion.70 = f32[66,128]{1,0:T(8,128)S(1)} fusion(s32[2,4]{1,0:T(2,128)} %param.13, s32[64,128]{1,0:T(8,128)} %param.12), kind=kLoop, calls=%fused_computation.104 | loop fusion | flops 16896 | bytes 66592 | tf_op jit(solution)/shard_map/convert_element_type | solution.py:133
  0.8 0.8 pad_maximum_fusion.9
  1.6 5.5 %collective-permute-start = (f32[130,128]{1,0:T(8,128)S(1)}, f32[130,128]{1,0:T(8,128)S(1)}, u32[]{:S(2)}, u32[]{:S(2)}) collective-permute-start(f32[130,128]{1,0:T(8,128)S(1)} %pad_maximum_fusion.9), channel_id=1, source_target_pairs={{0,32},{32,64},{64,96},{96,128},{128,160},{160,192},{192,224},{224... | collective-permute-start | bytes 199688 | tf_op jit(solution)/shard_map/ppermute | solution.py:23
  7.1 1.3 %collective-permute-start.1 = (f32[130,128]{1,0:T(8,128)S(1)}, f32[130,128]{1,0:T(8,128)S(1)}, u32[]{:S(2)}, u32[]{:S(2)}) collective-permute-start(f32[130,128]{1,0:T(8,128)S(1)} %pad_maximum_fusion.9), channel_id=1, source_target_pairs={{32,0},{64,32},{96,64},{128,96},{160,128},{192,160},{224,192},{256... | collective-permute-start | bytes 199688 | tf_op jit(solution)/shard_map/ppermute | solution.py:24
  8.4 1.3 %fusion.86 = (f32[1,1,129,129]{3,1,2,0:T(1,128)S(1)}, f32[1,1,129,129]{3,1,2,0:T(1,128)S(1)}) fusion(f32[1,2,129,129]{3,1,2,0:T(2,128)} %param.10), kind=kLoop, calls=%fused_computation.120 | loop fusion | bytes 266256 | tf_op jit(solution)/shard_map/slice | solution.py:156
  9.7 0.9 %fusion.13 = f32[384,258]{0,1:T(8,128)S(1)} fusion(f32[384,192]{1,0:T(8,128)S(1)} %copy-done.1, f32[129,129]{1,0:T(8,128)S(1)} %get-tuple-element.26, f32[129,129]{1,0:T(8,128)S(1)} %get-tuple-element.27), kind=kOutput, calls=%fused_computation.16 | convolution fusion | flops 153396736 | bytes 824328 | tf_op jit(solution)/shard_map/dot_general | solution.py:42
  10.9 1.2 %fusion.7 = f32[384,768]{1,0:T(8,128)S(1)} fusion(f32[384,768]{1,0:T(8,128)S(1)} %copy-done, f32[192,129]{0,1:T(8,128)S(1)} %get-tuple-element.17, f32[192,129]{0,1:T(8,128)S(1)} %get-tuple-element.16), kind=kOutput, calls=%fused_computation.10 | convolution fusion | flops 456573312 | bytes 1875968 | tf_op jit(solution)/shard_map/dot_general | solution.py:42
  12.8 0.8 %collective-permute-done.1 = f32[130,128]{1,0:T(8,128)S(1)} collective-permute-done((f32[130,128]{1,0:T(8,128)S(1)}, f32[130,128]{1,0:T(8,128)S(1)}, u32[]{:S(2)}, u32[]{:S(2)}) %collective-permute-start.1) | collective-permute-done | bytes 66592 | tf_op jit(solution)/shard_map/ppermute | solution.py:24
  13.6 0.8 %fusion.45 = f32[64,768]{1,0:T(8,128)S(1)} fusion(f32[384,768]{1,0:T(8,128)S(1)} %copy-done, f32[130,128]{1,0:T(8,128)S(1)} %collective-permute-done.1, f32[130,128]{1,0:T(8,128)S(1)} %collective-permute-done, f32[66,128]{1,0:T(8,128)S(1)} %fusion.70, f32[64,128]{1,0:T(8,128)S(1)} %copy-done.2), kind=kOutput, calls=%fused_computation.70 | convolution fusion | flops 226566144 | bytes 1575936 | tf_op jit(solution)/shard_map/dot_general | solution.py:42
  14.5 1.1 %fusion.25 = f32[384,768]{1,0:T(8,128)S(1)} fusion(f32[64,384]{1,0:T(8,128)S(1)} %get-tuple-element.25, f32[64,384]{1,0:T(8,128)S(1)} %get-tuple-element.24, f32[384,192]{1,0:T(8,128)S(1)} %copy-done.1), kind=kOutput, calls=%fused_computation.38 | convolution fusion | flops 226541568 | bytes 1572864 | tf_op jit(solution)/shard_map/dot_general | solution.py:42
  15.9 0.5 fusion.6
  16.4 0.5 fusion.5
  16.9 0.4 fusion.11
  17.8 22.1 %all_to_all.31 = f32[32,1,512]{2,1,0:T(1,128)S(1)} all-to-all(f32[32,1,512]{2,1,0:T(1,128)S(1)} %all_to_all.26), channel_id=1, replica_groups=mesh['tile'=32,'kern'=32] {'kern'}, dimensions={0} | all-to-all | bytes 131072 | tf_op jit(solution)/shard_map/all_to_all | solution.py:35
  40.0 0.7 broadcast_in_dim.8
  40.6 3.9 %all-to-all-start.1 = ((f32[32,1,512]{2,1,0:T(1,128)}), f32[32,1,512]{2,1,0:T(1,128)S(1)}, u32[]{:S(2)}, u32[]{:S(2)}) async-start(f32[32,1,512]{2,1,0:T(1,128)} %broadcast_in_dim.8), calls=%async_computation.1 | async-start | bytes 131072 | tf_op jit(solution)/shard_map/all_to_all | solution.py:37
  45.0 7.9 %all-to-all-done.1 = f32[32,1,512]{2,1,0:T(1,128)S(1)} async-done(((f32[32,1,512]{2,1,0:T(1,128)}), f32[32,1,512]{2,1,0:T(1,128)S(1)}, u32[]{:S(2)}, u32[]{:S(2)}) %all-to-all-start.1) | async-done | bytes 65568 | tf_op jit(solution)/shard_map/all_to_all | solution.py:37
  53.1 0.6 fusion.1
  53.7 1.1 %fusion.29 = f32[384,768]{1,0:T(8,128)S(1)} fusion(f32[64,384]{1,0:T(8,128)S(1)} %get-tuple-element.19, f32[64,384]{1,0:T(8,128)S(1)} %get-tuple-element.18, f32[384,192]{1,0:T(8,128)S(1)} %copy-done.1), kind=kOutput, calls=%fused_computation.43 | convolution fusion | flops 226541568 | bytes 1572864 | tf_op jit(solution)/shard_map/dot_general | solution.py:42
  54.9 0.5 fusion.4
  55.4 0.5 fusion.3
  56.4 11.3 %all_to_all.32 = f32[32,1,256]{2,1,0:T(1,128)S(1)} all-to-all(f32[32,1,256]{2,1,0:T(1,128)S(1)} %bitcast.16), channel_id=1, replica_groups=mesh['tile'=32,'kern'=32] {'kern'}, dimensions={0} | all-to-all | bytes 65536 | tf_op jit(solution)/shard_map/all_to_all | solution.py:35
  67.8 11.3 %all_to_all.33 = f32[32,1,256]{2,1,0:T(1,128)S(1)} all-to-all(f32[32,1,256]{2,1,0:T(1,128)S(1)} %broadcast_in_dim.21), channel_id=1, replica_groups=mesh['tile'=32,'kern'=32] {'kern'}, dimensions={0} | all-to-all | bytes 65536 | tf_op jit(solution)/shard_map/all_to_all | solution.py:37
  79.0 0.6 copy.45
  (36 shorter events, 2.6 us)
Async XLA Ops:
  0.0 9.7 %copy-start.1 = (f32[384,192]{1,0:T(8,128)S(1)}, f32[384,192]{1,0:T(8,128)}, u32[]{:S(2)}) copy-start(f32[384,192]{1,0:T(8,128)} %constant.45) | copy-start | bytes 884740
  1.6 11.2 %collective-permute-start = (f32[130,128]{1,0:T(8,128)S(1)}, f32[130,128]{1,0:T(8,128)S(1)}, u32[]{:S(2)}, u32[]{:S(2)}) collective-permute-start(f32[130,128]{1,0:T(8,128)S(1)} %pad_maximum_fusion.9), channel_id=1, source_target_pairs={{0,32},{32,64},{64,96},{96,128},{128,160},{160,192},{192,224},{224... | collective-permute-start | bytes 199688 | tf_op jit(solution)/shard_map/ppermute | solution.py:23
  7.1 6.6 %collective-permute-start.1 = (f32[130,128]{1,0:T(8,128)S(1)}, f32[130,128]{1,0:T(8,128)S(1)}, u32[]{:S(2)}, u32[]{:S(2)}) collective-permute-start(f32[130,128]{1,0:T(8,128)S(1)} %pad_maximum_fusion.9), channel_id=1, source_target_pairs={{32,0},{64,32},{96,64},{128,96},{160,128},{192,160},{224,192},{256... | collective-permute-start | bytes 199688 | tf_op jit(solution)/shard_map/ppermute | solution.py:24
  9.6 1.3 %copy-start = (f32[384,768]{1,0:T(8,128)S(1)}, f32[384,768]{1,0:T(8,128)}, u32[]{:S(2)}) copy-start(f32[384,768]{1,0:T(8,128)} %constant.46) | copy-start | bytes 3538948
  10.6 3.0 %copy-start.2 = (f32[64,128]{1,0:T(8,128)S(1)}, f32[64,128]{1,0:T(8,128)}, u32[]{:S(2)}) copy-start(f32[64,128]{1,0:T(8,128)} %param.9) | copy-start | bytes 98308
  40.6 12.3 %all-to-all-start.1 = ((f32[32,1,512]{2,1,0:T(1,128)}), f32[32,1,512]{2,1,0:T(1,128)S(1)}, u32[]{:S(2)}, u32[]{:S(2)}) async-start(f32[32,1,512]{2,1,0:T(1,128)} %broadcast_in_dim.8), calls=%async_computation.1 | async-start | bytes 131072 | tf_op jit(solution)/shard_map/all_to_all | solution.py:37

commit v12 on v11

--- a/solution.py
+++ b/solution.py
@@ -26,15 +26,18 @@
     return shard
 
 
-def exchange_sum(value, axis):
+def exchange_sum(value, axis, spread=False):
     peers = lax.axis_size(axis)
     rows, cols = value.shape
     if (rows * cols) % peers:
         return lax.psum(value, axis)
     parts = value.reshape(peers, rows * cols // peers)
     parts = lax.all_to_all(parts, axis, 0, 0, tiled=True)
-    total = jnp.sum(parts, axis=0, keepdims=True)
-    gathered = lax.all_to_all(jnp.broadcast_to(total, parts.shape), axis, 0, 0, tiled=True)
+    if spread:
+        spread_sum = product(jnp.ones((peers, peers), jnp.float32), parts)
+    else:
+        spread_sum = jnp.broadcast_to(jnp.sum(parts, axis=0, keepdims=True), parts.shape)
+    gathered = lax.all_to_all(spread_sum, axis, 0, 0, tiled=True)
     return gathered.reshape(rows, cols)
 
 
@@ -168,7 +171,7 @@
     field_imag = field_imag * scale
     share_sum = weights[kernel_index] * (field_real * field_real + field_imag * field_imag)
     share_sum = share_sum / total_kernels
-    intensity = exchange_sum(share_sum, "kern")
+    intensity = exchange_sum(share_sum, "kern", spread=True)
     drive = resist_drive(intensity, target_ext, pixel_active)
     source_real, source_imag = right_stacked(
         drive * field_real, drive * field_imag, col_stack[:field_cols, :], -1.0

time: 80.1 us -> 80.2 us (level)
    dot_general x14 -> x15, matrix products: 9.01 us -> 9.19 us  [product(): jnp.dot(left_mat, right_mat, precision=lax.Precision.HIGHEST, preferred_e...]
where the time goes in v12:
time: 80.2 us; the launch traced here: 79.8 us
  blocking collectives  44.6 us (56%)
  starting transfers between devices  10.6 us (13%)
  matrix products  9.19 us (11%)
  waiting for transfers between devices  8.7 us (11%)
  local copies, waits for them, and re-layouts  3.27 us (4%)
  other arithmetic  2.45 us (3%)
  between operations  0.94 us (1%)
    all_to_all x2, blocking collectives, exchange_sum(): parts = lax.all_to_all(parts, axis, 0, 0, tiled=True)  33.4 us
    all_to_all x1, blocking collectives, exchange_sum(): gathered = lax.all_to_all(spread_sum, axis, 0, 0, tiled=True)  11.3 us
    dot_general x15, matrix products, product(): jnp.dot(left_mat, right_mat, precision=lax.Precision.HIGHEST, preferred_e...  9.19 us
    all_to_all x1, waiting for transfers between devices, exchange_sum(): gathered = lax.all_to_all(spread_sum, axis, 0, 0, tiled=True)  7.89 us
    ppermute x1, starting transfers between devices, padded(): before = lax.ppermute(last, axis, up)  5.46 us
    all_to_all x1, starting transfers between devices, exchange_sum(): gathered = lax.all_to_all(spread_sum, axis, 0, 0, tiled=True)  3.87 us
  transfers between devices with their start and end apart: 3, of which 2 were waited for; matrix products, arithmetic and copies ran while one was open for 5% of the time, Pallas kernels for 0%

profile of v12, /device:TPU:1, one launch (start us, length us, event | category | flops | bytes accessed | tf_op | source)
XLA Modules:
  0.0 79.8 jit_solution(15877088242755583037)
XLA Ops:
  0.0 0.8 %fusion.72 = f32[66,128]{1,0:T(8,128)S(1)} fusion(s32[2,4]{1,0:T(2,128)} %param.13, s32[64,128]{1,0:T(8,128)} %param.12), kind=kLoop, calls=%fused_computation.107 | loop fusion | flops 16896 | bytes 66592 | tf_op jit(solution)/shard_map/convert_element_type | solution.py:136
  0.8 0.8 pad_maximum_fusion.9
  1.6 5.5 %collective-permute-start = (f32[130,128]{1,0:T(8,128)S(1)}, f32[130,128]{1,0:T(8,128)S(1)}, u32[]{:S(2)}, u32[]{:S(2)}) collective-permute-start(f32[130,128]{1,0:T(8,128)S(1)} %pad_maximum_fusion.9), channel_id=1, source_target_pairs={{0,32},{32,64},{64,96},{96,128},{128,160},{160,192},{192,224},{224... | collective-permute-start | bytes 199688 | tf_op jit(solution)/shard_map/ppermute | solution.py:23
  7.1 1.3 %collective-permute-start.1 = (f32[130,128]{1,0:T(8,128)S(1)}, f32[130,128]{1,0:T(8,128)S(1)}, u32[]{:S(2)}, u32[]{:S(2)}) collective-permute-start(f32[130,128]{1,0:T(8,128)S(1)} %pad_maximum_fusion.9), channel_id=1, source_target_pairs={{32,0},{64,32},{96,64},{128,96},{160,128},{192,160},{224,192},{256... | collective-permute-start | bytes 199688 | tf_op jit(solution)/shard_map/ppermute | solution.py:24
  8.4 1.3 %fusion.90 = (f32[1,1,129,129]{3,1,2,0:T(1,128)S(1)}, f32[1,1,129,129]{3,1,2,0:T(1,128)S(1)}) fusion(f32[1,2,129,129]{3,1,2,0:T(2,128)} %param.10), kind=kLoop, calls=%fused_computation.125 | loop fusion | bytes 266256 | tf_op jit(solution)/shard_map/slice | solution.py:159
  9.7 0.9 %fusion.13 = f32[384,258]{0,1:T(8,128)S(1)} fusion(f32[384,192]{1,0:T(8,128)S(1)} %copy-done.1, f32[129,129]{1,0:T(8,128)S(1)} %get-tuple-element.26, f32[129,129]{1,0:T(8,128)S(1)} %get-tuple-element.27), kind=kOutput, calls=%fused_computation.17 | convolution fusion | flops 153396736 | bytes 824328 | tf_op jit(solution)/shard_map/dot_general | solution.py:45
  10.9 1.2 %fusion.7 = f32[384,768]{1,0:T(8,128)S(1)} fusion(f32[384,768]{1,0:T(8,128)S(1)} %copy-done, f32[192,129]{0,1:T(8,128)S(1)} %get-tuple-element.17, f32[192,129]{0,1:T(8,128)S(1)} %get-tuple-element.16), kind=kOutput, calls=%fused_computation.11 | convolution fusion | flops 456573312 | bytes 1875968 | tf_op jit(solution)/shard_map/dot_general | solution.py:45
  12.8 0.8 %collective-permute-done.1 = f32[130,128]{1,0:T(8,128)S(1)} collective-permute-done((f32[130,128]{1,0:T(8,128)S(1)}, f32[130,128]{1,0:T(8,128)S(1)}, u32[]{:S(2)}, u32[]{:S(2)}) %collective-permute-start.1) | collective-permute-done | bytes 66592 | tf_op jit(solution)/shard_map/ppermute | solution.py:24
  13.6 0.8 %fusion.45 = f32[64,768]{1,0:T(8,128)S(1)} fusion(f32[384,768]{1,0:T(8,128)S(1)} %copy-done, f32[130,128]{1,0:T(8,128)S(1)} %collective-permute-done.1, f32[130,128]{1,0:T(8,128)S(1)} %collective-permute-done, f32[66,128]{1,0:T(8,128)S(1)} %fusion.72, f32[64,128]{1,0:T(8,128)S(1)} %copy-done.2), kind=kOutput, calls=%fused_computation.71 | convolution fusion | flops 226566144 | bytes 1575936 | tf_op jit(solution)/shard_map/dot_general | solution.py:45
  14.5 1.1 %fusion.25 = f32[384,768]{1,0:T(8,128)S(1)} fusion(f32[64,384]{1,0:T(8,128)S(1)} %get-tuple-element.25, f32[64,384]{1,0:T(8,128)S(1)} %get-tuple-element.24, f32[384,192]{1,0:T(8,128)S(1)} %copy-done.1), kind=kOutput, calls=%fused_computation.39 | convolution fusion | flops 226541568 | bytes 1572864 | tf_op jit(solution)/shard_map/dot_general | solution.py:45
  15.9 0.5 fusion.6
  16.4 0.5 fusion.5
  16.9 0.4 fusion.11
  17.8 22.1 %all_to_all.37 = f32[32,1,512]{2,1,0:T(1,128)S(1)} all-to-all(f32[32,1,512]{2,1,0:T(1,128)S(1)} %all_to_all.32), channel_id=1, replica_groups=mesh['tile'=32,'kern'=32] {'kern'}, dimensions={0} | all-to-all | bytes 131072 | tf_op jit(solution)/shard_map/all_to_all | solution.py:35
  40.1 0.7 copy.25
  40.8 3.9 %all-to-all-start.1 = ((f32[32,1,512]{2,1,0:T(1,128)}), f32[32,1,512]{2,1,0:T(1,128)S(1)}, u32[]{:S(2)}, u32[]{:S(2)}) async-start(f32[32,1,512]{2,1,0:T(1,128)} %copy.25), calls=%async_computation.1 | async-start | bytes 131072 | tf_op jit(solution)/shard_map/all_to_all | solution.py:40
  45.2 7.9 %all-to-all-done.1 = f32[32,1,512]{2,1,0:T(1,128)S(1)} async-done(((f32[32,1,512]{2,1,0:T(1,128)}), f32[32,1,512]{2,1,0:T(1,128)S(1)}, u32[]{:S(2)}, u32[]{:S(2)}) %all-to-all-start.1) | async-done | bytes 65568 | tf_op jit(solution)/shard_map/all_to_all | solution.py:40
  53.3 0.6 fusion.1
  53.9 1.1 %fusion.29 = f32[384,768]{1,0:T(8,128)S(1)} fusion(f32[64,384]{1,0:T(8,128)S(1)} %get-tuple-element.19, f32[64,384]{1,0:T(8,128)S(1)} %get-tuple-element.18, f32[384,192]{1,0:T(8,128)S(1)} %copy-done.1), kind=kOutput, calls=%fused_computation.44 | convolution fusion | flops 226541568 | bytes 1572864 | tf_op jit(solution)/shard_map/dot_general | solution.py:45
  55.1 0.5 fusion.4
  55.5 0.5 fusion.3
  56.6 11.3 %all_to_all.38 = f32[32,1,256]{2,1,0:T(1,128)S(1)} all-to-all(f32[32,1,256]{2,1,0:T(1,128)S(1)} %bitcast.21), channel_id=1, replica_groups=mesh['tile'=32,'kern'=32] {'kern'}, dimensions={0} | all-to-all | bytes 65536 | tf_op jit(solution)/shard_map/all_to_all | solution.py:35
  67.9 11.3 %all_to_all.39 = f32[32,1,256]{2,1,0:T(1,128)S(1)} all-to-all(f32[32,1,256]{2,1,0:T(1,128)S(1)} %broadcast_in_dim.18), channel_id=1, replica_groups=mesh['tile'=32,'kern'=32] {'kern'}, dimensions={0} | all-to-all | bytes 65536 | tf_op jit(solution)/shard_map/all_to_all | solution.py:40
  79.2 0.6 copy.52
  (36 shorter events, 2.7 us)
Async XLA Ops:
  0.0 9.7 %copy-start.1 = (f32[384,192]{1,0:T(8,128)S(1)}, f32[384,192]{1,0:T(8,128)}, u32[]{:S(2)}) copy-start(f32[384,192]{1,0:T(8,128)} %constant.46) | copy-start | bytes 884740
  1.6 11.2 %collective-permute-start = (f32[130,128]{1,0:T(8,128)S(1)}, f32[130,128]{1,0:T(8,128)S(1)}, u32[]{:S(2)}, u32[]{:S(2)}) collective-permute-start(f32[130,128]{1,0:T(8,128)S(1)} %pad_maximum_fusion.9), channel_id=1, source_target_pairs={{0,32},{32,64},{64,96},{96,128},{128,160},{160,192},{192,224},{224... | collective-permute-start | bytes 199688 | tf_op jit(solution)/shard_map/ppermute | solution.py:23
  7.1 6.6 %collective-permute-start.1 = (f32[130,128]{1,0:T(8,128)S(1)}, f32[130,128]{1,0:T(8,128)S(1)}, u32[]{:S(2)}, u32[]{:S(2)}) collective-permute-start(f32[130,128]{1,0:T(8,128)S(1)} %pad_maximum_fusion.9), channel_id=1, source_target_pairs={{32,0},{64,32},{96,64},{128,96},{160,128},{192,160},{224,192},{256... | collective-permute-start | bytes 199688 | tf_op jit(solution)/shard_map/ppermute | solution.py:24
  9.6 1.3 %copy-start = (f32[384,768]{1,0:T(8,128)S(1)}, f32[384,768]{1,0:T(8,128)}, u32[]{:S(2)}) copy-start(f32[384,768]{1,0:T(8,128)} %constant.47) | copy-start | bytes 3538948
  10.6 3.0 %copy-start.2 = (f32[64,128]{1,0:T(8,128)S(1)}, f32[64,128]{1,0:T(8,128)}, u32[]{:S(2)}) copy-start(f32[64,128]{1,0:T(8,128)} %param.9) | copy-start | bytes 98308
  40.8 12.3 %all-to-all-start.1 = ((f32[32,1,512]{2,1,0:T(1,128)}), f32[32,1,512]{2,1,0:T(1,128)S(1)}, u32[]{:S(2)}, u32[]{:S(2)}) async-start(f32[32,1,512]{2,1,0:T(1,128)} %copy.25), calls=%async_computation.1 | async-start | bytes 131072 | tf_op jit(solution)/shard_map/all_to_all | solution.py:40

commit v13 on v12

--- a/solution.py
+++ b/solution.py
@@ -125,7 +125,13 @@
     col_cos, col_sin = twiddle(frame_cols)
     row_stack = jnp.concatenate([row_cos, row_sin], axis=0)
     col_stack = jnp.concatenate([col_cos, col_sin], axis=1)
-    row_stack, col_stack = lax.optimization_barrier((row_stack, col_stack))
+    field_rows = jnp.concatenate([row_cos[:band], row_sin[:band]], axis=0)
+    back_rows = jnp.concatenate(
+        [row_cos[margin : margin + band], row_sin[margin : margin + band]], axis=0
+    )
+    row_stack, col_stack, field_rows, back_rows = lax.optimization_barrier(
+        (row_stack, col_stack, field_rows, back_rows)
+    )
     row_cos, row_sin = row_stack[:frame_rows], row_stack[frame_rows:]
     col_cos, col_sin = col_stack[:, :frame_cols], col_stack[:, frame_cols:]
     block_grid, blocks = active.shape
@@ -161,9 +167,7 @@
     kern_real, kern_imag = right_stacked(kern_real, kern_imag, col_stack[:width, :], 1.0)
     prod_real = spec_real * kern_real - spec_imag * kern_imag
     prod_imag = spec_real * kern_imag + spec_imag * kern_real
-    field_real, field_imag = apply_left(
-        row_cos[:band, :], row_sin[:band, :], 1.0, prod_real, prod_imag
-    )
+    field_real, field_imag = left_stacked(field_rows, 1.0, prod_real, prod_imag)
     field_real, field_imag = apply_right(
         field_real, field_imag, col_cos[:, :field_cols], col_sin[:, :field_cols], 1.0
     )
@@ -181,13 +185,7 @@
     )
     quot_real = source_real * kern_real + source_imag * kern_imag
     quot_imag = source_imag * kern_real - source_real * kern_imag
-    back_real, back_imag = apply_left(
-        row_cos[margin : margin + band, :],
-        row_sin[margin : margin + band, :],
-        1.0,
-        quot_real,
-        quot_imag,
-    )
+    back_real, back_imag = left_stacked(back_rows, 1.0, quot_real, quot_imag)
     grad_scale = 2.0 * weights[kernel_index] * scale / total_kernels
     own_cos = col_cos[:, reach : reach + own_cols]
     own_sin = col_sin[:, reach : reach + own_cols]

time: 80.2 us -> 81 us (level)
  local copies, waits for them, and re-layouts: 3.27 us -> 4.84 us
  matrix products: 9.19 us -> 8.29 us
    unnamed x7 -> x11, local copies, waits for them, and re-layouts: 0.78 us -> 2.35 us
    dot_general x15 -> x13, matrix products: 9.19 us -> 8.29 us  [product(): jnp.dot(left_mat, right_mat, precision=lax.Precision.HIGHEST, preferred_e...]
where the time goes in v13:
time: 81 us; the launch traced here: 80.5 us
  blocking collectives  44.6 us (55%)
  starting transfers between devices  10.6 us (13%)
  waiting for transfers between devices  8.7 us (11%)
  matrix products  8.29 us (10%)
  local copies, waits for them, and re-layouts  4.84 us (6%)
  other arithmetic  2.45 us (3%)
  between operations  0.94 us (1%)
    all_to_all x2, blocking collectives, exchange_sum(): parts = lax.all_to_all(parts, axis, 0, 0, tiled=True)  33.4 us
    all_to_all x1, blocking collectives, exchange_sum(): gathered = lax.all_to_all(spread_sum, axis, 0, 0, tiled=True)  11.3 us
    dot_general x13, matrix products, product(): jnp.dot(left_mat, right_mat, precision=lax.Precision.HIGHEST, preferred_e...  8.29 us
    all_to_all x1, waiting for transfers between devices, exchange_sum(): gathered = lax.all_to_all(spread_sum, axis, 0, 0, tiled=True)  7.89 us
    ppermute x1, starting transfers between devices, padded(): before = lax.ppermute(last, axis, up)  5.46 us
    all_to_all x1, starting transfers between devices, exchange_sum(): gathered = lax.all_to_all(spread_sum, axis, 0, 0, tiled=True)  3.88 us
    unnamed x11, local copies, waits for them, and re-layouts  2.35 us
  transfers between devices with their start and end apart: 3, of which 2 were waited for; matrix products, arithmetic and copies ran while one was open for 5% of the time, Pallas kernels for 0%

profile of v13, /device:TPU:1, one launch (start us, length us, event | category | flops | bytes accessed | tf_op | source)
XLA Modules:
  0.0 80.5 jit_solution(14639552606498836040)
XLA Ops:
  0.0 0.8 %fusion.72 = f32[66,128]{1,0:T(8,128)S(1)} fusion(s32[2,4]{1,0:T(2,128)} %param.13, s32[64,128]{1,0:T(8,128)} %param.12), kind=kLoop, calls=%fused_computation.105 | loop fusion | flops 16896 | bytes 66592 | tf_op jit(solution)/shard_map/convert_element_type | solution.py:142
  0.8 0.8 pad_maximum_fusion.3
  1.6 5.5 %collective-permute-start = (f32[130,128]{1,0:T(8,128)S(1)}, f32[130,128]{1,0:T(8,128)S(1)}, u32[]{:S(2)}, u32[]{:S(2)}) collective-permute-start(f32[130,128]{1,0:T(8,128)S(1)} %pad_maximum_fusion.3), channel_id=1, source_target_pairs={{0,32},{32,64},{64,96},{96,128},{128,160},{160,192},{192,224},{224... | collective-permute-start | bytes 199688 | tf_op jit(solution)/shard_map/ppermute | solution.py:23
  7.1 1.3 %collective-permute-start.1 = (f32[130,128]{1,0:T(8,128)S(1)}, f32[130,128]{1,0:T(8,128)S(1)}, u32[]{:S(2)}, u32[]{:S(2)}) collective-permute-start(f32[130,128]{1,0:T(8,128)S(1)} %pad_maximum_fusion.3), channel_id=1, source_target_pairs={{32,0},{64,32},{96,64},{128,96},{160,128},{192,160},{224,192},{256... | collective-permute-start | bytes 199688 | tf_op jit(solution)/shard_map/ppermute | solution.py:24
  8.4 1.3 %fusion.88 = (f32[1,1,129,129]{3,1,2,0:T(1,128)S(1)}, f32[1,1,129,129]{3,1,2,0:T(1,128)S(1)}) fusion(f32[1,2,129,129]{3,1,2,0:T(2,128)} %param.10), kind=kLoop, calls=%fused_computation.121 | loop fusion | bytes 266256 | tf_op jit(solution)/shard_map/slice | solution.py:165
  9.7 0.9 %fusion.17 = f32[384,258]{0,1:T(8,128)S(1)} fusion(f32[384,192]{1,0:T(8,128)S(1)} %copy-done.1, f32[129,129]{1,0:T(8,128)S(1)} %get-tuple-element.30, f32[129,129]{1,0:T(8,128)S(1)} %get-tuple-element.31), kind=kOutput, calls=%fused_computation.19 | convolution fusion | flops 153396736 | bytes 824328 | tf_op jit(solution)/shard_map/dot_general | solution.py:45
  10.9 1.2 %fusion.11 = f32[384,768]{1,0:T(8,128)S(1)} fusion(f32[384,768]{1,0:T(8,128)S(1)} %copy-done, f32[192,129]{0,1:T(8,128)S(1)} %get-tuple-element.21, f32[192,129]{0,1:T(8,128)S(1)} %get-tuple-element.20), kind=kOutput, calls=%fused_computation.13 | convolution fusion | flops 456573312 | bytes 1875968 | tf_op jit(solution)/shard_map/dot_general | solution.py:45
  12.8 0.8 collective-permute-done.1
  13.6 0.8 %fusion.49 = f32[64,768]{1,0:T(8,128)S(1)} fusion(f32[384,768]{1,0:T(8,128)S(1)} %copy-done, f32[130,128]{1,0:T(8,128)S(1)} %collective-permute-done.1, f32[130,128]{1,0:T(8,128)S(1)} %collective-permute-done, f32[66,128]{1,0:T(8,128)S(1)} %fusion.72, f32[64,128]{1,0:T(8,128)S(1)} %copy-done.2), kind=kOutput, calls=%fused_computation.73 | convolution fusion | flops 226566144 | bytes 1575936 | tf_op jit(solution)/shard_map/dot_general | solution.py:45
  14.5 1.1 %fusion.29 = f32[384,768]{1,0:T(8,128)S(1)} fusion(f32[64,384]{1,0:T(8,128)S(1)} %get-tuple-element.29, f32[64,384]{1,0:T(8,128)S(1)} %get-tuple-element.28, f32[384,192]{1,0:T(8,128)S(1)} %copy-done.1), kind=kOutput, calls=%fused_computation.41 | convolution fusion | flops 226541568 | bytes 1572864 | tf_op jit(solution)/shard_map/dot_general | solution.py:45
  15.9 0.8 copy-done.4
  16.7 0.5 fusion.3
  17.2 0.4 fusion.15
  18.1 22.1 %all_to_all.37 = f32[32,1,512]{2,1,0:T(1,128)S(1)} all-to-all(f32[32,1,512]{2,1,0:T(1,128)S(1)} %all_to_all.32), channel_id=1, replica_groups=mesh['tile'=32,'kern'=32] {'kern'}, dimensions={0} | all-to-all | bytes 131072 | tf_op jit(solution)/shard_map/all_to_all | solution.py:35
  40.4 0.7 copy.25
  41.1 3.9 %all-to-all-start.1 = ((f32[32,1,512]{2,1,0:T(1,128)}), f32[32,1,512]{2,1,0:T(1,128)S(1)}, u32[]{:S(2)}, u32[]{:S(2)}) async-start(f32[32,1,512]{2,1,0:T(1,128)} %copy.25), calls=%async_computation.1 | async-start | bytes 131072 | tf_op jit(solution)/shard_map/all_to_all | solution.py:40
  45.5 7.9 %all-to-all-done.1 = f32[32,1,512]{2,1,0:T(1,128)S(1)} async-done(((f32[32,1,512]{2,1,0:T(1,128)}), f32[32,1,512]{2,1,0:T(1,128)S(1)}, u32[]{:S(2)}, u32[]{:S(2)}) %all-to-all-start.1) | async-done | bytes 65568 | tf_op jit(solution)/shard_map/all_to_all | solution.py:40
  53.6 0.6 fusion.1
  54.2 1.1 %fusion.33 = f32[384,768]{1,0:T(8,128)S(1)} fusion(f32[64,384]{1,0:T(8,128)S(1)} %get-tuple-element.23, f32[64,384]{1,0:T(8,128)S(1)} %get-tuple-element.22, f32[384,192]{1,0:T(8,128)S(1)} %copy-done.1), kind=kOutput, calls=%fused_computation.46 | convolution fusion | flops 226541568 | bytes 1572864 | tf_op jit(solution)/shard_map/dot_general | solution.py:45
  55.4 0.8 copy-done.3
  56.2 0.5 fusion.7
  57.3 11.3 %all_to_all.38 = f32[32,1,256]{2,1,0:T(1,128)S(1)} all-to-all(f32[32,1,256]{2,1,0:T(1,128)S(1)} %bitcast.24), channel_id=1, replica_groups=mesh['tile'=32,'kern'=32] {'kern'}, dimensions={0} | all-to-all | bytes 65536 | tf_op jit(solution)/shard_map/all_to_all | solution.py:35
  68.6 11.3 %all_to_all.39 = f32[32,1,256]{2,1,0:T(1,128)S(1)} all-to-all(f32[32,1,256]{2,1,0:T(1,128)S(1)} %broadcast_in_dim.18), channel_id=1, replica_groups=mesh['tile'=32,'kern'=32] {'kern'}, dimensions={0} | all-to-all | bytes 65536 | tf_op jit(solution)/shard_map/all_to_all | solution.py:40
  79.9 0.6 copy.52
  (38 shorter events, 2.7 us)
Async XLA Ops:
  0.0 9.7 %copy-start.1 = (f32[384,192]{1,0:T(8,128)S(1)}, f32[384,192]{1,0:T(8,128)}, u32[]{:S(2)}) copy-start(f32[384,192]{1,0:T(8,128)} %constant.46) | copy-start | bytes 884740
  1.6 11.2 %collective-permute-start = (f32[130,128]{1,0:T(8,128)S(1)}, f32[130,128]{1,0:T(8,128)S(1)}, u32[]{:S(2)}, u32[]{:S(2)}) collective-permute-start(f32[130,128]{1,0:T(8,128)S(1)} %pad_maximum_fusion.3), channel_id=1, source_target_pairs={{0,32},{32,64},{64,96},{96,128},{128,160},{160,192},{192,224},{224... | collective-permute-start | bytes 199688 | tf_op jit(solution)/shard_map/ppermute | solution.py:23
  7.1 6.6 %collective-permute-start.1 = (f32[130,128]{1,0:T(8,128)S(1)}, f32[130,128]{1,0:T(8,128)S(1)}, u32[]{:S(2)}, u32[]{:S(2)}) collective-permute-start(f32[130,128]{1,0:T(8,128)S(1)} %pad_maximum_fusion.3), channel_id=1, source_target_pairs={{32,0},{64,32},{96,64},{128,96},{160,128},{192,160},{224,192},{256... | collective-permute-start | bytes 199688 | tf_op jit(solution)/shard_map/ppermute | solution.py:24
  9.6 1.3 %copy-start = (f32[384,768]{1,0:T(8,128)S(1)}, f32[384,768]{1,0:T(8,128)}, u32[]{:S(2)}) copy-start(f32[384,768]{1,0:T(8,128)} %constant.47) | copy-start | bytes 3538948
  10.6 3.0 %copy-start.2 = (f32[64,128]{1,0:T(8,128)S(1)}, f32[64,128]{1,0:T(8,128)}, u32[]{:S(2)}) copy-start(f32[64,128]{1,0:T(8,128)} %param.9) | copy-start | bytes 98308
  15.7 0.9 %copy-start.4 = (f32[128,192]{1,0:T(8,128)S(1)}, f32[128,192]{1,0:T(8,128)}, u32[]{:S(2)}) copy-start(f32[128,192]{1,0:T(8,128)} %constant.50) | copy-start | bytes 294916
  41.1 12.3 %all-to-all-start.1 = ((f32[32,1,512]{2,1,0:T(1,128)}), f32[32,1,512]{2,1,0:T(1,128)S(1)}, u32[]{:S(2)}, u32[]{:S(2)}) async-start(f32[32,1,512]{2,1,0:T(1,128)} %copy.25), calls=%async_computation.1 | async-start | bytes 131072 | tf_op jit(solution)/shard_map/all_to_all | solution.py:40
  55.3 0.9 %copy-start.3 = (f32[128,192]{1,0:T(8,128)S(1)}, f32[128,192]{1,0:T(8,128)}, u32[]{:S(2)}) copy-start(f32[128,192]{1,0:T(8,128)} %constant.53) | copy-start | bytes 294916
